TPU v7x, 512 devices: a whole 4x4x16 slice. The times are simulated.
512 devices in a mesh: dp: 32 (over x_lo, z), ctx: 16 (over y, x_hi, core).
Axes of the slice: x: 4 (x_hi: 2, x_lo: 2; x = x_hi * 2 + x_lo), y: 4, z: 16, core: 2. Of those that a mesh axis runs over, the one named last changes fastest.
Arguments:
- queries: bfloat16 [32, 2048, 2048], P('dp', 'ctx'), may hold values from -6 to 6
- key_state_matrix: bfloat16 [32, 2048, 2048], P('dp', 'ctx'), may hold values from -6 to 6
- value_state_matrix: bfloat16 [32, 2048, 2048], P('dp', 'ctx'), may hold values from -6 to 6
- cotangent: bfloat16 [32, 2048, 2048], P('dp', 'ctx'), may hold values from -6 to 6
- sublayer_norm_gain: float32 [2048], replicated, may hold values from 0.5 to 1.5
- sublayer_norm_bias: float32 [2048], replicated, may hold values from -3 to 3
- segment_blocks: int32 [4], replicated, may hold values from 1 to 16, as said below
- dilation_rates: int32 [4], replicated, may hold values from 1 to 16, as said below
Outputs:
- normed: bfloat16 [32, 2048, 2048], P('dp', 'ctx')
- grad_queries: bfloat16 [32, 2048, 2048], P('dp', 'ctx')
- grad_keys: bfloat16 [32, 2048, 2048], P('dp', 'ctx')
- grad_values: bfloat16 [32, 2048, 2048], P('dp', 'ctx')
- grad_gain: float32 [2048], P('ctx')
- grad_bias: float32 [2048], P('ctx')
Inputs may be any that keep to these rules, and one draw needn't show every extreme that they name: segment_blocks[0] is 1; the other entries are powers of two from 2 to 16, and at least one of them equals 16. dilation_rates[0] is 1; entries 1 to 3 are 2, 16 and one of 4 or 8, in some order.
All inputs are finite; a program needn't handle non-finite values.
Results may differ from a plain program's by a relative error of at most 0.011.
Values may be sent and summed in bfloat16 or wider, within the bound.
No kernel may reach another device: no remote copies, remote signals or barrier semaphores. Data moves between devices by JAX's collectives and lax.ppermute only.
A program may use at most 64 MiB of HBM per device.

v0:
```python
import math

import jax
import jax.numpy as jnp
from jax import lax
from jax.sharding import PartitionSpec as P

H = 16
BLK = 128
G = 4


epsilon = 1e-05


def pick_rows(array, parity):
    pairs = array.reshape((array.shape[0] // 2, 2) + array.shape[1:])
    cond = (parity == 0).reshape((-1,) + (1,) * (array.ndim - 2))
    return jnp.where(cond, pairs[:, 0], pairs[:, 1])


def spread_rows(packed, parity, base):
    pairs = base.reshape((base.shape[0] // 2, 2) + base.shape[1:])
    cond = (parity == 0).reshape((-1,) + (1,) * (base.ndim - 2))
    first_branch = jnp.where(cond, packed, pairs[:, 0])
    second = jnp.where(cond, pairs[:, 1], packed)
    return jnp.stack([first_branch, second], axis=1).reshape(base.shape)


def add_parts(full_part, packed_part, parity):
    spread = spread_rows(packed_part, parity, jnp.zeros_like(full_part))
    full_part = lax.optimization_barrier(full_part)
    spread = lax.optimization_barrier(spread)
    return (full_part.astype(jnp.float32) + spread.astype(jnp.float32)).astype(jnp.bfloat16)


def block_view(array):
    return array.reshape((array.shape[0] // BLK, BLK) + array.shape[1:])


def lse_view(log_norm):
    return jnp.transpose(block_view(log_norm), (0, 2, 1))


def local_scores(query_row_set, key_row_set):
    scaling = 1.0 / math.sqrt(query_row_set.shape[-1])
    return (
        jnp.einsum(
            "bqhd,bkhd->bhqk",
            block_view(query_row_set),
            block_view(key_row_set),
            preferred_element_type=jnp.float32,
        )
        * scaling
    )


def local_lse(query_row_set, key_row_set):
    scores = local_scores(query_row_set, key_row_set)
    row_max = jnp.max(scores, axis=3)
    total = row_max + jnp.log(jnp.sum(jnp.exp(scores - row_max[..., None]), axis=3))
    return jnp.transpose(total, (0, 2, 1)).reshape(query_row_set.shape[0], query_row_set.shape[1])


def local_output(query_row_set, key_row_set, value_row_set, log_norm):
    scores = local_scores(query_row_set, key_row_set)
    prob_bf = jnp.exp(scores - lse_view(log_norm)[..., None]).astype(jnp.bfloat16)
    output = jnp.einsum(
        "bhqk,bkhd->bqhd", prob_bf, block_view(value_row_set), preferred_element_type=jnp.float32
    )
    return output.astype(jnp.bfloat16).reshape(query_row_set.shape)


def local_backward(query_row_set, key_row_set, value_row_set, grad_rows, log_norm, delta_row):
    scaling = 1.0 / math.sqrt(query_row_set.shape[-1])
    scores = local_scores(query_row_set, key_row_set)
    prob_full = jnp.exp(scores - lse_view(log_norm)[..., None])
    prob_bf = prob_full.astype(jnp.bfloat16)
    grad_prob = jnp.einsum(
        "bqhd,bkhd->bhqk",
        block_view(grad_rows),
        block_view(value_row_set),
        preferred_element_type=jnp.float32,
    )
    grad_score = (prob_full * (grad_prob - lse_view(delta_row)[..., None])).astype(jnp.bfloat16)
    grad_q = jnp.einsum(
        "bhqk,bkhd->bqhd", grad_score, block_view(key_row_set), preferred_element_type=jnp.float32
    )
    grad_k = jnp.einsum(
        "bhqk,bqhd->bkhd", grad_score, block_view(query_row_set), preferred_element_type=jnp.float32
    )
    grad_v = jnp.einsum(
        "bhqk,bqhd->bkhd", prob_bf, block_view(grad_rows), preferred_element_type=jnp.float32
    )
    shape = query_row_set.shape
    return (
        (grad_q * scaling).astype(jnp.bfloat16).reshape(shape),
        (grad_k * scaling).astype(jnp.bfloat16).reshape(shape),
        grad_v.astype(jnp.bfloat16).reshape(shape),
    )


def packed_positions(start, count, head_indices):
    rows = start + jnp.arange(count, dtype=jnp.int32)
    return 2 * rows[None, :] + (head_indices % 2)[:, None]


def dilation_multiplier(
    query_positions, key_positions, head_indices, segment_blocks, dilation_rates
):
    counted = jnp.zeros(
        (head_indices.shape[0], query_positions.shape[1], key_positions.shape[1]), jnp.float32
    )
    for dilation_branch in range(1, G):
        seg_width = segment_blocks[dilation_branch] * BLK
        dilation_rate = dilation_rates[dilation_branch]
        same_seg = (
            query_positions[:, :, None] // seg_width == key_positions[:, None, :] // seg_width
        )
        selected_queries = query_positions % dilation_rate == head_indices[:, None] % dilation_rate
        selected_keys = key_positions % dilation_rate == head_indices[:, None] % dilation_rate
        counted = counted + (
            same_seg & selected_queries[:, :, None] & selected_keys[:, None, :]
        ).astype(jnp.float32)
    return counted


def sparse_attention_forward(
    query_row_set,
    key_row_set,
    value_row_set,
    baseline_logsumexp,
    head_indices,
    segment_blocks,
    dilation_rates,
):
    length_all, heads_here, head_size = query_row_set.shape
    rows_per_block = min(512, length_all)
    blocks = length_all // rows_per_block
    scaling = 1.0 / math.sqrt(head_size)
    key_positions = packed_positions(0, length_all, head_indices)

    def one_block(block_id):
        starting_row = block_id * rows_per_block
        q_block = lax.dynamic_slice_in_dim(query_row_set, starting_row, rows_per_block, 0)
        own_lse = lax.dynamic_slice_in_dim(baseline_logsumexp, starting_row, rows_per_block, 0).T
        counted = dilation_multiplier(
            packed_positions(starting_row, rows_per_block, head_indices),
            key_positions,
            head_indices,
            segment_blocks,
            dilation_rates,
        )
        scores = (
            jnp.einsum("qhd,khd->hqk", q_block, key_row_set, preferred_element_type=jnp.float32)
            * scaling
        )
        masked = jnp.where(counted > 0, scores, -1e30)
        row_max = jnp.max(masked, axis=2)
        part_lse = row_max + jnp.log(
            jnp.sum(counted * jnp.exp(masked - row_max[:, :, None]), axis=2)
        )
        top = jnp.maximum(part_lse, own_lse)
        log_norm = top + jnp.log(jnp.exp(part_lse - top) + jnp.exp(own_lse - top))
        prob_bf = (counted * jnp.exp(masked - log_norm[:, :, None])).astype(jnp.bfloat16)
        output = jnp.einsum(
            "hqk,khd->qhd", prob_bf, value_row_set, preferred_element_type=jnp.float32
        ).astype(jnp.bfloat16)
        return (output, log_norm)

    outputs, lse_blocks = lax.map(one_block, jnp.arange(blocks, dtype=jnp.int32))
    return (
        outputs.reshape(length_all, heads_here, head_size),
        jnp.transpose(lse_blocks, (0, 2, 1)).reshape(length_all, heads_here),
    )


def dilated_backward(
    query_row_set,
    key_row_set,
    value_row_set,
    grad_rows,
    log_norm,
    delta_row,
    head_indices,
    segment_blocks,
    dilation_rates,
):
    length_all, heads_here, head_size = query_row_set.shape
    rows_per_block = min(512, length_all)
    blocks = length_all // rows_per_block
    scaling = 1.0 / math.sqrt(head_size)
    key_positions = packed_positions(0, length_all, head_indices)

    def step(carry, block_id):
        acc_k, acc_v = carry
        starting_row = block_id * rows_per_block
        q_block = lax.dynamic_slice_in_dim(query_row_set, starting_row, rows_per_block, 0)
        g_block = lax.dynamic_slice_in_dim(grad_rows, starting_row, rows_per_block, 0)
        lse_block = lax.dynamic_slice_in_dim(log_norm, starting_row, rows_per_block, 0).T
        delta_block = lax.dynamic_slice_in_dim(delta_row, starting_row, rows_per_block, 0).T
        counted = dilation_multiplier(
            packed_positions(starting_row, rows_per_block, head_indices),
            key_positions,
            head_indices,
            segment_blocks,
            dilation_rates,
        )
        scores = (
            jnp.einsum("qhd,khd->hqk", q_block, key_row_set, preferred_element_type=jnp.float32)
            * scaling
        )
        masked = jnp.where(counted > 0, scores, -1e30)
        prob_full = counted * jnp.exp(masked - lse_block[:, :, None])
        prob_bf = prob_full.astype(jnp.bfloat16)
        grad_prob = jnp.einsum(
            "qhd,khd->hqk", g_block, value_row_set, preferred_element_type=jnp.float32
        )
        grad_score = (prob_full * (grad_prob - delta_block[:, :, None])).astype(jnp.bfloat16)
        grad_q = (
            jnp.einsum("hqk,khd->qhd", grad_score, key_row_set, preferred_element_type=jnp.float32)
            * scaling
        ).astype(jnp.bfloat16)
        acc_k = acc_k + jnp.einsum(
            "hqk,qhd->khd", grad_score, q_block, preferred_element_type=jnp.float32
        )
        acc_v = acc_v + jnp.einsum(
            "hqk,qhd->khd", prob_bf, g_block, preferred_element_type=jnp.float32
        )
        return ((acc_k, acc_v), grad_q)

    zeros_all = jnp.zeros((length_all, heads_here, head_size), jnp.float32)
    (acc_k, acc_v), grad_q = lax.scan(
        step, (zeros_all, zeros_all), jnp.arange(blocks, dtype=jnp.int32)
    )
    return (
        grad_q.reshape(length_all, heads_here, head_size),
        (acc_k * scaling).astype(jnp.bfloat16),
        acc_v.astype(jnp.bfloat16),
    )


def dense_attention_forward(
    query_row_set, key_row_set, value_row_set, head_indices, segment_blocks, dilation_rates
):
    parity = head_indices % 2
    own_lse = local_lse(query_row_set, key_row_set)
    packed_out, packed_lse = sparse_attention_forward(
        pick_rows(query_row_set, parity),
        pick_rows(key_row_set, parity),
        pick_rows(value_row_set, parity),
        pick_rows(own_lse, parity),
        head_indices,
        segment_blocks,
        dilation_rates,
    )
    log_norm = spread_rows(packed_lse, parity, own_lse)
    attended = add_parts(
        local_output(query_row_set, key_row_set, value_row_set, log_norm), packed_out, parity
    )
    return (attended, log_norm)


def full_backward(
    query_row_set,
    key_row_set,
    value_row_set,
    attended,
    grad_attended,
    log_norm,
    head_indices,
    segment_blocks,
    dilation_rates,
):
    parity = head_indices % 2
    delta_row = jnp.sum(grad_attended.astype(jnp.float32) * attended.astype(jnp.float32), axis=2)
    local_parts = local_backward(
        query_row_set, key_row_set, value_row_set, grad_attended, log_norm, delta_row
    )
    packed_parts = dilated_backward(
        pick_rows(query_row_set, parity),
        pick_rows(key_row_set, parity),
        pick_rows(value_row_set, parity),
        pick_rows(grad_attended, parity),
        pick_rows(log_norm, parity),
        pick_rows(delta_row, parity),
        head_indices,
        segment_blocks,
        dilation_rates,
    )
    return tuple(
        (
            add_parts(first_branch, second, parity)
            for first_branch, second in zip(local_parts, packed_parts)
        )
    )


def head_major(array, groups):
    tokens, width = array.shape
    return jnp.swapaxes(array.reshape(tokens, groups, width // groups), 0, 1)


def token_major(array):
    groups, tokens, width = array.shape
    return jnp.swapaxes(array, 0, 1).reshape(1, tokens, groups * width)


def head_norm(values, cot_rows, gain, bias):
    feature_axes = (0, 2)
    mean_row = jnp.mean(values, axis=feature_axes, keepdims=True)
    var_row = jnp.mean(values * values, axis=feature_axes, keepdims=True) - mean_row * mean_row
    inv_std = lax.rsqrt(var_row + epsilon)
    centered = (values - mean_row) * inv_std
    normed = (centered * gain + bias).astype(jnp.bfloat16)
    grad_y = cot_rows.astype(jnp.float32)
    scaled = grad_y * gain
    grad_tokens = (
        inv_std
        * (
            scaled
            - jnp.mean(scaled, axis=feature_axes, keepdims=True)
            - centered * jnp.mean(scaled * centered, axis=feature_axes, keepdims=True)
        )
    ).astype(jnp.bfloat16)
    return (normed, grad_tokens, jnp.sum(grad_y * centered, axis=1), jnp.sum(grad_y, axis=1))


def shards(
    queries,
    key_state_matrix,
    value_state_matrix,
    cotangent,
    sublayer_norm_gain,
    sublayer_norm_bias,
    segment_blocks,
    dilation_rates,
):
    tokens_here = queries.shape[1]
    width_all = queries.shape[2]
    head_size = width_all // H
    ctx_count = lax.axis_size("ctx")
    heads_here = H // ctx_count
    width_here = width_all // ctx_count
    head_first = lax.axis_index("ctx") * heads_here
    head_indices = head_first + jnp.arange(heads_here, dtype=jnp.int32)
    loss_scale = 1.0 / math.sqrt(lax.axis_size("dp") * tokens_here * ctx_count)
    tokens_all = tokens_here * ctx_count

    def to_rows(array):
        return array.reshape(tokens_all, heads_here, head_size)

    stacked_in = jnp.stack(
        [
            head_major(queries[0], ctx_count),
            head_major(key_state_matrix[0], ctx_count),
            head_major(value_state_matrix[0], ctx_count),
        ]
    )
    stacked_in = lax.all_to_all(stacked_in, "ctx", split_axis=1, concat_axis=1, tiled=True)
    query_head_tensor, key_head_tensor, value_head_tensor = (
        to_rows(stacked_in[0]),
        to_rows(stacked_in[1]),
        to_rows(stacked_in[2]),
    )
    attended, log_norm = dense_attention_forward(
        query_head_tensor,
        key_head_tensor,
        value_head_tensor,
        head_indices,
        segment_blocks,
        dilation_rates,
    )
    attended_hm = lax.all_to_all(
        attended.reshape(ctx_count, tokens_here, width_here), "ctx", 0, 0, tiled=True
    )
    gain_hm = sublayer_norm_gain.reshape(ctx_count, 1, width_here)
    bias_hm = sublayer_norm_bias.reshape(ctx_count, 1, width_here)
    normed_hm, grad_hm, gain_part, bias_part = head_norm(
        attended_hm.astype(jnp.float32),
        head_major(cotangent[0], ctx_count),
        gain_hm,
        bias_hm,
    )
    normed = token_major(normed_hm)
    grad_attended = to_rows(lax.all_to_all(grad_hm, "ctx", 0, 0, tiled=True))
    both = jnp.stack([gain_part, bias_part], axis=1)
    both = jnp.sum(lax.all_to_all(both, "ctx", 0, 0, tiled=True), axis=0)
    dp_count = lax.axis_size("dp")
    both = jnp.broadcast_to(both[None], (dp_count,) + both.shape)
    both = jnp.sum(lax.all_to_all(both, "dp", 0, 0, tiled=True), axis=0)
    grad_gain, grad_bias = both[0], both[1]
    grad_q, grad_k, grad_v = full_backward(
        query_head_tensor,
        key_head_tensor,
        value_head_tensor,
        attended,
        grad_attended,
        log_norm,
        head_indices,
        segment_blocks,
        dilation_rates,
    )
    stacked_out = lax.all_to_all(
        jnp.stack([part.reshape(ctx_count, tokens_here, width_here) for part in (grad_q, grad_k, grad_v)]),
        "ctx",
        split_axis=1,
        concat_axis=1,
        tiled=True,
    )
    return (
        normed,
        token_major(stacked_out[0]),
        token_major(stacked_out[1]),
        token_major(stacked_out[2]),
        grad_gain * loss_scale,
        grad_bias * loss_scale,
    )


def solution(mesh):
    return jax.shard_map(
        shards,
        mesh=mesh,
        in_specs=(
            P("dp", "ctx", None),
            P("dp", "ctx", None),
            P("dp", "ctx", None),
            P("dp", "ctx", None),
            P(),
            P(),
            P(),
            P(),
        ),
        out_specs=(
            P("dp", "ctx", None),
            P("dp", "ctx", None),
            P("dp", "ctx", None),
            P("dp", "ctx", None),
            P("ctx"),
            P("ctx"),
        ),
        check_vma=False,
    )
```

profile of v0, /device:TPU:1, one launch (start us, length us, event | category | flops | bytes accessed | tf_op | source)
XLA Modules:
  0.0 203.6 jit_solution(10587991710740403346)
XLA Ops:
  0.6 1.4 copy.199
  2.0 1.3 copy.200
  3.8 1.6 copy.202
  5.4 10.5 %all-to-all-start = ((bf16[3,16,128,128]{3,2,0,1:T(8,128)(2,1)}), bf16[3,16,128,128]{3,2,0,1:T(8,128)(2,1)S(1)}, u32[]{:S(2)}, u32[]{:S(2)}) async-start(bf16[3,16,128,128]{3,2,0,1:T(8,128)(2,1)} %copy.202), calls=%async_computation | async-start | bytes 3145728 | tf_op jit(solution)/shard_map/all_to_all | solution.py:360
  23.0 15.7 %all-to-all-done = bf16[3,16,128,128]{3,2,0,1:T(8,128)(2,1)S(1)} async-done(((bf16[3,16,128,128]{3,2,0,1:T(8,128)(2,1)}), bf16[3,16,128,128]{3,2,0,1:T(8,128)(2,1)S(1)}, u32[]{:S(2)}, u32[]{:S(2)}) %all-to-all-start) | async-done | bytes 1572896 | tf_op jit(solution)/shard_map/all_to_all | solution.py:360
  42.7 0.8 fusion.141
  43.5 0.8 fusion.139
  45.1 25.3 %while.37 = (s32[]{:T(128)}, bf16[2,512,1,128]{3,1,2,0:T(8,128)(2,1)}, f32[2,1,512]{2,1,0:T(1,128)S(1)}, s32[2]{0:T(128)S(1)}, s32[1]{0:T(128)}, /*index=5*/s32[...) while((s32[]{:T(128)}, ...), condition=%wide.region_5.6_spmd.clone.clone, body=%wide.region_2.5_spmd.clone.clone.sunk | while | flops 295863296 | bytes 9357893 | solution.py:171
  50.1 2.7 %fusion.207 = (f32[512]{0:T(512)S(1)}, f32[512,1024]{1,0:T(8,128)S(1)}) fusion(bf16[1024,1,128]{2,0,1:T(8,128)(2,1)} %get-tuple-element.1870, bf16[1024,1,128]{2,0,1:T(8,128)(2,1)} %get-tuple-element.1869, s32[]{:T(128)S(6)} %select_n.859, pred[1024]{0:T(1024)(128)(4,1)S(1)} %fusion.200, pred[512]{0:T(512)(128)(4,1)S(1)} %fusion.201, ...), kind=kOutput, calls=%fused_computation.270.clone.1 | convolution fusion | flops 143654400 | bytes 2515460 | tf_op jit(solution)/shard_map/while/body/eval_jaxpr/qhd,khd->hqk/dot_general | solution.py:155
  52.8 2.2 %multiply_reduce_fusion.2 = f32[512]{0:T(512)S(1)} fusion(f32[512,1024]{1,0:T(8,128)S(1)} %get-tuple-element.1743, f32[512]{0:T(512)S(1)} %get-tuple-element.1744, s32[1024]{0:T(1024)S(1)} %add_select_fusion.34, s32[1024]{0:T(1024)S(1)} %add_select_fusion.36, s32[1024]{0:T(1024)S(1)} %add_select_fusion.37, s32[512]{0:T(512)S(1)} %get-tuple-element.1733, ...), kind=kLoop, calls=%fused_computation.5.clone.1 | loop fusion | flops 8912384 | bytes 2124288 | tf_op jit(solution)/shard_map/while/body/eval_jaxpr/reduce_sum | solution.py:161
  55.0 2.0 fusion.208
  62.8 2.7 %fusion.207 = (f32[512]{0:T(512)S(1)}, f32[512,1024]{1,0:T(8,128)S(1)}) fusion(bf16[1024,1,128]{2,0,1:T(8,128)(2,1)} %get-tuple-element.1870, bf16[1024,1,128]{2,0,1:T(8,128)(2,1)} %get-tuple-element.1869, s32[]{:T(128)S(6)} %select_n.859, pred[1024]{0:T(1024)(128)(4,1)S(1)} %fusion.200, pred[512]{0:T(512)(128)(4,1)S(1)} %fusion.201, ...), kind=kOutput, calls=%fused_computation.270.clone.1 | convolution fusion | flops 143654400 | bytes 2515460 | tf_op jit(solution)/shard_map/while/body/eval_jaxpr/qhd,khd->hqk/dot_general | solution.py:155
  65.4 2.2 %multiply_reduce_fusion.2 = f32[512]{0:T(512)S(1)} fusion(f32[512,1024]{1,0:T(8,128)S(1)} %get-tuple-element.1743, f32[512]{0:T(512)S(1)} %get-tuple-element.1744, s32[1024]{0:T(1024)S(1)} %add_select_fusion.34, s32[1024]{0:T(1024)S(1)} %add_select_fusion.36, s32[1024]{0:T(1024)S(1)} %add_select_fusion.37, s32[512]{0:T(512)S(1)} %get-tuple-element.1733, ...), kind=kLoop, calls=%fused_computation.5.clone.1 | loop fusion | flops 8912384 | bytes 2124288 | tf_op jit(solution)/shard_map/while/body/eval_jaxpr/reduce_sum | solution.py:161
  67.7 2.0 fusion.208
  70.4 1.0 broadcast_select_fusion.3
  71.5 1.3 copy.215
  72.8 1.0 copy.212
  73.8 1.2 slice_select_fusion.2
  75.1 1.0 pad_maximum_fusion.2
  76.1 1.3 sub.224
  77.8 0.9 add_convert_fusion.3
  78.7 4.5 %all-to-all-start.1 = ((bf16[16,128,128]{2,1,0:T(8,128)(2,1)}), bf16[16,128,128]{2,1,0:T(8,128)(2,1)S(1)}, u32[]{:S(2)}, u32[]{:S(2)}) async-start(bf16[16,128,128]{2,1,0:T(8,128)(2,1)} %bitcast.361), calls=%async_computation.1 | async-start | bytes 1048576 | tf_op jit(solution)/shard_map/all_to_all | solution.py:374
  83.2 2.0 %copy.217 = bf16[1,128,2048]{1,2,0:T(8,128)(2,1)} copy(bf16[1,128,2048]{2,1,0:T(8,128)(2,1)} %param.15) | data formatting | bytes 1048576 | tf_op args[3]
  85.2 2.2 %copy.218 = f32[128,16,128]{2,0,1:T(8,128)} copy(bf16[128,16,128]{0,2,1:T(8,128)(2,1)} %bitcast.371) | data formatting | bytes 1572864 | tf_op jit(solution)/shard_map/convert_element_type | solution.py:316
  87.5 7.0 %all-to-all-done.1 = bf16[16,128,128]{2,1,0:T(8,128)(2,1)S(1)} async-done(((bf16[16,128,128]{2,1,0:T(8,128)(2,1)}), bf16[16,128,128]{2,1,0:T(8,128)(2,1)S(1)}, u32[]{:S(2)}, u32[]{:S(2)}) %all-to-all-start.1) | async-done | bytes 524320 | tf_op jit(solution)/shard_map/all_to_all | solution.py:374
  94.7 1.7 fusion.125
  97.1 4.5 %all-to-all-start.4 = ((f32[16,2,128]{2,1,0:T(2,128)}), f32[16,2,128]{2,1,0:T(2,128)S(1)}, u32[]{:S(2)}, u32[]{:S(2)}) async-start(f32[16,2,128]{2,1,0:T(2,128)} %pad_maximum_fusion.7), calls=%async_computation.4 | async-start | bytes 32768 | tf_op jit(solution)/shard_map/all_to_all | solution.py:388
  101.6 2.8 %fusion.124 = (bf16[16,128,128]{2,1,0:T(8,128)(2,1)}, bf16[128,16,128]{2,0,1:T(8,128)(2,1)}) fusion(bf16[16,128,128]{2,1,0:T(8,128)(2,1)S(1)} %all-to-all-done.1, f32[128,16,128]{2,0,1:T(8,128)} %copy.218, f32[128]{0:T(128)S(1)} %broadcast_multiply_fusion, f32[128]{0:T(128)S(1)} %broadcast_multiply_fusion.1, f32[16,128]{1,0:T(8,128)S(1)} %bitcast.411, ...), kind=kLoop, calls=%fused_computation.202 | loop fusion | flops 3145728 | bytes 2639872 | tf_op jit(solution)/shard_map/convert_element_type | solution.py:325
  104.4 4.5 %all-to-all-done.4 = f32[16,2,128]{2,1,0:T(2,128)S(1)} async-done(((f32[16,2,128]{2,1,0:T(2,128)}), f32[16,2,128]{2,1,0:T(2,128)S(1)}, u32[]{:S(2)}, u32[]{:S(2)}) %all-to-all-start.4) | async-done | bytes 16416 | tf_op jit(solution)/shard_map/all_to_all | solution.py:388
  109.0 3.8 %all-to-all-start.2 = ((bf16[16,128,128]{2,1,0:T(8,128)(2,1)}), bf16[16,128,128]{2,1,0:T(8,128)(2,1)S(1)}, u32[]{:S(2)}, u32[]{:S(2)}) async-start(bf16[16,128,128]{2,1,0:T(8,128)(2,1)} %get-tuple-element.1371), calls=%async_computation.2 | async-start | bytes 1048576 | tf_op jit(solution)/shard_map/all_to_all | solution.py:386
  112.8 11.2 %all-to-all-done.2 = bf16[16,128,128]{2,1,0:T(8,128)(2,1)S(1)} async-done(((bf16[16,128,128]{2,1,0:T(8,128)(2,1)}), bf16[16,128,128]{2,1,0:T(8,128)(2,1)S(1)}, u32[]{:S(2)}, u32[]{:S(2)}) %all-to-all-start.2) | async-done | bytes 524320 | tf_op jit(solution)/shard_map/all_to_all | solution.py:386
  124.6 13.3 %all-to-all-start.5 = ((f32[32,2,128]{2,1,0:T(2,128)}), f32[32,2,128]{2,1,0:T(2,128)S(1)}, u32[]{:S(2)}, u32[]{:S(2)}) async-start(f32[32,2,128]{2,1,0:T(2,128)} %broadcast_in_dim.146), calls=%async_computation.5 | async-start | bytes 65536 | tf_op jit(solution)/shard_map/all_to_all | solution.py:391
  137.9 1.1 convolution_convert_fusion.1
  139.3 1.3 reshape.1628
  141.1 1.1 fusion.112
  144.2 20.0 %while.38 = (s32[]{:T(128)}, f32[1024,1,128]{0,2,1:T(8,128)S(1)}, f32[1024,1,128]{0,2,1:T(8,128)S(1)}, bf16[2,512,1,128]{3,1,2,0:T(8,128)(2,1)S(1)}, s32[2]{0:T(...) while((s32[]{:T(128)}, f32[1024,1,128]{0,2,1:T(8,128)S(1)}, ...), condition=%wide.region_12.13_spmd.clone.clone.clone, body=%wide.region_11.12_spmd.clone.clone.clone.sunk | while | flops 683897344 | bytes 14145108 | solution.py:233
  149.2 2.8 %exponential_multiply_fusion.2 = f32[512,1024]{1,0:T(8,128)S(1)} fusion(f32[512]{0:T(512)S(1)} %bitcast.404, s32[1024]{0:T(1024)S(1)} %add_select_fusion.39, s32[1024]{0:T(1024)S(1)} %add_select_fusion.40, s32[1024]{0:T(1024)S(1)} %add_select_fusion.41, s32[512]{0:T(512)S(1)} %get-tuple-element.1783, s32[512]{0:T(512)S(1)} %get-tuple-element.1784, ...), kind=kOutput, calls=%fused_computation.90.clone.1 | convolution fusion | flops 144179200 | bytes 2515460 | tf_op jit(solution)/shard_map/while/body/eval_jaxpr/qhd,khd->hqk/dot_general | solution.py:210
  159.3 2.8 %exponential_multiply_fusion.2 = f32[512,1024]{1,0:T(8,128)S(1)} fusion(f32[512]{0:T(512)S(1)} %bitcast.404, s32[1024]{0:T(1024)S(1)} %add_select_fusion.39, s32[1024]{0:T(1024)S(1)} %add_select_fusion.40, s32[1024]{0:T(1024)S(1)} %add_select_fusion.41, s32[512]{0:T(512)S(1)} %get-tuple-element.1783, s32[512]{0:T(512)S(1)} %get-tuple-element.1784, ...), kind=kOutput, calls=%fused_computation.90.clone.1 | convolution fusion | flops 144179200 | bytes 2515460 | tf_op jit(solution)/shard_map/while/body/eval_jaxpr/qhd,khd->hqk/dot_general | solution.py:210
  164.9 0.8 select_bitcast_fusion.3
  166.7 1.8 pad_maximum_fusion.5
  168.5 1.3 copy.224
  170.3 1.3 pad_maximum_fusion.1
  171.6 5.1 %all-to-all-start.3 = ((bf16[3,16,128,128]{3,2,0,1:T(8,128)(2,1)}), bf16[3,16,128,128]{3,2,0,1:T(8,128)(2,1)S(1)}, u32[]{:S(2)}, u32[]{:S(2)}) async-start(bf16[3,16,128,128]{3,2,0,1:T(8,128)(2,1)} %pad_maximum_fusion.1), calls=%async_computation.3 | async-start | bytes 3145728 | tf_op jit(solution)/shard_map/all_to_all | solution.py:404
  177.0 1.0 copy.232
  178.6 21.0 %all-to-all-done.3 = bf16[3,16,128,128]{3,2,0,1:T(8,128)(2,1)S(1)} async-done(((bf16[3,16,128,128]{3,2,0,1:T(8,128)(2,1)}), bf16[3,16,128,128]{3,2,0,1:T(8,128)(2,1)S(1)}, u32[]{:S(2)}, u32[]{:S(2)}) %all-to-all-start.3) | async-done | bytes 1572896 | tf_op jit(solution)/shard_map/all_to_all | solution.py:404
  200.0 1.0 copy.235
  201.3 1.0 copy.234
  202.6 1.0 copy.233
  (184 shorter events, 38.0 us)
Async XLA Ops:
  0.6 2.7 %copy-start.12 = (bf16[1,128,2048]{2,1,0:T(8,128)(2,1)S(1)}, bf16[1,128,2048]{2,1,0:T(8,128)(2,1)}, u32[]{:S(2)}) copy-start(bf16[1,128,2048]{2,1,0:T(8,128)(2,1)} %param.14) | copy-start | bytes 1572868
  5.4 10.5 %copy-start.16 = (s32[4]{0:T(128)S(1)}, s32[4]{0:T(128)}, u32[]{:S(2)}) copy-start(s32[4]{0:T(128)} %param.19) | copy-start | bytes 52
  5.4 15.0 %copy-start.17 = (s32[4]{0:T(128)S(1)}, s32[4]{0:T(128)}, u32[]{:S(2)}) copy-start(s32[4]{0:T(128)} %param.18) | copy-start | bytes 52
  5.4 33.3 %all-to-all-start = ((bf16[3,16,128,128]{3,2,0,1:T(8,128)(2,1)}), bf16[3,16,128,128]{3,2,0,1:T(8,128)(2,1)S(1)}, u32[]{:S(2)}, u32[]{:S(2)}) async-start(bf16[3,16,128,128]{3,2,0,1:T(8,128)(2,1)} %copy.202), calls=%async_computation | async-start | bytes 3145728 | tf_op jit(solution)/shard_map/all_to_all | solution.py:360
  52.8 2.2 %copy-start.9 = (bf16[2,512,1,128]{3,1,2,0:T(8,128)(2,1)S(1)}, bf16[2,512,1,128]{3,1,2,0:T(8,128)(2,1)}, u32[]{:S(2)}) copy-start(bf16[2,512,1,128]{3,1,2,0:T(8,128)(2,1)} %get-tuple-element.1821) | copy-start | bytes 786436 | tf_op jit(solution)/shard_map/while
  57.0 0.7 copy-start.10
  65.4 2.2 %copy-start.9 = (bf16[2,512,1,128]{3,1,2,0:T(8,128)(2,1)S(1)}, bf16[2,512,1,128]{3,1,2,0:T(8,128)(2,1)}, u32[]{:S(2)}) copy-start(bf16[2,512,1,128]{3,1,2,0:T(8,128)(2,1)} %get-tuple-element.1821) | copy-start | bytes 786436 | tf_op jit(solution)/shard_map/while
  69.7 0.7 copy-start.10
  75.1 2.7 %copy-start.6 = (bf16[1024,2,1,128]{3,1,0,2:T(2,128)(2,1)S(1)}, bf16[1024,2,1,128]{3,1,0,2:T(2,128)(2,1)}, u32[]{:S(2)}) copy-start(bf16[1024,2,1,128]{3,1,0,2:T(2,128)(2,1)} %copy.215) | copy-start | bytes 1572868
  78.7 16.0 %copy-start.14 = (f32[2048]{0:T(1024)S(1)}, f32[2048]{0:T(1024)}, u32[]{:S(2)}) copy-start(f32[2048]{0:T(1024)} %param.16) | copy-start | bytes 24580
  78.7 15.8 %all-to-all-start.1 = ((bf16[16,128,128]{2,1,0:T(8,128)(2,1)}), bf16[16,128,128]{2,1,0:T(8,128)(2,1)S(1)}, u32[]{:S(2)}, u32[]{:S(2)}) async-start(bf16[16,128,128]{2,1,0:T(8,128)(2,1)} %bitcast.361), calls=%async_computation.1 | async-start | bytes 1048576 | tf_op jit(solution)/shard_map/all_to_all | solution.py:374
  85.2 16.4 %copy-start.15 = (f32[2048]{0:T(1024)S(1)}, f32[2048]{0:T(1024)}, u32[]{:S(2)}) copy-start(f32[2048]{0:T(1024)} %param.17) | copy-start | bytes 24580
  97.1 11.9 %all-to-all-start.4 = ((f32[16,2,128]{2,1,0:T(2,128)}), f32[16,2,128]{2,1,0:T(2,128)S(1)}, u32[]{:S(2)}, u32[]{:S(2)}) async-start(f32[16,2,128]{2,1,0:T(2,128)} %pad_maximum_fusion.7), calls=%async_computation.4 | async-start | bytes 32768 | tf_op jit(solution)/shard_map/all_to_all | solution.py:388
  109.0 15.0 %all-to-all-start.2 = ((bf16[16,128,128]{2,1,0:T(8,128)(2,1)}), bf16[16,128,128]{2,1,0:T(8,128)(2,1)S(1)}, u32[]{:S(2)}, u32[]{:S(2)}) async-start(bf16[16,128,128]{2,1,0:T(8,128)(2,1)} %get-tuple-element.1371), calls=%async_computation.2 | async-start | bytes 1048576 | tf_op jit(solution)/shard_map/all_to_all | solution.py:386
  124.6 47.0 %all-to-all-start.5 = ((f32[32,2,128]{2,1,0:T(2,128)}), f32[32,2,128]{2,1,0:T(2,128)S(1)}, u32[]{:S(2)}, u32[]{:S(2)}) async-start(f32[32,2,128]{2,1,0:T(2,128)} %broadcast_in_dim.146), calls=%async_computation.5 | async-start | bytes 65536 | tf_op jit(solution)/shard_map/all_to_all | solution.py:391
  137.8 1.1 copy-start.2
  141.1 1.5 copy-start.3
  142.9 1.0 copy-start
  142.9 1.2 copy-start.1
  142.9 1.2 copy-start.4
  152.4 1.0 copy-start.13
  162.4 1.0 copy-start.13
  165.7 0.9 copy-start.11
  165.8 4.0 %copy-start.5 = (bf16[16,128,128]{1,2,0:T(8,128)(2,1)S(1)}, bf16[16,128,128]{1,2,0:T(8,128)(2,1)}, u32[]{:S(2)}) copy-start(bf16[16,128,128]{1,2,0:T(8,128)(2,1)} %fusion.112) | copy-start | bytes 1572868
  166.3 3.7 %copy-start.7 = (bf16[16,128,128]{1,2,0:T(8,128)(2,1)S(1)}, bf16[16,128,128]{1,2,0:T(8,128)(2,1)}, u32[]{:S(2)}) copy-start(bf16[16,128,128]{1,2,0:T(8,128)(2,1)} %convolution_convert_fusion.1) | copy-start | bytes 1572868
  171.6 5.2 %copy-start.8 = (bf16[128,16,128]{2,0,1:T(8,128)(2,1)S(1)}, bf16[128,16,128]{2,0,1:T(8,128)(2,1)}, u32[]{:S(2)}) copy-start(bf16[128,16,128]{2,0,1:T(8,128)(2,1)} %get-tuple-element.1372) | copy-start | bytes 1572868
  171.6 28.0 %all-to-all-start.3 = ((bf16[3,16,128,128]{3,2,0,1:T(8,128)(2,1)}), bf16[3,16,128,128]{3,2,0,1:T(8,128)(2,1)S(1)}, u32[]{:S(2)}, u32[]{:S(2)}) async-start(bf16[3,16,128,128]{3,2,0,1:T(8,128)(2,1)} %pad_maximum_fusion.1), calls=%async_computation.3 | async-start | bytes 3145728 | tf_op jit(solution)/shard_map/all_to_all | solution.py:404
where the time goes:
time: 205 us; the launch traced here: 204 us
  waiting for transfers between devices  59.3 us (29%)
  starting transfers between devices  41.7 us (20%)
  other arithmetic  36.8 us (18%)
  local copies, waits for them, and re-layouts  33.6 us (16%)
  matrix products  22.1 us (11%)
  between operations  7.08 us (3%)
  loops' own time  3.06 us (1%)
    all_to_all x1, waiting for transfers between devices, shards(): lax.all_to_all(jnp.stack([part.reshape(ctx_count, tokens_here, width_here...  21 us
    all_to_all x1, waiting for transfers between devices, shards(): lax.all_to_all(stacked_in, 'ctx', split_axis=1, concat_axis=1, tiled=True)  15.7 us
    all_to_all x1, starting transfers between devices, shards(): both = jnp.sum(lax.all_to_all(both, 'dp', 0, 0, tiled=True), axis=0)  13.3 us
    all_to_all x1, waiting for transfers between devices, shards(): grad_attended = to_rows(lax.all_to_all(grad_hm, 'ctx', 0, 0, tiled=True))  11.2 us
    unnamed x41, local copies, waits for them, and re-layouts  10.7 us
    all_to_all x1, starting transfers between devices, shards(): lax.all_to_all(stacked_in, 'ctx', split_axis=1, concat_axis=1, tiled=True)  10.5 us
    all_to_all x1, waiting for transfers between devices, shards(): lax.all_to_all(attended.reshape(ctx_count, tokens_here, width_here), 'ctx...  6.97 us
    dot_general x2, matrix products, step(): jnp.einsum('qhd,khd->hqk', q_block, key_row_set, preferred_element_type=j...  5.5 us
  transfers between devices with their start and end apart: 6, of which 5 were waited for; matrix products, arithmetic and copies ran while one was open for 20% of the time, Pallas kernels for 0%

commit v1 on v0

--- a/solution.py
+++ b/solution.py
@@ -135,7 +135,7 @@
     dilation_rates,
 ):
     length_all, heads_here, head_size = query_row_set.shape
-    rows_per_block = min(512, length_all)
+    rows_per_block = length_all
     blocks = length_all // rows_per_block
     scaling = 1.0 / math.sqrt(head_size)
     key_positions = packed_positions(0, length_all, head_indices)
@@ -187,7 +187,7 @@
     dilation_rates,
 ):
     length_all, heads_here, head_size = query_row_set.shape
-    rows_per_block = min(512, length_all)
+    rows_per_block = length_all
     blocks = length_all // rows_per_block
     scaling = 1.0 / math.sqrt(head_size)
     key_positions = packed_positions(0, length_all, head_indices)

time: 205 us -> 189 us (0.922)
  other arithmetic: 36.8 us -> 19.5 us
  loops' own time: 3.06 us -> 0 us
  matrix products: 22.1 us -> 24.9 us
  local copies, waits for them, and re-layouts: 33.6 us -> 36.1 us
    unnamed x41 -> x39, local copies, waits for them, and re-layouts: 10.7 us -> 17.8 us
    dot_general x2 -> x0, matrix products: 5.5 us -> none  [step(): jnp.einsum('qhd,khd->hqk', q_block, key_row_set, preferred_element_type=j...]
    rem x12 -> x0, other arithmetic: 5.5 us -> none  [dilation_multiplier(): key_positions % dilation_rate == head_indices[:, None] % dilation_rate]
    dot_general x2 -> x1, matrix products: 0.76 us -> 5.95 us  [step(): jnp.einsum('hqk,qhd->khd', prob_bf, g_block, preferred_element_type=jnp.f...]
    ne x16 -> x0, other arithmetic: 4.5 us -> none  [dilation_multiplier(): key_positions[:, None, :] // seg_width]
    another operation x2 -> x0, loops' own time: 3.06 us -> none  [the longest x1 1.55 us: dilated_backward(): lax.scan(step, (zeros_all, zeros_all), jnp.arange(blocks, dtype=jnp.int32))]
    dot_general x2 -> x1, matrix products: 0.89 us -> 3.92 us  [step(): jnp.einsum('qhd,khd->hqk', g_block, value_row_set, preferred_element_type...]
    slice x5 -> x6, local copies, waits for them, and re-layouts: 3.42 us -> 6.35 us  [pick_rows(): return jnp.where(cond, pairs[:, 0], pairs[:, 1])]
  transfers between devices with their start and end apart: 6 -> 6, of which waited for: 5 -> 5; matrix products, arithmetic and copies ran while one was open for 20% -> 22% of each run, Pallas kernels for 0% -> 0%
where the time goes in v1:
time: 189 us; the launch traced here: 188 us
  waiting for transfers between devices  58.7 us (31%)
  starting transfers between devices  41.3 us (22%)
  local copies, waits for them, and re-layouts  36.1 us (19%)
  matrix products  24.9 us (13%)
  other arithmetic  19.5 us (10%)
  between operations  7.14 us (4%)
    all_to_all x1, waiting for transfers between devices, shards(): lax.all_to_all(jnp.stack([part.reshape(ctx_count, tokens_here, width_here...  21 us
    unnamed x39, local copies, waits for them, and re-layouts  17.8 us
    all_to_all x1, waiting for transfers between devices, shards(): lax.all_to_all(stacked_in, 'ctx', split_axis=1, concat_axis=1, tiled=True)  15 us
    all_to_all x1, starting transfers between devices, shards(): both = jnp.sum(lax.all_to_all(both, 'dp', 0, 0, tiled=True), axis=0)  13.2 us
    all_to_all x1, waiting for transfers between devices, shards(): grad_attended = to_rows(lax.all_to_all(grad_hm, 'ctx', 0, 0, tiled=True))  11.2 us
    all_to_all x1, starting transfers between devices, shards(): lax.all_to_all(stacked_in, 'ctx', split_axis=1, concat_axis=1, tiled=True)  10.3 us
    all_to_all x1, waiting for transfers between devices, shards(): lax.all_to_all(attended.reshape(ctx_count, tokens_here, width_here), 'ctx...  7 us
    slice x6, local copies, waits for them, and re-layouts, pick_rows(): return jnp.where(cond, pairs[:, 0], pairs[:, 1])  6.35 us
  transfers between devices with their start and end apart: 6, of which 5 were waited for; matrix products, arithmetic and copies ran while one was open for 22% of the time, Pallas kernels for 0%

profile of v1, /device:TPU:1, one launch (start us, length us, event | category | flops | bytes accessed | tf_op | source)
XLA Modules:
  0.0 187.6 jit_solution(13231519784178200614)
XLA Ops:
  0.6 1.3 copy.172
  1.9 1.3 copy.173
  3.3 1.3 copy.174
  4.8 1.6 copy.175
  6.4 10.3 %all-to-all-start = ((bf16[3,16,128,128]{3,2,0,1:T(8,128)(2,1)}), bf16[3,16,128,128]{3,2,0,1:T(8,128)(2,1)S(1)}, u32[]{:S(2)}, u32[]{:S(2)}) async-start(bf16[3,16,128,128]{3,2,0,1:T(8,128)(2,1)} %copy.175), calls=%async_computation | async-start | bytes 3145728 | tf_op jit(solution)/shard_map/all_to_all | solution.py:360
  24.5 15.0 %all-to-all-done = bf16[3,16,128,128]{3,2,0,1:T(8,128)(2,1)S(1)} async-done(((bf16[3,16,128,128]{3,2,0,1:T(8,128)(2,1)}), bf16[3,16,128,128]{3,2,0,1:T(8,128)(2,1)S(1)}, u32[]{:S(2)}, u32[]{:S(2)}) %all-to-all-start) | async-done | bytes 1572896 | tf_op jit(solution)/shard_map/all_to_all | solution.py:360
  40.7 1.1 fusion.80
  41.8 1.2 copy.226
  43.0 1.2 copy.227
  46.7 0.8 fusion.38
  47.6 3.1 %fusion.87 = (f32[1024]{0:T(1024)S(1)}, f32[1024,1024]{0,1:T(8,128)S(1)}) fusion(bf16[1024,128]{1,0:T(8,128)(2,1)S(1)} %fusion.40, bf16[1024,128]{1,0:T(8,128)(2,1)S(1)} %get-tuple-element.170, pred[1024]{0:T(1024)(128)(4,1)S(1)} %fusion.45, s32[1024]{0:T(1024)S(1)} %get-tuple-element.171, pred[1024]{0:T(1024)(128)(4,1)S(1)} %get-tuple-element.174, ...), kind=kOutput, calls=%fused_computation.159 | convolution fusion | flops 287308800 | bytes 4738048 | tf_op jit(solution)/shard_map/while/body/eval_jaxpr/qhd,khd->hqk/dot_general | solution.py:155
  50.7 1.9 %copy-done = f32[1024,1024]{0,1:T(8,128)} copy-done((f32[1024,1024]{0,1:T(8,128)}, f32[1024,1024]{0,1:T(8,128)S(1)}, u32[]{:S(2)}) %copy-start) | copy-done | bytes 4194328
  52.6 3.8 %multiply_reduce_fusion = f32[1024]{0:T(1024)S(1)} fusion(f32[1024,1024]{0,1:T(8,128)S(1)} %get-tuple-element.168, f32[1024]{0:T(1024)S(1)} %get-tuple-element.167, pred[1024]{0:T(1024)(128)(4,1)S(1)} %get-tuple-element.173, s32[1024]{0:T(1024)S(1)} %add_select_fusion.5, pred[1024]{0:T(1024)(128)(4,1)S(1)} %get-tuple-element.174, ...), kind=kLoop, calls=%fused_computation.3 | loop fusion | flops 17824768 | bytes 4217856 | tf_op jit(solution)/shard_map/while/body/eval_jaxpr/reduce_sum | solution.py:161
  57.1 5.9 %select_bitcast_fusion.7 = (bf16[1024,1,1,128]{0,3,2,1:T(8,128)(2,1)S(1)}, bf16[1024,1,1,128]{0,3,2,1:T(8,128)(2,1)S(1)}) fusion(pred[]{:T(512)} %bitcast.13, bf16[1024,128]{1,0:T(8,128)(2,1)} %get-tuple-element.169, f32[1024,1024]{0,1:T(8,128)} %copy-done, f32[1024]{0:T(1024)S(1)} %log_add_fusion.1, pred[1024]{0:T(1024)(128)(4,1)S(1)} %get-tuple-element.173, ...), kind=kOutput, calls=%fused_computation.85 | convolution fusion | flops 286654464 | bytes 5000193 | tf_op jit(solution)/shard_map/while/body/eval_jaxpr/hqk,khd->qhd/dot_general | solution.py:166
  63.0 0.8 pad_maximum_fusion.2
  63.8 1.3 copy.189
  65.5 0.9 add_convert_fusion.3
  66.4 4.4 %all-to-all-start.1 = ((bf16[16,128,128]{2,1,0:T(8,128)(2,1)}), bf16[16,128,128]{2,1,0:T(8,128)(2,1)S(1)}, u32[]{:S(2)}, u32[]{:S(2)}) async-start(bf16[16,128,128]{2,1,0:T(8,128)(2,1)} %bitcast.219), calls=%async_computation.1 | async-start | bytes 1048576 | tf_op jit(solution)/shard_map/all_to_all | solution.py:374
  70.8 2.0 %copy.191 = bf16[1,128,2048]{1,2,0:T(8,128)(2,1)} copy(bf16[1,128,2048]{2,1,0:T(8,128)(2,1)} %param.11) | data formatting | bytes 1048576 | tf_op args[3]
  72.9 2.2 %copy.192 = f32[128,16,128]{2,0,1:T(8,128)} copy(bf16[128,16,128]{0,2,1:T(8,128)(2,1)} %bitcast.229) | data formatting | bytes 1572864 | tf_op jit(solution)/shard_map/convert_element_type | solution.py:316
  75.1 7.0 %all-to-all-done.1 = bf16[16,128,128]{2,1,0:T(8,128)(2,1)S(1)} async-done(((bf16[16,128,128]{2,1,0:T(8,128)(2,1)}), bf16[16,128,128]{2,1,0:T(8,128)(2,1)S(1)}, u32[]{:S(2)}, u32[]{:S(2)}) %all-to-all-start.1) | async-done | bytes 524320 | tf_op jit(solution)/shard_map/all_to_all | solution.py:374
  82.3 1.7 fusion.25
  84.7 4.5 %all-to-all-start.4 = ((f32[16,2,128]{2,1,0:T(2,128)}), f32[16,2,128]{2,1,0:T(2,128)S(1)}, u32[]{:S(2)}, u32[]{:S(2)}) async-start(f32[16,2,128]{2,1,0:T(2,128)} %pad_maximum_fusion.6), calls=%async_computation.4 | async-start | bytes 32768 | tf_op jit(solution)/shard_map/all_to_all | solution.py:388
  89.2 2.8 %fusion.24 = (bf16[16,128,128]{2,1,0:T(8,128)(2,1)}, bf16[128,16,128]{2,0,1:T(8,128)(2,1)}) fusion(bf16[16,128,128]{2,1,0:T(8,128)(2,1)S(1)} %all-to-all-done.1, f32[128,16,128]{2,0,1:T(8,128)} %copy.192, f32[128]{0:T(128)S(1)} %broadcast_multiply_fusion, f32[128]{0:T(128)S(1)} %broadcast_multiply_fusion.1, f32[16,128]{1,0:T(8,128)S(1)} %bitcast.249, ...), kind=kLoop, calls=%fused_computation.44 | loop fusion | flops 3145728 | bytes 2639872 | tf_op jit(solution)/shard_map/convert_element_type | solution.py:325
  92.1 4.5 %all-to-all-done.4 = f32[16,2,128]{2,1,0:T(2,128)S(1)} async-done(((f32[16,2,128]{2,1,0:T(2,128)}), f32[16,2,128]{2,1,0:T(2,128)S(1)}, u32[]{:S(2)}, u32[]{:S(2)}) %all-to-all-start.4) | async-done | bytes 16416 | tf_op jit(solution)/shard_map/all_to_all | solution.py:388
  96.6 3.8 %all-to-all-start.2 = ((bf16[16,128,128]{2,1,0:T(8,128)(2,1)}), bf16[16,128,128]{2,1,0:T(8,128)(2,1)S(1)}, u32[]{:S(2)}, u32[]{:S(2)}) async-start(bf16[16,128,128]{2,1,0:T(8,128)(2,1)} %get-tuple-element.133), calls=%async_computation.2 | async-start | bytes 1048576 | tf_op jit(solution)/shard_map/all_to_all | solution.py:386
  100.4 11.2 %all-to-all-done.2 = bf16[16,128,128]{2,1,0:T(8,128)(2,1)S(1)} async-done(((bf16[16,128,128]{2,1,0:T(8,128)(2,1)}), bf16[16,128,128]{2,1,0:T(8,128)(2,1)S(1)}, u32[]{:S(2)}, u32[]{:S(2)}) %all-to-all-start.2) | async-done | bytes 524320 | tf_op jit(solution)/shard_map/all_to_all | solution.py:386
  112.2 13.2 %all-to-all-start.5 = ((f32[32,2,128]{2,1,0:T(2,128)}), f32[32,2,128]{2,1,0:T(2,128)S(1)}, u32[]{:S(2)}, u32[]{:S(2)}) async-start(f32[32,2,128]{2,1,0:T(2,128)} %broadcast_in_dim.151), calls=%async_computation.5 | async-start | bytes 65536 | tf_op jit(solution)/shard_map/all_to_all | solution.py:391
  125.5 1.4 fusion.27
  126.9 1.3 reshape.858
  128.1 2.3 %fusion.78 = (f32[1024,1,1]{1,0,2:T(8,128)}, f32[1024,1,1]{1,0,2:T(8,128)}) fusion(f32[1024,2,1]{1,0,2:T(8,128)} %reshape.858), kind=kLoop, calls=%fused_computation.150 | loop fusion | bytes 16384 | tf_op jit(solution)/shard_map/slice | solution.py:19
  130.4 1.2 copy.233
  131.7 1.2 copy.232
  133.7 6.0 %select_bitcast_fusion.1 = (bf16[1024,1,1,128]{0,3,2,1:T(8,128)(2,1)S(1)}, bf16[1024,1,1,128]{0,3,2,1:T(8,128)(2,1)S(1)}) fusion(pred[]{:T(512)} %bitcast.13, f32[1024,1024]{0,1:T(8,128)} %copy-done, f32[1024]{0:T(1024)S(1)} %get-tuple-element.123, pred[1024]{0:T(1024)(128)(4,1)S(1)} %fusion.45, s32[1024]{0:T(1024)S(1)} %get-tuple-element.171, ...), kind=kOutput, calls=%fused_computation.79 | convolution fusion | flops 286785536 | bytes 5262337 | tf_op jit(solution)/shard_map/while/body/eval_jaxpr/hqk,qhd->khd/dot_general | solution.py:227
  139.7 3.9 %multiply_convert_fusion = bf16[1024,1024]{0,1:T(8,128)(2,1)S(1)} fusion(bf16[1024,128]{1,0:T(8,128)(2,1)S(1)} %copy-done.7, f32[1024]{0:T(1024)S(1)} %bitcast.253, f32[1024,1024]{0,1:T(8,128)S(1)} %copy-done.1, f32[1024]{0:T(1024)S(1)} %get-tuple-element.123, pred[1024]{0:T(1024)(128)(4,1)S(1)} %fusion.45, s32[1024]{0:T(1024)S(1)} %get-tuple-element.171, ...), kind=kOutput, calls=%fused_computation | convolution fusion | flops 288489472 | bytes 7101441 | tf_op jit(solution)/shard_map/while/body/eval_jaxpr/qhd,khd->hqk/dot_general | solution.py:216
  143.6 1.6 select_bitcast_fusion.3
  145.2 1.3 select_bitcast_fusion.5
  146.5 1.1 convolution_convert_fusion
  149.3 1.1 pad_maximum_fusion.3
  150.8 1.8 pad_maximum_fusion.4
  152.6 1.3 copy.201
  154.4 1.3 pad_maximum_fusion.1
  155.7 5.0 %all-to-all-start.3 = ((bf16[3,16,128,128]{3,2,0,1:T(8,128)(2,1)}), bf16[3,16,128,128]{3,2,0,1:T(8,128)(2,1)S(1)}, u32[]{:S(2)}, u32[]{:S(2)}) async-start(bf16[3,16,128,128]{3,2,0,1:T(8,128)(2,1)} %pad_maximum_fusion.1), calls=%async_computation.3 | async-start | bytes 3145728 | tf_op jit(solution)/shard_map/all_to_all | solution.py:404
  161.0 1.0 copy.210
  162.6 21.0 %all-to-all-done.3 = bf16[3,16,128,128]{3,2,0,1:T(8,128)(2,1)S(1)} async-done(((bf16[3,16,128,128]{3,2,0,1:T(8,128)(2,1)}), bf16[3,16,128,128]{3,2,0,1:T(8,128)(2,1)S(1)}, u32[]{:S(2)}, u32[]{:S(2)}) %all-to-all-start.3) | async-done | bytes 1572896 | tf_op jit(solution)/shard_map/all_to_all | solution.py:404
  184.0 1.0 copy.213
  185.3 1.0 copy.212
  186.6 1.0 copy.211
  (73 shorter events, 13.0 us)
Async XLA Ops:
  4.6 12.1 %copy-start.10 = (s32[4]{0:T(128)S(1)}, s32[4]{0:T(128)}, u32[]{:S(2)}) copy-start(s32[4]{0:T(128)} %param.15) | copy-start | bytes 52
  4.6 16.7 %copy-start.11 = (s32[4]{0:T(128)S(1)}, s32[4]{0:T(128)}, u32[]{:S(2)}) copy-start(s32[4]{0:T(128)} %param.14) | copy-start | bytes 52
  6.4 33.2 %all-to-all-start = ((bf16[3,16,128,128]{3,2,0,1:T(8,128)(2,1)}), bf16[3,16,128,128]{3,2,0,1:T(8,128)(2,1)S(1)}, u32[]{:S(2)}, u32[]{:S(2)}) async-start(bf16[3,16,128,128]{3,2,0,1:T(8,128)(2,1)} %copy.175), calls=%async_computation | async-start | bytes 3145728 | tf_op jit(solution)/shard_map/all_to_all | solution.py:360
  47.6 3.1 %copy-start.5 = (bf16[1024,128]{1,0:T(8,128)(2,1)}, bf16[1024,128]{1,0:T(8,128)(2,1)S(1)}, u32[]{:S(2)}) copy-start(bf16[1024,128]{1,0:T(8,128)(2,1)S(1)} %get-tuple-element.170) | copy-start | bytes 786436
  50.7 2.0 %copy-start = (f32[1024,1024]{0,1:T(8,128)}, f32[1024,1024]{0,1:T(8,128)S(1)}, u32[]{:S(2)}) copy-start(f32[1024,1024]{0,1:T(8,128)S(1)} %get-tuple-element.168) | copy-start | bytes 12582916
  65.1 17.2 %copy-start.8 = (f32[2048]{0:T(1024)S(1)}, f32[2048]{0:T(1024)}, u32[]{:S(2)}) copy-start(f32[2048]{0:T(1024)} %param.12) | copy-start | bytes 24580
  65.5 23.7 %copy-start.9 = (f32[2048]{0:T(1024)S(1)}, f32[2048]{0:T(1024)}, u32[]{:S(2)}) copy-start(f32[2048]{0:T(1024)} %param.13) | copy-start | bytes 24580
  66.4 15.6 %all-to-all-start.1 = ((bf16[16,128,128]{2,1,0:T(8,128)(2,1)}), bf16[16,128,128]{2,1,0:T(8,128)(2,1)S(1)}, u32[]{:S(2)}, u32[]{:S(2)}) async-start(bf16[16,128,128]{2,1,0:T(8,128)(2,1)} %bitcast.219), calls=%async_computation.1 | async-start | bytes 1048576 | tf_op jit(solution)/shard_map/all_to_all | solution.py:374
  84.7 11.9 %all-to-all-start.4 = ((f32[16,2,128]{2,1,0:T(2,128)}), f32[16,2,128]{2,1,0:T(2,128)S(1)}, u32[]{:S(2)}, u32[]{:S(2)}) async-start(f32[16,2,128]{2,1,0:T(2,128)} %pad_maximum_fusion.6), calls=%async_computation.4 | async-start | bytes 32768 | tf_op jit(solution)/shard_map/all_to_all | solution.py:388
  96.6 15.0 %all-to-all-start.2 = ((bf16[16,128,128]{2,1,0:T(8,128)(2,1)}), bf16[16,128,128]{2,1,0:T(8,128)(2,1)S(1)}, u32[]{:S(2)}, u32[]{:S(2)}) async-start(bf16[16,128,128]{2,1,0:T(8,128)(2,1)} %get-tuple-element.133), calls=%async_computation.2 | async-start | bytes 1048576 | tf_op jit(solution)/shard_map/all_to_all | solution.py:386
  112.2 43.5 %all-to-all-start.5 = ((f32[32,2,128]{2,1,0:T(2,128)}), f32[32,2,128]{2,1,0:T(2,128)S(1)}, u32[]{:S(2)}, u32[]{:S(2)}) async-start(f32[32,2,128]{2,1,0:T(2,128)} %broadcast_in_dim.151), calls=%async_computation.5 | async-start | bytes 65536 | tf_op jit(solution)/shard_map/all_to_all | solution.py:391
  133.7 6.0 %copy-start.1 = (f32[1024,1024]{0,1:T(8,128)S(1)}, f32[1024,1024]{0,1:T(8,128)}, u32[]{:S(2)}) copy-start(f32[1024,1024]{0,1:T(8,128)} %copy-done) | copy-start | bytes 12582916
  133.7 6.0 %copy-start.7 = (bf16[1024,128]{1,0:T(8,128)(2,1)S(1)}, bf16[1024,128]{1,0:T(8,128)(2,1)}, u32[]{:S(2)}) copy-start(bf16[1024,128]{1,0:T(8,128)(2,1)} %get-tuple-element.169) | copy-start | bytes 786436
  139.7 5.6 %copy-start.6 = (bf16[1024,128]{1,0:T(8,128)(2,1)S(1)}, bf16[1024,128]{1,0:T(8,128)(2,1)}, u32[]{:S(2)}) copy-start(bf16[1024,128]{1,0:T(8,128)(2,1)} %copy-done.5) | copy-start | bytes 786436
  148.1 2.7 %copy-start.4 = (bf16[1024,1,1,128]{0,3,2,1:T(8,128)(2,1)S(1)}, bf16[1024,1,1,128]{0,3,2,1:T(8,128)(2,1)}, u32[]{:S(2)}) copy-start(bf16[1024,1,1,128]{0,3,2,1:T(8,128)(2,1)} %get-tuple-element.149) | copy-start | bytes 786436
  148.5 5.4 %copy-start.2 = (bf16[16,128,128]{1,2,0:T(8,128)(2,1)S(1)}, bf16[16,128,128]{1,2,0:T(8,128)(2,1)}, u32[]{:S(2)}) copy-start(bf16[16,128,128]{1,2,0:T(8,128)(2,1)} %convolution_convert_fusion) | copy-start | bytes 1572868
  154.2 6.5 %copy-start.3 = (bf16[128,16,128]{2,0,1:T(8,128)(2,1)S(1)}, bf16[128,16,128]{2,0,1:T(8,128)(2,1)}, u32[]{:S(2)}) copy-start(bf16[128,16,128]{2,0,1:T(8,128)(2,1)} %get-tuple-element.134) | copy-start | bytes 1572868
  155.7 27.9 %all-to-all-start.3 = ((bf16[3,16,128,128]{3,2,0,1:T(8,128)(2,1)}), bf16[3,16,128,128]{3,2,0,1:T(8,128)(2,1)S(1)}, u32[]{:S(2)}, u32[]{:S(2)}) async-start(bf16[3,16,128,128]{3,2,0,1:T(8,128)(2,1)} %pad_maximum_fusion.1), calls=%async_computation.3 | async-start | bytes 3145728 | tf_op jit(solution)/shard_map/all_to_all | solution.py:404

commit v2 on v1

--- a/solution.py
+++ b/solution.py
@@ -135,44 +135,29 @@
     dilation_rates,
 ):
     length_all, heads_here, head_size = query_row_set.shape
-    rows_per_block = length_all
-    blocks = length_all // rows_per_block
     scaling = 1.0 / math.sqrt(head_size)
-    key_positions = packed_positions(0, length_all, head_indices)
-
-    def one_block(block_id):
-        starting_row = block_id * rows_per_block
-        q_block = lax.dynamic_slice_in_dim(query_row_set, starting_row, rows_per_block, 0)
-        own_lse = lax.dynamic_slice_in_dim(baseline_logsumexp, starting_row, rows_per_block, 0).T
-        counted = dilation_multiplier(
-            packed_positions(starting_row, rows_per_block, head_indices),
-            key_positions,
-            head_indices,
-            segment_blocks,
-            dilation_rates,
-        )
-        scores = (
-            jnp.einsum("qhd,khd->hqk", q_block, key_row_set, preferred_element_type=jnp.float32)
-            * scaling
-        )
-        masked = jnp.where(counted > 0, scores, -1e30)
-        row_max = jnp.max(masked, axis=2)
-        part_lse = row_max + jnp.log(
-            jnp.sum(counted * jnp.exp(masked - row_max[:, :, None]), axis=2)
-        )
-        top = jnp.maximum(part_lse, own_lse)
-        log_norm = top + jnp.log(jnp.exp(part_lse - top) + jnp.exp(own_lse - top))
-        prob_bf = (counted * jnp.exp(masked - log_norm[:, :, None])).astype(jnp.bfloat16)
-        output = jnp.einsum(
-            "hqk,khd->qhd", prob_bf, value_row_set, preferred_element_type=jnp.float32
-        ).astype(jnp.bfloat16)
-        return (output, log_norm)
-
-    outputs, lse_blocks = lax.map(one_block, jnp.arange(blocks, dtype=jnp.int32))
-    return (
-        outputs.reshape(length_all, heads_here, head_size),
-        jnp.transpose(lse_blocks, (0, 2, 1)).reshape(length_all, heads_here),
-    )
+    positions = packed_positions(0, length_all, head_indices)
+    counted = dilation_multiplier(
+        positions, positions, head_indices, segment_blocks, dilation_rates
+    )
+    own_lse = baseline_logsumexp.T
+    scores = (
+        jnp.einsum("qhd,khd->hqk", query_row_set, key_row_set, preferred_element_type=jnp.float32)
+        * scaling
+    )
+    masked = jnp.where(counted > 0, scores, -1e30)
+    row_max = jnp.max(masked, axis=2)
+    part_lse = row_max + jnp.log(jnp.sum(counted * jnp.exp(masked - row_max[:, :, None]), axis=2))
+    top = jnp.maximum(part_lse, own_lse)
+    log_norm = top + jnp.log(jnp.exp(part_lse - top) + jnp.exp(own_lse - top))
+    prob_full = counted * jnp.exp(masked - log_norm[:, :, None])
+    output = jnp.einsum(
+        "hqk,khd->qhd",
+        prob_full.astype(jnp.bfloat16),
+        value_row_set,
+        preferred_element_type=jnp.float32,
+    ).astype(jnp.bfloat16)
+    return (output, log_norm.T, prob_full)
 
 
 def dilated_backward(
@@ -180,64 +165,28 @@
     key_row_set,
     value_row_set,
     grad_rows,
-    log_norm,
+    prob_full,
     delta_row,
-    head_indices,
-    segment_blocks,
-    dilation_rates,
-):
-    length_all, heads_here, head_size = query_row_set.shape
-    rows_per_block = length_all
-    blocks = length_all // rows_per_block
+):
+    head_size = query_row_set.shape[-1]
     scaling = 1.0 / math.sqrt(head_size)
-    key_positions = packed_positions(0, length_all, head_indices)
-
-    def step(carry, block_id):
-        acc_k, acc_v = carry
-        starting_row = block_id * rows_per_block
-        q_block = lax.dynamic_slice_in_dim(query_row_set, starting_row, rows_per_block, 0)
-        g_block = lax.dynamic_slice_in_dim(grad_rows, starting_row, rows_per_block, 0)
-        lse_block = lax.dynamic_slice_in_dim(log_norm, starting_row, rows_per_block, 0).T
-        delta_block = lax.dynamic_slice_in_dim(delta_row, starting_row, rows_per_block, 0).T
-        counted = dilation_multiplier(
-            packed_positions(starting_row, rows_per_block, head_indices),
-            key_positions,
-            head_indices,
-            segment_blocks,
-            dilation_rates,
-        )
-        scores = (
-            jnp.einsum("qhd,khd->hqk", q_block, key_row_set, preferred_element_type=jnp.float32)
-            * scaling
-        )
-        masked = jnp.where(counted > 0, scores, -1e30)
-        prob_full = counted * jnp.exp(masked - lse_block[:, :, None])
-        prob_bf = prob_full.astype(jnp.bfloat16)
-        grad_prob = jnp.einsum(
-            "qhd,khd->hqk", g_block, value_row_set, preferred_element_type=jnp.float32
-        )
-        grad_score = (prob_full * (grad_prob - delta_block[:, :, None])).astype(jnp.bfloat16)
-        grad_q = (
-            jnp.einsum("hqk,khd->qhd", grad_score, key_row_set, preferred_element_type=jnp.float32)
-            * scaling
-        ).astype(jnp.bfloat16)
-        acc_k = acc_k + jnp.einsum(
-            "hqk,qhd->khd", grad_score, q_block, preferred_element_type=jnp.float32
-        )
-        acc_v = acc_v + jnp.einsum(
-            "hqk,qhd->khd", prob_bf, g_block, preferred_element_type=jnp.float32
-        )
-        return ((acc_k, acc_v), grad_q)
-
-    zeros_all = jnp.zeros((length_all, heads_here, head_size), jnp.float32)
-    (acc_k, acc_v), grad_q = lax.scan(
-        step, (zeros_all, zeros_all), jnp.arange(blocks, dtype=jnp.int32)
-    )
-    return (
-        grad_q.reshape(length_all, heads_here, head_size),
-        (acc_k * scaling).astype(jnp.bfloat16),
-        acc_v.astype(jnp.bfloat16),
-    )
+    prob_bf = prob_full.astype(jnp.bfloat16)
+    grad_prob = jnp.einsum(
+        "qhd,khd->hqk", grad_rows, value_row_set, preferred_element_type=jnp.float32
+    )
+    grad_score = (prob_full * (grad_prob - delta_row.T[:, :, None])).astype(jnp.bfloat16)
+    grad_q = (
+        jnp.einsum("hqk,khd->qhd", grad_score, key_row_set, preferred_element_type=jnp.float32)
+        * scaling
+    ).astype(jnp.bfloat16)
+    grad_k = (
+        jnp.einsum("hqk,qhd->khd", grad_score, query_row_set, preferred_element_type=jnp.float32)
+        * scaling
+    ).astype(jnp.bfloat16)
+    grad_v = jnp.einsum(
+        "hqk,qhd->khd", prob_bf, grad_rows, preferred_element_type=jnp.float32
+    ).astype(jnp.bfloat16)
+    return (grad_q, grad_k, grad_v)
 
 
 def dense_attention_forward(
@@ -245,7 +194,7 @@
 ):
     parity = head_indices % 2
     own_lse = local_lse(query_row_set, key_row_set)
-    packed_out, packed_lse = sparse_attention_forward(
+    packed_out, packed_lse, prob_full = sparse_attention_forward(
         pick_rows(query_row_set, parity),
         pick_rows(key_row_set, parity),
         pick_rows(value_row_set, parity),
@@ -258,7 +207,7 @@
     attended = add_parts(
         local_output(query_row_set, key_row_set, value_row_set, log_norm), packed_out, parity
     )
-    return (attended, log_norm)
+    return (attended, log_norm, prob_full)
 
 
 def full_backward(
@@ -268,9 +217,8 @@
     attended,
     grad_attended,
     log_norm,
+    prob_full,
     head_indices,
-    segment_blocks,
-    dilation_rates,
 ):
     parity = head_indices % 2
     delta_row = jnp.sum(grad_attended.astype(jnp.float32) * attended.astype(jnp.float32), axis=2)
@@ -282,11 +230,8 @@
         pick_rows(key_row_set, parity),
         pick_rows(value_row_set, parity),
         pick_rows(grad_attended, parity),
-        pick_rows(log_norm, parity),
+        prob_full,
         pick_rows(delta_row, parity),
-        head_indices,
-        segment_blocks,
-        dilation_rates,
     )
     return tuple(
         (
@@ -363,7 +308,7 @@
         to_rows(stacked_in[1]),
         to_rows(stacked_in[2]),
     )
-    attended, log_norm = dense_attention_forward(
+    attended, log_norm, prob_full = dense_attention_forward(
         query_head_tensor,
         key_head_tensor,
         value_head_tensor,
@@ -397,9 +342,8 @@
         attended,
         grad_attended,
         log_norm,
+        prob_full,
         head_indices,
-        segment_blocks,
-        dilation_rates,
     )
     stacked_out = lax.all_to_all(
         jnp.stack([part.reshape(ctx_count, tokens_here, width_here) for part in (grad_q, grad_k, grad_v)]),

time: 189 us -> 201 us (1.063)
  local copies, waits for them, and re-layouts: 36.1 us -> 48.5 us
  matrix products: 24.9 us -> 14.8 us
  other arithmetic: 19.5 us -> 28.6 us
    dot_general x6, matrix products: 21.8 us -> 10.6 us  [the longest x1 3.5 us: dilated_backward(): jnp.einsum('hqk,qhd->khd', prob_bf, grad_rows, preferred_element_type=jnp...]
    mul x0 -> x1, other arithmetic: none -> 5.31 us  [sparse_attention_forward(): prob_full = counted * jnp.exp(masked - log_norm[:, :, None])]
    another operation x5, local copies, waits for them, and re-layouts: 3.66 us -> 8.33 us  [spread_rows(): return jnp.stack([first_branch, second], axis=1).reshape(base.shape)]
    slice x6, local copies, waits for them, and re-layouts: 6.35 us -> 10.3 us  [pick_rows(): return jnp.where(cond, pairs[:, 0], pairs[:, 1])]
    unnamed x39 -> x55, local copies, waits for them, and re-layouts: 17.8 us -> 20.7 us
    select_n x4 -> x3, other arithmetic: 0.92 us -> 3.02 us  [pick_rows(): return jnp.where(cond, pairs[:, 0], pairs[:, 1])]
  transfers between devices with their start and end apart: 6 -> 6, of which waited for: 5 -> 5; matrix products, arithmetic and copies ran while one was open for 22% -> 21% of each run, Pallas kernels for 0% -> 0%
where the time goes in v2:
time: 201 us; the launch traced here: 199 us
  waiting for transfers between devices  58.8 us (29%)
  local copies, waits for them, and re-layouts  48.5 us (24%)
  starting transfers between devices  41.3 us (21%)
  other arithmetic  28.6 us (14%)
  matrix products  14.8 us (7%)
  between operations  7.04 us (4%)
    all_to_all x1, waiting for transfers between devices, shards(): lax.all_to_all(jnp.stack([part.reshape(ctx_count, tokens_here, width_here...  21 us
    unnamed x55, local copies, waits for them, and re-layouts  20.7 us
    all_to_all x1, waiting for transfers between devices, shards(): lax.all_to_all(stacked_in, 'ctx', split_axis=1, concat_axis=1, tiled=True)  15.1 us
    all_to_all x1, starting transfers between devices, shards(): both = jnp.sum(lax.all_to_all(both, 'dp', 0, 0, tiled=True), axis=0)  13.2 us
    all_to_all x1, waiting for transfers between devices, shards(): grad_attended = to_rows(lax.all_to_all(grad_hm, 'ctx', 0, 0, tiled=True))  11.2 us
    all_to_all x1, starting transfers between devices, shards(): lax.all_to_all(stacked_in, 'ctx', split_axis=1, concat_axis=1, tiled=True)  10.3 us
    slice x6, local copies, waits for them, and re-layouts, pick_rows(): return jnp.where(cond, pairs[:, 0], pairs[:, 1])  10.3 us
    another operation x5, local copies, waits for them, and re-layouts, spread_rows(): return jnp.stack([first_branch, second], axis=1).reshape(base.shape)  8.33 us
  transfers between devices with their start and end apart: 6, of which 5 were waited for; matrix products, arithmetic and copies ran while one was open for 21% of the time, Pallas kernels for 0%

profile of v2, /device:TPU:1, one launch (start us, length us, event | category | flops | bytes accessed | tf_op | source)
XLA Modules:
  0.0 199.1 jit_solution(12748967873068116032)
XLA Ops:
  0.6 1.3 copy.174
  1.9 1.3 copy.173
  3.3 1.3 copy.172
  4.8 1.6 copy.175
  6.4 10.3 %all-to-all-start = ((bf16[3,16,128,128]{3,2,0,1:T(8,128)(2,1)}), bf16[3,16,128,128]{3,2,0,1:T(8,128)(2,1)S(1)}, u32[]{:S(2)}, u32[]{:S(2)}) async-start(bf16[3,16,128,128]{3,2,0,1:T(8,128)(2,1)} %copy.175), calls=%async_computation | async-start | bytes 3145728 | tf_op jit(solution)/shard_map/all_to_all | solution.py:305
  24.4 15.1 %all-to-all-done = bf16[3,16,128,128]{3,2,0,1:T(8,128)(2,1)S(1)} async-done(((bf16[3,16,128,128]{3,2,0,1:T(8,128)(2,1)}), bf16[3,16,128,128]{3,2,0,1:T(8,128)(2,1)S(1)}, u32[]{:S(2)}, u32[]{:S(2)}) %all-to-all-start) | async-done | bytes 1572896 | tf_op jit(solution)/shard_map/all_to_all | solution.py:305
  39.7 1.7 fusion.78
  41.4 1.7 fusion.76
  43.0 1.7 fusion.77
  45.9 1.2 fusion.75
  47.1 1.2 copy.226
  48.3 1.3 fusion.35
  49.6 1.7 fusion.33
  52.1 3.1 %fusion.82 = (f32[1024]{0:T(1024)S(1)}, f32[1024,1024]{0,1:T(8,128)S(1)}) fusion(bf16[1024,128]{1,0:T(8,128)(2,1)S(1)} %fusion.35, bf16[1024,128]{1,0:T(8,128)(2,1)S(1)} %get-tuple-element.88, pred[1024]{0:T(1024)(128)(4,1)S(1)} %fusion.40, s32[1024]{0:T(1024)S(1)} %get-tuple-element.89, pred[1024]{0:T(1024)(128)(4,1)S(1)} %get-tuple-element.92, ...), kind=kOutput, calls=%fused_computation.156 | convolution fusion | flops 287308800 | bytes 4738048 | tf_op jit(solution)/shard_map/qhd,khd->hqk/dot_general | solution.py:145
  55.2 1.9 copy-done.2
  57.2 3.8 %multiply_reduce_fusion = f32[1024]{0:T(1024)S(1)} fusion(f32[1024,1024]{0,1:T(8,128)S(1)} %get-tuple-element.86, f32[1024]{0:T(1024)S(1)} %get-tuple-element.85, s32[1024]{0:T(1024)S(1)} %get-tuple-element.89, s32[1024]{0:T(1024)S(1)} %get-tuple-element.90, s32[1024]{0:T(1024)S(1)} %add_select_fusion.5, pred[1024]{0:T(1024)(128)(4,1)S(1)} %fusion.40, ...), kind=kLoop, calls=%fused_computation.2 | loop fusion | flops 17824768 | bytes 4217856 | tf_op jit(solution)/shard_map/reduce_sum | solution.py:150
  61.2 5.3 %exponential_multiply_fusion = f32[1024,1024]{0,1:T(8,128)S(1)} fusion(f32[1024,1024]{0,1:T(8,128)} %copy-done.2, f32[1024]{0:T(1024)S(1)} %log_add_fusion.1, s32[1024]{0:T(1024)S(1)} %get-tuple-element.89, s32[1024]{0:T(1024)S(1)} %get-tuple-element.90, s32[1024]{0:T(1024)S(1)} %add_select_fusion.5, pred[1024]{0:T(1024)(128)(4,1)S(1)} %fusion.40, ...), kind=kLoop, calls=%fused_computation.1 | loop fusion | flops 16777216 | bytes 8408064 | tf_op jit(solution)/shard_map/mul | solution.py:153
  66.6 1.9 copy-done
  69.8 1.3 copy.189
  72.2 1.3 sub.154
  74.8 4.4 %all-to-all-start.1 = ((bf16[16,128,128]{2,1,0:T(8,128)(2,1)}), bf16[16,128,128]{2,1,0:T(8,128)(2,1)S(1)}, u32[]{:S(2)}, u32[]{:S(2)}) async-start(bf16[16,128,128]{2,1,0:T(8,128)(2,1)} %bitcast.218), calls=%async_computation.1 | async-start | bytes 1048576 | tf_op jit(solution)/shard_map/all_to_all | solution.py:319
  79.2 2.0 %copy.191 = bf16[1,128,2048]{1,2,0:T(8,128)(2,1)} copy(bf16[1,128,2048]{2,1,0:T(8,128)(2,1)} %param.11) | data formatting | bytes 1048576 | tf_op args[3]
  81.3 2.2 %copy.192 = f32[128,16,128]{2,0,1:T(8,128)} copy(bf16[128,16,128]{0,2,1:T(8,128)(2,1)} %bitcast.228) | data formatting | bytes 1572864 | tf_op jit(solution)/shard_map/convert_element_type | solution.py:261
  83.5 7.0 %all-to-all-done.1 = bf16[16,128,128]{2,1,0:T(8,128)(2,1)S(1)} async-done(((bf16[16,128,128]{2,1,0:T(8,128)(2,1)}), bf16[16,128,128]{2,1,0:T(8,128)(2,1)S(1)}, u32[]{:S(2)}, u32[]{:S(2)}) %all-to-all-start.1) | async-done | bytes 524320 | tf_op jit(solution)/shard_map/all_to_all | solution.py:319
  90.7 1.7 fusion.18
  93.1 4.5 %all-to-all-start.4 = ((f32[16,2,128]{2,1,0:T(2,128)}), f32[16,2,128]{2,1,0:T(2,128)S(1)}, u32[]{:S(2)}, u32[]{:S(2)}) async-start(f32[16,2,128]{2,1,0:T(2,128)} %pad_maximum_fusion.6), calls=%async_computation.4 | async-start | bytes 32768 | tf_op jit(solution)/shard_map/all_to_all | solution.py:333
  97.6 2.8 %fusion.17 = (bf16[16,128,128]{2,1,0:T(8,128)(2,1)}, bf16[128,16,128]{2,0,1:T(8,128)(2,1)}) fusion(bf16[16,128,128]{2,1,0:T(8,128)(2,1)S(1)} %all-to-all-done.1, f32[128,16,128]{2,0,1:T(8,128)} %copy.192, f32[128]{0:T(128)S(1)} %broadcast_multiply_fusion, f32[128]{0:T(128)S(1)} %broadcast_multiply_fusion.1, f32[16,128]{1,0:T(8,128)S(1)} %bitcast.244, ...), kind=kLoop, calls=%fused_computation.40 | loop fusion | flops 3145728 | bytes 2639872 | tf_op jit(solution)/shard_map/convert_element_type | solution.py:270
  100.5 4.5 %all-to-all-done.4 = f32[16,2,128]{2,1,0:T(2,128)S(1)} async-done(((f32[16,2,128]{2,1,0:T(2,128)}), f32[16,2,128]{2,1,0:T(2,128)S(1)}, u32[]{:S(2)}, u32[]{:S(2)}) %all-to-all-start.4) | async-done | bytes 16416 | tf_op jit(solution)/shard_map/all_to_all | solution.py:333
  105.0 3.8 %all-to-all-start.2 = ((bf16[16,128,128]{2,1,0:T(8,128)(2,1)}), bf16[16,128,128]{2,1,0:T(8,128)(2,1)S(1)}, u32[]{:S(2)}, u32[]{:S(2)}) async-start(bf16[16,128,128]{2,1,0:T(8,128)(2,1)} %get-tuple-element.51), calls=%async_computation.2 | async-start | bytes 1048576 | tf_op jit(solution)/shard_map/all_to_all | solution.py:331
  108.8 11.2 %all-to-all-done.2 = bf16[16,128,128]{2,1,0:T(8,128)(2,1)S(1)} async-done(((bf16[16,128,128]{2,1,0:T(8,128)(2,1)}), bf16[16,128,128]{2,1,0:T(8,128)(2,1)S(1)}, u32[]{:S(2)}, u32[]{:S(2)}) %all-to-all-start.2) | async-done | bytes 524320 | tf_op jit(solution)/shard_map/all_to_all | solution.py:331
  120.6 13.2 %all-to-all-start.5 = ((f32[32,2,128]{2,1,0:T(2,128)}), f32[32,2,128]{2,1,0:T(2,128)S(1)}, u32[]{:S(2)}, u32[]{:S(2)}) async-start(f32[32,2,128]{2,1,0:T(2,128)} %broadcast_in_dim.94), calls=%async_computation.5 | async-start | bytes 65536 | tf_op jit(solution)/shard_map/all_to_all | solution.py:336
  133.9 1.7 fusion.74
  135.6 1.4 fusion.20
  137.0 1.3 reshape.784
  138.2 2.3 %fusion.73 = (f32[1024,1,1]{1,0,2:T(8,128)}, f32[1024,1,1]{1,0,2:T(8,128)}) fusion(f32[1024,2,1]{1,0,2:T(8,128)} %reshape.784), kind=kLoop, calls=%fused_computation.147 | loop fusion | bytes 16384 | tf_op jit(solution)/shard_map/slice | solution.py:19
  140.6 1.2 copy.232
  141.8 1.2 copy.233
  143.0 3.5 %select_bitcast_fusion.1 = (bf16[1024,1,1,128]{0,3,2,1:T(8,128)(2,1)S(1)}, bf16[1024,1,1,128]{0,3,2,1:T(8,128)(2,1)S(1)}) fusion(pred[]{:T(512)} %bitcast.13, f32[1024,1024]{0,1:T(8,128)} %copy-done, bf16[1024,1,1,128]{3,1,0,2:T(2,128)(2,1)} %get-tuple-element.56, bf16[1024,1,1,128]{3,1,0,2:T(2,128)(2,1)} %get-tuple-element.55), kind=kOutput, calls=%fused_computation.77 | convolution fusion | flops 270008320 | bytes 5242881 | tf_op jit(solution)/shard_map/hqk,qhd->khd/dot_general | solution.py:186
  147.8 1.6 select_bitcast_fusion.3
  151.4 2.0 %copy.202 = bf16[1024,2,1,128]{3,1,0,2:T(2,128)(2,1)} copy(bf16[1024,2,1,128]{0,3,2,1:T(8,128)(2,1)} %pad_maximum_fusion.5) | data formatting | bytes 1048576 | tf_op jit(solution)/shard_map/stack | solution.py:27
  154.5 1.9 pad_maximum_fusion.4
  156.4 2.0 %copy.201 = bf16[1024,2,1,128]{3,1,0,2:T(2,128)(2,1)} copy(bf16[1024,2,1,128]{0,3,2,1:T(8,128)(2,1)} %pad_maximum_fusion.4) | data formatting | bytes 1048576 | tf_op jit(solution)/shard_map/stack | solution.py:27
  160.9 2.0 %copy.200 = bf16[1024,2,1,128]{3,1,0,2:T(2,128)(2,1)} copy(bf16[1024,2,1,128]{0,3,2,1:T(8,128)(2,1)} %pad_maximum_fusion.3) | data formatting | bytes 1048576 | tf_op jit(solution)/shard_map/stack | solution.py:27
  162.9 1.4 fusion.3
  164.4 1.2 add_convert_fusion
  165.9 1.3 pad_maximum_fusion.1
  167.2 5.0 %all-to-all-start.3 = ((bf16[3,16,128,128]{3,2,0,1:T(8,128)(2,1)}), bf16[3,16,128,128]{3,2,0,1:T(8,128)(2,1)S(1)}, u32[]{:S(2)}, u32[]{:S(2)}) async-start(bf16[3,16,128,128]{3,2,0,1:T(8,128)(2,1)} %pad_maximum_fusion.1), calls=%async_computation.3 | async-start | bytes 3145728 | tf_op jit(solution)/shard_map/all_to_all | solution.py:348
  174.1 21.0 %all-to-all-done.3 = bf16[3,16,128,128]{3,2,0,1:T(8,128)(2,1)S(1)} async-done(((bf16[3,16,128,128]{3,2,0,1:T(8,128)(2,1)}), bf16[3,16,128,128]{3,2,0,1:T(8,128)(2,1)S(1)}, u32[]{:S(2)}, u32[]{:S(2)}) %all-to-all-start.3) | async-done | bytes 1572896 | tf_op jit(solution)/shard_map/all_to_all | solution.py:348
  (90 shorter events, 22.2 us)
Async XLA Ops:
  4.6 12.1 %copy-start.18 = (s32[4]{0:T(128)S(1)}, s32[4]{0:T(128)}, u32[]{:S(2)}) copy-start(s32[4]{0:T(128)} %param.15) | copy-start | bytes 52
  4.6 16.7 %copy-start.19 = (s32[4]{0:T(128)S(1)}, s32[4]{0:T(128)}, u32[]{:S(2)}) copy-start(s32[4]{0:T(128)} %param.14) | copy-start | bytes 52
  6.4 33.2 %all-to-all-start = ((bf16[3,16,128,128]{3,2,0,1:T(8,128)(2,1)}), bf16[3,16,128,128]{3,2,0,1:T(8,128)(2,1)S(1)}, u32[]{:S(2)}, u32[]{:S(2)}) async-start(bf16[3,16,128,128]{3,2,0,1:T(8,128)(2,1)} %copy.175), calls=%async_computation | async-start | bytes 3145728 | tf_op jit(solution)/shard_map/all_to_all | solution.py:305
  49.6 1.8 copy-start.11
  51.4 0.7 copy-start.14
  55.2 2.0 copy-start.2
  55.2 5.8 %copy-start.10 = (f32[1024,1,1]{1,0,2:T(8,128)S(1)}, f32[1024,1,1]{1,0,2:T(8,128)}, u32[]{:S(2)}) copy-start(f32[1024,1,1]{1,0,2:T(8,128)} %get-tuple-element.57) | copy-start | bytes 12292
  66.6 2.0 copy-start
  72.2 18.5 %copy-start.16 = (f32[2048]{0:T(1024)S(1)}, f32[2048]{0:T(1024)}, u32[]{:S(2)}) copy-start(f32[2048]{0:T(1024)} %param.12) | copy-start | bytes 24580
  73.9 23.7 %copy-start.17 = (f32[2048]{0:T(1024)S(1)}, f32[2048]{0:T(1024)}, u32[]{:S(2)}) copy-start(f32[2048]{0:T(1024)} %param.13) | copy-start | bytes 24580
  74.8 15.6 %all-to-all-start.1 = ((bf16[16,128,128]{2,1,0:T(8,128)(2,1)}), bf16[16,128,128]{2,1,0:T(8,128)(2,1)S(1)}, u32[]{:S(2)}, u32[]{:S(2)}) async-start(bf16[16,128,128]{2,1,0:T(8,128)(2,1)} %bitcast.218), calls=%async_computation.1 | async-start | bytes 1048576 | tf_op jit(solution)/shard_map/all_to_all | solution.py:319
  93.1 11.9 %all-to-all-start.4 = ((f32[16,2,128]{2,1,0:T(2,128)}), f32[16,2,128]{2,1,0:T(2,128)S(1)}, u32[]{:S(2)}, u32[]{:S(2)}) async-start(f32[16,2,128]{2,1,0:T(2,128)} %pad_maximum_fusion.6), calls=%async_computation.4 | async-start | bytes 32768 | tf_op jit(solution)/shard_map/all_to_all | solution.py:333
  105.0 15.0 %all-to-all-start.2 = ((bf16[16,128,128]{2,1,0:T(8,128)(2,1)}), bf16[16,128,128]{2,1,0:T(8,128)(2,1)S(1)}, u32[]{:S(2)}, u32[]{:S(2)}) async-start(bf16[16,128,128]{2,1,0:T(8,128)(2,1)} %get-tuple-element.51), calls=%async_computation.2 | async-start | bytes 1048576 | tf_op jit(solution)/shard_map/all_to_all | solution.py:331
  120.6 46.6 %all-to-all-start.5 = ((f32[32,2,128]{2,1,0:T(2,128)}), f32[32,2,128]{2,1,0:T(2,128)S(1)}, u32[]{:S(2)}, u32[]{:S(2)}) async-start(f32[32,2,128]{2,1,0:T(2,128)} %broadcast_in_dim.94), calls=%async_computation.5 | async-start | bytes 65536 | tf_op jit(solution)/shard_map/all_to_all | solution.py:336
  143.0 3.8 %copy-start.1 = (f32[1024,1024]{0,1:T(8,128)S(1)}, f32[1024,1024]{0,1:T(8,128)}, u32[]{:S(2)}) copy-start(f32[1024,1024]{0,1:T(8,128)} %copy-done) | copy-start | bytes 12582916
  143.0 3.9 %copy-start.7 = (bf16[1024,1,1,128]{3,1,0,2:T(2,128)(2,1)S(1)}, bf16[1024,1,1,128]{3,1,0,2:T(2,128)(2,1)}, u32[]{:S(2)}) copy-start(bf16[1024,1,1,128]{3,1,0,2:T(2,128)(2,1)} %get-tuple-element.55) | copy-start | bytes 786436
  143.0 4.0 %copy-start.8 = (bf16[1024,1,1,128]{3,1,0,2:T(2,128)(2,1)S(1)}, bf16[1024,1,1,128]{3,1,0,2:T(2,128)(2,1)}, u32[]{:S(2)}) copy-start(bf16[1024,1,1,128]{3,1,0,2:T(2,128)(2,1)} %get-tuple-element.56) | copy-start | bytes 786436
  146.5 1.2 copy-start.12
  147.0 2.4 %copy-start.15 = (bf16[1024,128]{1,0:T(8,128)(2,1)S(1)}, bf16[1024,128]{1,0:T(8,128)(2,1)}, u32[]{:S(2)}) copy-start(bf16[1024,128]{1,0:T(8,128)(2,1)} %copy-done.14) | copy-start | bytes 786436
  158.4 1.6 copy-start.13
  158.9 0.8 copy-start.3
  159.7 4.6 %copy-start.4 = (bf16[1024,2,1,128]{3,1,0,2:T(2,128)(2,1)S(1)}, bf16[1024,2,1,128]{3,1,0,2:T(2,128)(2,1)}, u32[]{:S(2)}) copy-start(bf16[1024,2,1,128]{3,1,0,2:T(2,128)(2,1)} %copy.202) | copy-start | bytes 1572868
  159.7 5.8 %copy-start.5 = (bf16[1024,2,1,128]{3,1,0,2:T(2,128)(2,1)S(1)}, bf16[1024,2,1,128]{3,1,0,2:T(2,128)(2,1)}, u32[]{:S(2)}) copy-start(bf16[1024,2,1,128]{3,1,0,2:T(2,128)(2,1)} %copy.201) | copy-start | bytes 1572868
  162.9 2.8 %copy-start.6 = (bf16[1024,2,1,128]{3,1,0,2:T(2,128)(2,1)S(1)}, bf16[1024,2,1,128]{3,1,0,2:T(2,128)(2,1)}, u32[]{:S(2)}) copy-start(bf16[1024,2,1,128]{3,1,0,2:T(2,128)(2,1)} %copy.200) | copy-start | bytes 1572868
  165.7 6.5 %copy-start.9 = (bf16[128,16,128]{2,0,1:T(8,128)(2,1)S(1)}, bf16[128,16,128]{2,0,1:T(8,128)(2,1)}, u32[]{:S(2)}) copy-start(bf16[128,16,128]{2,0,1:T(8,128)(2,1)} %get-tuple-element.52) | copy-start | bytes 1572868
  167.2 27.9 %all-to-all-start.3 = ((bf16[3,16,128,128]{3,2,0,1:T(8,128)(2,1)}), bf16[3,16,128,128]{3,2,0,1:T(8,128)(2,1)S(1)}, u32[]{:S(2)}, u32[]{:S(2)}) async-start(bf16[3,16,128,128]{3,2,0,1:T(8,128)(2,1)} %pad_maximum_fusion.1), calls=%async_computation.3 | async-start | bytes 3145728 | tf_op jit(solution)/shard_map/all_to_all | solution.py:348

commit v3 on v1

--- a/solution.py
+++ b/solution.py
@@ -113,12 +113,10 @@
     )
     for dilation_branch in range(1, G):
         seg_width = segment_blocks[dilation_branch] * BLK
-        dilation_rate = dilation_rates[dilation_branch]
-        same_seg = (
-            query_positions[:, :, None] // seg_width == key_positions[:, None, :] // seg_width
-        )
-        selected_queries = query_positions % dilation_rate == head_indices[:, None] % dilation_rate
-        selected_keys = key_positions % dilation_rate == head_indices[:, None] % dilation_rate
+        low_bits = dilation_rates[dilation_branch] - 1
+        same_seg = (query_positions[:, :, None] ^ key_positions[:, None, :]) < seg_width
+        selected_queries = ((query_positions ^ head_indices[:, None]) & low_bits) == 0
+        selected_keys = ((key_positions ^ head_indices[:, None]) & low_bits) == 0
         counted = counted + (
             same_seg & selected_queries[:, :, None] & selected_keys[:, None, :]
         ).astype(jnp.float32)

time: 189 us -> 188 us (level)
  waiting for transfers between devices: 58.7 us -> 61.4 us
  between operations: 7.14 us -> 5.05 us
    all_to_all x1, waiting for transfers between devices: 15 us -> 17.7 us  [shards(): lax.all_to_all(stacked_in, 'ctx', split_axis=1, concat_axis=1, tiled=True)]
  transfers between devices with their start and end apart: 6 -> 6, of which waited for: 5 -> 5; matrix products, arithmetic and copies ran while one was open for 22% -> 21% of each run, Pallas kernels for 0% -> 0%
where the time goes in v3:
time: 188 us; the launch traced here: 187 us
  waiting for transfers between devices  61.4 us (33%)
  starting transfers between devices  41.3 us (22%)
  local copies, waits for them, and re-layouts  35.9 us (19%)
  matrix products  24.4 us (13%)
  other arithmetic  18.8 us (10%)
  between operations  5.05 us (3%)
    all_to_all x1, waiting for transfers between devices, shards(): lax.all_to_all(jnp.stack([part.reshape(ctx_count, tokens_here, width_here...  21 us
    unnamed x39, local copies, waits for them, and re-layouts  17.8 us
    all_to_all x1, waiting for transfers between devices, shards(): lax.all_to_all(stacked_in, 'ctx', split_axis=1, concat_axis=1, tiled=True)  17.7 us
    all_to_all x1, starting transfers between devices, shards(): both = jnp.sum(lax.all_to_all(both, 'dp', 0, 0, tiled=True), axis=0)  13.2 us
    all_to_all x1, waiting for transfers between devices, shards(): grad_attended = to_rows(lax.all_to_all(grad_hm, 'ctx', 0, 0, tiled=True))  11.2 us
    all_to_all x1, starting transfers between devices, shards(): lax.all_to_all(stacked_in, 'ctx', split_axis=1, concat_axis=1, tiled=True)  10.3 us
    all_to_all x1, waiting for transfers between devices, shards(): lax.all_to_all(attended.reshape(ctx_count, tokens_here, width_here), 'ctx...  7.01 us
    slice x6, local copies, waits for them, and re-layouts, pick_rows(): return jnp.where(cond, pairs[:, 0], pairs[:, 1])  6.35 us
  transfers between devices with their start and end apart: 6, of which 5 were waited for; matrix products, arithmetic and copies ran while one was open for 21% of the time, Pallas kernels for 0%

profile of v3, /device:TPU:1, one launch (start us, length us, event | category | flops | bytes accessed | tf_op | source)
XLA Modules:
  0.0 187.0 jit_solution(15872272002224957903)
XLA Ops:
  0.6 1.3 copy.172
  1.9 1.3 copy.173
  3.3 1.3 copy.174
  4.8 1.6 copy.175
  6.4 10.3 %all-to-all-start = ((bf16[3,16,128,128]{3,2,0,1:T(8,128)(2,1)}), bf16[3,16,128,128]{3,2,0,1:T(8,128)(2,1)S(1)}, u32[]{:S(2)}, u32[]{:S(2)}) async-start(bf16[3,16,128,128]{3,2,0,1:T(8,128)(2,1)} %copy.175), calls=%async_computation | async-start | bytes 3145728 | tf_op jit(solution)/shard_map/all_to_all | solution.py:358
  21.9 17.7 %all-to-all-done = bf16[3,16,128,128]{3,2,0,1:T(8,128)(2,1)S(1)} async-done(((bf16[3,16,128,128]{3,2,0,1:T(8,128)(2,1)}), bf16[3,16,128,128]{3,2,0,1:T(8,128)(2,1)S(1)}, u32[]{:S(2)}, u32[]{:S(2)}) %all-to-all-start) | async-done | bytes 1572896 | tf_op jit(solution)/shard_map/all_to_all | solution.py:358
  40.7 1.1 fusion.64
  41.8 1.2 copy.226
  43.0 1.2 copy.227
  46.7 0.8 fusion.47
  47.5 3.2 %fusion.71 = (f32[1024]{0:T(1024)S(1)}, f32[1024,1024]{0,1:T(8,128)S(1)}) fusion(bf16[1024,128]{1,0:T(8,128)(2,1)S(1)} %fusion.49, bf16[1024,128]{1,0:T(8,128)(2,1)S(1)} %get-tuple-element.172, pred[1024]{0:T(1024)(128)(4,1)S(1)} %get-tuple-element.169, s32[]{:T(128)} %bitcast.19, pred[1024]{0:T(1024)(128)(4,1)S(1)} %get-tuple-element.170, s32[]{:T(128)} %bitcast.17, ...), kind=kOutput, calls=%fused_computation.134 | convolution fusion | flops 288357376 | bytes 4729868 | tf_op jit(solution)/shard_map/while/body/eval_jaxpr/qhd,khd->hqk/dot_general | solution.py:153
  50.7 1.9 %copy-done = f32[1024,1024]{0,1:T(8,128)} copy-done((f32[1024,1024]{0,1:T(8,128)}, f32[1024,1024]{0,1:T(8,128)S(1)}, u32[]{:S(2)}) %copy-start) | copy-done | bytes 4194328
  52.6 3.6 %multiply_reduce_fusion = f32[1024]{0:T(1024)S(1)} fusion(f32[1024,1024]{0,1:T(8,128)S(1)} %get-tuple-element.168, f32[1024]{0:T(1024)S(1)} %get-tuple-element.167, pred[1024]{0:T(1024)(128)(4,1)S(1)} %get-tuple-element.169, s32[]{:T(128)} %bitcast.19, s32[1024]{0:T(1024)S(1)} %multiply_add_fusion, pred[1024]{0:T(1024)(128)(4,1)S(1)} %get-tuple-element.170, ...), kind=kLoop, calls=%fused_computation.6 | loop fusion | flops 18873344 | bytes 4209676 | tf_op jit(solution)/shard_map/while/body/eval_jaxpr/reduce_sum | solution.py:159
  56.9 5.6 %select_bitcast_fusion.7 = (bf16[1024,1,1,128]{0,3,2,1:T(8,128)(2,1)S(1)}, bf16[1024,1,1,128]{0,3,2,1:T(8,128)(2,1)S(1)}) fusion(pred[]{:T(512)} %bitcast.13, bf16[1024,128]{1,0:T(8,128)(2,1)} %get-tuple-element.171, f32[1024,1024]{0,1:T(8,128)} %copy-done, f32[1024]{0:T(1024)S(1)} %log_add_fusion.1, pred[1024]{0:T(1024)(128)(4,1)S(1)} %get-tuple-element.169, ...), kind=kOutput, calls=%fused_computation.91 | convolution fusion | flops 287703040 | bytes 4992013 | tf_op jit(solution)/shard_map/while/body/eval_jaxpr/hqk,khd->qhd/dot_general | solution.py:164
  62.5 0.8 pad_maximum_fusion.2
  63.4 1.3 copy.189
  65.1 0.9 add_convert_fusion.3
  66.0 4.4 %all-to-all-start.1 = ((bf16[16,128,128]{2,1,0:T(8,128)(2,1)}), bf16[16,128,128]{2,1,0:T(8,128)(2,1)S(1)}, u32[]{:S(2)}, u32[]{:S(2)}) async-start(bf16[16,128,128]{2,1,0:T(8,128)(2,1)} %bitcast.209), calls=%async_computation.1 | async-start | bytes 1048576 | tf_op jit(solution)/shard_map/all_to_all | solution.py:372
  70.4 2.0 %copy.191 = bf16[1,128,2048]{1,2,0:T(8,128)(2,1)} copy(bf16[1,128,2048]{2,1,0:T(8,128)(2,1)} %param.11) | data formatting | bytes 1048576 | tf_op args[3]
  72.4 2.2 %copy.192 = f32[128,16,128]{2,0,1:T(8,128)} copy(bf16[128,16,128]{0,2,1:T(8,128)(2,1)} %bitcast.219) | data formatting | bytes 1572864 | tf_op jit(solution)/shard_map/convert_element_type | solution.py:314
  74.6 7.0 %all-to-all-done.1 = bf16[16,128,128]{2,1,0:T(8,128)(2,1)S(1)} async-done(((bf16[16,128,128]{2,1,0:T(8,128)(2,1)}), bf16[16,128,128]{2,1,0:T(8,128)(2,1)S(1)}, u32[]{:S(2)}, u32[]{:S(2)}) %all-to-all-start.1) | async-done | bytes 524320 | tf_op jit(solution)/shard_map/all_to_all | solution.py:372
  81.9 1.7 fusion.34
  84.2 4.5 %all-to-all-start.4 = ((f32[16,2,128]{2,1,0:T(2,128)}), f32[16,2,128]{2,1,0:T(2,128)S(1)}, u32[]{:S(2)}, u32[]{:S(2)}) async-start(f32[16,2,128]{2,1,0:T(2,128)} %pad_maximum_fusion.6), calls=%async_computation.4 | async-start | bytes 32768 | tf_op jit(solution)/shard_map/all_to_all | solution.py:386
  88.8 2.8 %fusion.33 = (bf16[16,128,128]{2,1,0:T(8,128)(2,1)}, bf16[128,16,128]{2,0,1:T(8,128)(2,1)}) fusion(bf16[16,128,128]{2,1,0:T(8,128)(2,1)S(1)} %all-to-all-done.1, f32[128,16,128]{2,0,1:T(8,128)} %copy.192, f32[128]{0:T(128)S(1)} %broadcast_multiply_fusion, f32[128]{0:T(128)S(1)} %broadcast_multiply_fusion.1, f32[16,128]{1,0:T(8,128)S(1)} %bitcast.239, ...), kind=kLoop, calls=%fused_computation.50 | loop fusion | flops 3145728 | bytes 2639872 | tf_op jit(solution)/shard_map/convert_element_type | solution.py:323
  91.6 4.5 %all-to-all-done.4 = f32[16,2,128]{2,1,0:T(2,128)S(1)} async-done(((f32[16,2,128]{2,1,0:T(2,128)}), f32[16,2,128]{2,1,0:T(2,128)S(1)}, u32[]{:S(2)}, u32[]{:S(2)}) %all-to-all-start.4) | async-done | bytes 16416 | tf_op jit(solution)/shard_map/all_to_all | solution.py:386
  96.1 3.8 %all-to-all-start.2 = ((bf16[16,128,128]{2,1,0:T(8,128)(2,1)}), bf16[16,128,128]{2,1,0:T(8,128)(2,1)S(1)}, u32[]{:S(2)}, u32[]{:S(2)}) async-start(bf16[16,128,128]{2,1,0:T(8,128)(2,1)} %get-tuple-element.133), calls=%async_computation.2 | async-start | bytes 1048576 | tf_op jit(solution)/shard_map/all_to_all | solution.py:384
  99.9 11.2 %all-to-all-done.2 = bf16[16,128,128]{2,1,0:T(8,128)(2,1)S(1)} async-done(((bf16[16,128,128]{2,1,0:T(8,128)(2,1)}), bf16[16,128,128]{2,1,0:T(8,128)(2,1)S(1)}, u32[]{:S(2)}, u32[]{:S(2)}) %all-to-all-start.2) | async-done | bytes 524320 | tf_op jit(solution)/shard_map/all_to_all | solution.py:384
  111.8 13.2 %all-to-all-start.5 = ((f32[32,2,128]{2,1,0:T(2,128)}), f32[32,2,128]{2,1,0:T(2,128)S(1)}, u32[]{:S(2)}, u32[]{:S(2)}) async-start(f32[32,2,128]{2,1,0:T(2,128)} %broadcast_in_dim.151), calls=%async_computation.5 | async-start | bytes 65536 | tf_op jit(solution)/shard_map/all_to_all | solution.py:389
  125.0 1.4 fusion.36
  126.4 1.3 reshape.663
  127.7 2.3 %fusion.62 = (f32[1024,1,1]{1,0,2:T(8,128)}, f32[1024,1,1]{1,0,2:T(8,128)}) fusion(f32[1024,2,1]{1,0,2:T(8,128)} %reshape.663), kind=kLoop, calls=%fused_computation.125 | loop fusion | bytes 16384 | tf_op jit(solution)/shard_map/slice | solution.py:19
  130.0 1.2 copy.233
  131.2 1.2 copy.232
  133.2 5.7 %select_bitcast_fusion.1 = (bf16[1024,1,1,128]{0,3,2,1:T(8,128)(2,1)S(1)}, bf16[1024,1,1,128]{0,3,2,1:T(8,128)(2,1)S(1)}) fusion(pred[]{:T(512)} %bitcast.13, f32[1024,1024]{0,1:T(8,128)} %copy-done, f32[1024]{0:T(1024)S(1)} %get-tuple-element.123, pred[1024]{0:T(1024)(128)(4,1)S(1)} %get-tuple-element.169, s32[]{:T(128)} %bitcast.19, ...), kind=kOutput, calls=%fused_computation.85 | convolution fusion | flops 287834112 | bytes 5254157 | tf_op jit(solution)/shard_map/while/body/eval_jaxpr/hqk,qhd->khd/dot_general | solution.py:225
  138.9 4.0 %multiply_convert_fusion = bf16[1024,1024]{0,1:T(8,128)(2,1)S(1)} fusion(bf16[1024,128]{1,0:T(8,128)(2,1)S(1)} %copy-done.7, f32[1024]{0:T(1024)S(1)} %bitcast.243, f32[1024,1024]{0,1:T(8,128)S(1)} %copy-done.1, f32[1024]{0:T(1024)S(1)} %get-tuple-element.123, pred[1024]{0:T(1024)(128)(4,1)S(1)} %get-tuple-element.169, s32[]{:T(128)} %bitcast.19, ...), kind=kOutput, calls=%fused_computation.3 | convolution fusion | flops 289538048 | bytes 7093261 | tf_op jit(solution)/shard_map/while/body/eval_jaxpr/qhd,khd->hqk/dot_general | solution.py:214
  142.9 1.6 select_bitcast_fusion.3
  144.6 1.3 select_bitcast_fusion.5
  145.9 1.1 convolution_convert_fusion
  148.6 1.1 pad_maximum_fusion.3
  150.2 1.8 pad_maximum_fusion.4
  151.9 1.3 copy.201
  153.7 1.3 pad_maximum_fusion.1
  155.1 5.0 %all-to-all-start.3 = ((bf16[3,16,128,128]{3,2,0,1:T(8,128)(2,1)}), bf16[3,16,128,128]{3,2,0,1:T(8,128)(2,1)S(1)}, u32[]{:S(2)}, u32[]{:S(2)}) async-start(bf16[3,16,128,128]{3,2,0,1:T(8,128)(2,1)} %pad_maximum_fusion.1), calls=%async_computation.3 | async-start | bytes 3145728 | tf_op jit(solution)/shard_map/all_to_all | solution.py:402
  160.4 1.0 copy.210
  162.0 21.0 %all-to-all-done.3 = bf16[3,16,128,128]{3,2,0,1:T(8,128)(2,1)S(1)} async-done(((bf16[3,16,128,128]{3,2,0,1:T(8,128)(2,1)}), bf16[3,16,128,128]{3,2,0,1:T(8,128)(2,1)S(1)}, u32[]{:S(2)}, u32[]{:S(2)}) %all-to-all-start.3) | async-done | bytes 1572896 | tf_op jit(solution)/shard_map/all_to_all | solution.py:402
  183.4 1.0 copy.213
  184.6 1.0 copy.212
  185.9 1.0 copy.211
  (72 shorter events, 12.4 us)
Async XLA Ops:
  4.6 12.2 %copy-start.10 = (s32[4]{0:T(128)S(1)}, s32[4]{0:T(128)}, u32[]{:S(2)}) copy-start(s32[4]{0:T(128)} %param.14) | copy-start | bytes 52
  4.6 14.7 %copy-start.11 = (s32[4]{0:T(128)S(1)}, s32[4]{0:T(128)}, u32[]{:S(2)}) copy-start(s32[4]{0:T(128)} %param.15) | copy-start | bytes 52
  6.4 33.2 %all-to-all-start = ((bf16[3,16,128,128]{3,2,0,1:T(8,128)(2,1)}), bf16[3,16,128,128]{3,2,0,1:T(8,128)(2,1)S(1)}, u32[]{:S(2)}, u32[]{:S(2)}) async-start(bf16[3,16,128,128]{3,2,0,1:T(8,128)(2,1)} %copy.175), calls=%async_computation | async-start | bytes 3145728 | tf_op jit(solution)/shard_map/all_to_all | solution.py:358
  47.5 3.2 %copy-start.5 = (bf16[1024,128]{1,0:T(8,128)(2,1)}, bf16[1024,128]{1,0:T(8,128)(2,1)S(1)}, u32[]{:S(2)}) copy-start(bf16[1024,128]{1,0:T(8,128)(2,1)S(1)} %get-tuple-element.172) | copy-start | bytes 786436
  50.7 1.9 %copy-start = (f32[1024,1024]{0,1:T(8,128)}, f32[1024,1024]{0,1:T(8,128)S(1)}, u32[]{:S(2)}) copy-start(f32[1024,1024]{0,1:T(8,128)S(1)} %get-tuple-element.168) | copy-start | bytes 12582916
  64.7 17.2 %copy-start.8 = (f32[2048]{0:T(1024)S(1)}, f32[2048]{0:T(1024)}, u32[]{:S(2)}) copy-start(f32[2048]{0:T(1024)} %param.12) | copy-start | bytes 24580
  65.1 23.7 %copy-start.9 = (f32[2048]{0:T(1024)S(1)}, f32[2048]{0:T(1024)}, u32[]{:S(2)}) copy-start(f32[2048]{0:T(1024)} %param.13) | copy-start | bytes 24580
  66.0 15.6 %all-to-all-start.1 = ((bf16[16,128,128]{2,1,0:T(8,128)(2,1)}), bf16[16,128,128]{2,1,0:T(8,128)(2,1)S(1)}, u32[]{:S(2)}, u32[]{:S(2)}) async-start(bf16[16,128,128]{2,1,0:T(8,128)(2,1)} %bitcast.209), calls=%async_computation.1 | async-start | bytes 1048576 | tf_op jit(solution)/shard_map/all_to_all | solution.py:372
  84.2 11.9 %all-to-all-start.4 = ((f32[16,2,128]{2,1,0:T(2,128)}), f32[16,2,128]{2,1,0:T(2,128)S(1)}, u32[]{:S(2)}, u32[]{:S(2)}) async-start(f32[16,2,128]{2,1,0:T(2,128)} %pad_maximum_fusion.6), calls=%async_computation.4 | async-start | bytes 32768 | tf_op jit(solution)/shard_map/all_to_all | solution.py:386
  96.1 15.0 %all-to-all-start.2 = ((bf16[16,128,128]{2,1,0:T(8,128)(2,1)}), bf16[16,128,128]{2,1,0:T(8,128)(2,1)S(1)}, u32[]{:S(2)}, u32[]{:S(2)}) async-start(bf16[16,128,128]{2,1,0:T(8,128)(2,1)} %get-tuple-element.133), calls=%async_computation.2 | async-start | bytes 1048576 | tf_op jit(solution)/shard_map/all_to_all | solution.py:384
  111.8 43.3 %all-to-all-start.5 = ((f32[32,2,128]{2,1,0:T(2,128)}), f32[32,2,128]{2,1,0:T(2,128)S(1)}, u32[]{:S(2)}, u32[]{:S(2)}) async-start(f32[32,2,128]{2,1,0:T(2,128)} %broadcast_in_dim.151), calls=%async_computation.5 | async-start | bytes 65536 | tf_op jit(solution)/shard_map/all_to_all | solution.py:389
  133.2 5.7 %copy-start.1 = (f32[1024,1024]{0,1:T(8,128)S(1)}, f32[1024,1024]{0,1:T(8,128)}, u32[]{:S(2)}) copy-start(f32[1024,1024]{0,1:T(8,128)} %copy-done) | copy-start | bytes 12582916
  133.2 5.7 %copy-start.7 = (bf16[1024,128]{1,0:T(8,128)(2,1)S(1)}, bf16[1024,128]{1,0:T(8,128)(2,1)}, u32[]{:S(2)}) copy-start(bf16[1024,128]{1,0:T(8,128)(2,1)} %get-tuple-element.171) | copy-start | bytes 786436
  138.9 5.6 %copy-start.6 = (bf16[1024,128]{1,0:T(8,128)(2,1)S(1)}, bf16[1024,128]{1,0:T(8,128)(2,1)}, u32[]{:S(2)}) copy-start(bf16[1024,128]{1,0:T(8,128)(2,1)} %copy-done.5) | copy-start | bytes 786436
  147.5 2.7 %copy-start.4 = (bf16[1024,1,1,128]{0,3,2,1:T(8,128)(2,1)S(1)}, bf16[1024,1,1,128]{0,3,2,1:T(8,128)(2,1)}, u32[]{:S(2)}) copy-start(bf16[1024,1,1,128]{0,3,2,1:T(8,128)(2,1)} %get-tuple-element.149) | copy-start | bytes 786436
  147.8 5.4 %copy-start.2 = (bf16[16,128,128]{1,2,0:T(8,128)(2,1)S(1)}, bf16[16,128,128]{1,2,0:T(8,128)(2,1)}, u32[]{:S(2)}) copy-start(bf16[16,128,128]{1,2,0:T(8,128)(2,1)} %convolution_convert_fusion) | copy-start | bytes 1572868
  153.6 6.5 %copy-start.3 = (bf16[128,16,128]{2,0,1:T(8,128)(2,1)S(1)}, bf16[128,16,128]{2,0,1:T(8,128)(2,1)}, u32[]{:S(2)}) copy-start(bf16[128,16,128]{2,0,1:T(8,128)(2,1)} %get-tuple-element.134) | copy-start | bytes 1572868
  155.1 27.9 %all-to-all-start.3 = ((bf16[3,16,128,128]{3,2,0,1:T(8,128)(2,1)}), bf16[3,16,128,128]{3,2,0,1:T(8,128)(2,1)S(1)}, u32[]{:S(2)}, u32[]{:S(2)}) async-start(bf16[3,16,128,128]{3,2,0,1:T(8,128)(2,1)} %pad_maximum_fusion.1), calls=%async_computation.3 | async-start | bytes 3145728 | tf_op jit(solution)/shard_map/all_to_all | solution.py:402

commit v4 on v3

--- a/solution.py
+++ b/solution.py
@@ -3,6 +3,8 @@
 import jax
 import jax.numpy as jnp
 from jax import lax
+from jax.experimental import pallas as pl
+from jax.experimental.pallas import tpu as pltpu
 from jax.sharding import PartitionSpec as P
 
 H = 16
@@ -121,6 +123,92 @@
             same_seg & selected_queries[:, :, None] & selected_keys[:, None, :]
         ).astype(jnp.float32)
     return counted
+
+
+def dilated_mask(params_ref, rows, keys, row_first):
+    head = params_ref[2 * G]
+    parity = params_ref[2 * G + 1]
+    query_positions = 2 * (row_first + lax.broadcasted_iota(jnp.int32, (rows, keys), 0)) + parity
+    key_positions = 2 * lax.broadcasted_iota(jnp.int32, (rows, keys), 1) + parity
+    apart = query_positions ^ key_positions
+    query_phase = query_positions ^ head
+    key_phase = key_positions ^ head
+    counted = jnp.zeros((rows, keys), jnp.float32)
+    for branch in range(1, G):
+        low_bits = params_ref[G + branch]
+        kept = (
+            (apart < params_ref[branch])
+            & ((query_phase & low_bits) == 0)
+            & ((key_phase & low_bits) == 0)
+        )
+        counted = counted + jnp.where(kept, 1.0, 0.0)
+    return counted
+
+
+def dilated_forward_kernel(params_ref, q_ref, k_ref, v_ref, own_ref, out_ref, lse_ref):
+    rows, head_size = q_ref.shape
+    keys = k_ref.shape[0]
+    scaling = 1.0 / math.sqrt(head_size)
+    counted = dilated_mask(params_ref, rows, keys, pl.program_id(0) * rows)
+    scores = (
+        lax.dot_general(
+            q_ref[...], k_ref[...], (((1,), (1,)), ((), ())), preferred_element_type=jnp.float32
+        )
+        * scaling
+    )
+    masked = jnp.where(counted > 0, scores, -1e30)
+    row_max = jnp.max(masked, axis=1, keepdims=True)
+    part_lse = row_max + jnp.log(
+        jnp.sum(counted * jnp.exp(masked - row_max), axis=1, keepdims=True)
+    )
+    own_lse = own_ref[...]
+    top = jnp.maximum(part_lse, own_lse)
+    log_norm = top + jnp.log(jnp.exp(part_lse - top) + jnp.exp(own_lse - top))
+    prob_bf = (counted * jnp.exp(masked - log_norm)).astype(jnp.bfloat16)
+    out_ref[...] = jnp.dot(prob_bf, v_ref[...], preferred_element_type=jnp.float32).astype(
+        out_ref.dtype
+    )
+    lse_ref[...] = log_norm
+
+
+def mask_params(head, segment_blocks, dilation_rates):
+    return jnp.concatenate(
+        [
+            segment_blocks.astype(jnp.int32) * BLK,
+            dilation_rates.astype(jnp.int32) - 1,
+            jnp.stack([head, head % 2]).astype(jnp.int32),
+        ]
+    )
+
+
+def dilated_forward_call(params, q, k, v, own, row_block=256):
+    rows, head_size = q.shape
+    keys = k.shape[0]
+    grid = (rows // row_block,)
+    return pl.pallas_call(
+        dilated_forward_kernel,
+        grid=grid,
+        in_specs=[
+            pl.BlockSpec(memory_space=pltpu.SMEM),
+            pl.BlockSpec((row_block, head_size), lambda i: (i, 0)),
+            pl.BlockSpec((keys, head_size), lambda i: (0, 0)),
+            pl.BlockSpec((keys, head_size), lambda i: (0, 0)),
+            pl.BlockSpec((row_block, 1), lambda i: (i, 0)),
+        ],
+        out_specs=[
+            pl.BlockSpec((row_block, head_size), lambda i: (i, 0)),
+            pl.BlockSpec((row_block, 1), lambda i: (i, 0)),
+        ],
+        out_shape=[
+            jax.ShapeDtypeStruct((rows, head_size), jnp.bfloat16),
+            jax.ShapeDtypeStruct((rows, 1), jnp.float32),
+        ],
+        cost_estimate=pl.CostEstimate(
+            flops=4 * rows * keys * head_size,
+            transcendentals=rows * keys,
+            bytes_accessed=2 * (3 * rows * head_size + rows * head_size) + 8 * rows,
+        ),
+    )(params, q, k, v, own)
 
 
 def sparse_attention_forward(
@@ -243,15 +331,26 @@
 ):
     parity = head_indices % 2
     own_lse = local_lse(query_row_set, key_row_set)
-    packed_out, packed_lse = sparse_attention_forward(
-        pick_rows(query_row_set, parity),
-        pick_rows(key_row_set, parity),
-        pick_rows(value_row_set, parity),
-        pick_rows(own_lse, parity),
-        head_indices,
-        segment_blocks,
-        dilation_rates,
-    )
+    if query_row_set.shape[1] == 1:
+        params = mask_params(head_indices[0], segment_blocks, dilation_rates)
+        packed_out, packed_lse = dilated_forward_call(
+            params,
+            pick_rows(query_row_set, parity)[:, 0],
+            pick_rows(key_row_set, parity)[:, 0],
+            pick_rows(value_row_set, parity)[:, 0],
+            pick_rows(own_lse, parity),
+        )
+        packed_out = packed_out[:, None]
+    else:
+        packed_out, packed_lse = sparse_attention_forward(
+            pick_rows(query_row_set, parity),
+            pick_rows(key_row_set, parity),
+            pick_rows(value_row_set, parity),
+            pick_rows(own_lse, parity),
+            head_indices,
+            segment_blocks,
+            dilation_rates,
+        )
     log_norm = spread_rows(packed_lse, parity, own_lse)
     attended = add_parts(
         local_output(query_row_set, key_row_set, value_row_set, log_norm), packed_out, parity

time: 188 us -> 171 us (0.910)
  local copies, waits for them, and re-layouts: 35.9 us -> 24.5 us
  matrix products: 24.4 us -> 15.8 us
  Pallas kernels: 0 us -> 7.48 us
  waiting for transfers between devices: 61.4 us -> 54.5 us
    pallas_call x0 -> x1, Pallas kernels: none -> 7.48 us  [dilated_forward_call(): pl.pallas_call(dilated_forward_kernel, grid=grid, in_specs=[pl.BlockSpec(...]
    unnamed x39 -> x37, local copies, waits for them, and re-layouts: 17.8 us -> 10.5 us
    all_to_all x1, waiting for transfers between devices: 11.2 us -> 5.01 us  [shards(): grad_attended = to_rows(lax.all_to_all(grad_hm, 'ctx', 0, 0, tiled=True))]
    select_n x4 -> x5, other arithmetic: 0.93 us -> 6.06 us  [pick_rows(): return jnp.where(cond, pairs[:, 0], pairs[:, 1])]
    all_to_all x1, waiting for transfers between devices: 7.01 us -> 1.89 us  [shards(): lax.all_to_all(attended.reshape(ctx_count, tokens_here, width_here), 'ctx...]
    all_to_all x1, waiting for transfers between devices: 17.7 us -> 22.2 us  [shards(): lax.all_to_all(stacked_in, 'ctx', split_axis=1, concat_axis=1, tiled=True)]
    reduce_sum x1 -> x0, other arithmetic: 3.65 us -> none  [one_block(): jnp.sum(counted * jnp.exp(masked - row_max[:, :, None]), axis=2)]
    slice x6 -> x4, local copies, waits for them, and re-layouts: 6.35 us -> 2.92 us  [pick_rows(): return jnp.where(cond, pairs[:, 0], pairs[:, 1])]
  transfers between devices with their start and end apart: 6 -> 6, of which waited for: 5 -> 5; matrix products, arithmetic and copies ran while one was open for 21% -> 22% of each run, Pallas kernels for 0% -> 0%
where the time goes in v4:
time: 171 us; the launch traced here: 170 us
  waiting for transfers between devices  54.5 us (32%)
  starting transfers between devices  42.5 us (25%)
  local copies, waits for them, and re-layouts  24.5 us (14%)
  other arithmetic  20.2 us (12%)
  matrix products  15.8 us (9%)
  Pallas kernels  7.48 us (4%)
  between operations  4.94 us (3%)
    all_to_all x1, waiting for transfers between devices, shards(): lax.all_to_all(stacked_in, 'ctx', split_axis=1, concat_axis=1, tiled=True)  22.2 us
    all_to_all x1, waiting for transfers between devices, shards(): lax.all_to_all(jnp.stack([part.reshape(ctx_count, tokens_here, width_here...  21 us
    all_to_all x1, starting transfers between devices, shards(): both = jnp.sum(lax.all_to_all(both, 'dp', 0, 0, tiled=True), axis=0)  13.3 us
    unnamed x37, local copies, waits for them, and re-layouts  10.5 us
    all_to_all x1, starting transfers between devices, shards(): lax.all_to_all(stacked_in, 'ctx', split_axis=1, concat_axis=1, tiled=True)  10.5 us
    pallas_call x1, Pallas kernels, dilated_forward_call(): pl.pallas_call(dilated_forward_kernel, grid=grid, in_specs=[pl.BlockSpec(...  7.48 us
    dot_general x1, matrix products, step(): jnp.einsum('qhd,khd->hqk', q_block, key_row_set, preferred_element_type=j...  6.22 us
    select_n x5, other arithmetic, pick_rows(): return jnp.where(cond, pairs[:, 0], pairs[:, 1])  6.06 us
  transfers between devices with their start and end apart: 6, of which 5 were waited for; matrix products, arithmetic and copies ran while one was open for 22% of the time, Pallas kernels for 0%

profile of v4, /device:TPU:1, one launch (start us, length us, event | category | flops | bytes accessed | tf_op | source)
XLA Modules:
  0.0 169.9 jit_solution(10563886128543550786)
XLA Ops:
  0.6 1.4 copy.152
  2.0 1.3 copy.153
  3.8 1.6 copy.155
  5.4 10.5 %all-to-all-start = ((bf16[3,16,128,128]{3,2,0,1:T(8,128)(2,1)}), bf16[3,16,128,128]{3,2,0,1:T(8,128)(2,1)S(1)}, u32[]{:S(2)}, u32[]{:S(2)}) async-start(bf16[3,16,128,128]{3,2,0,1:T(8,128)(2,1)} %copy.155), calls=%async_computation | async-start | bytes 3145728 | tf_op jit(solution)/shard_map/all_to_all | solution.py:457
  16.5 22.2 %all-to-all-done = bf16[3,16,128,128]{3,2,0,1:T(8,128)(2,1)S(1)} async-done(((bf16[3,16,128,128]{3,2,0,1:T(8,128)(2,1)}), bf16[3,16,128,128]{3,2,0,1:T(8,128)(2,1)S(1)}, u32[]{:S(2)}, u32[]{:S(2)}) %all-to-all-start) | async-done | bytes 1572896 | tf_op jit(solution)/shard_map/all_to_all | solution.py:457
  39.9 0.7 fusion.64
  40.7 0.7 fusion.62
  41.4 0.7 fusion.63
  42.1 1.0 fusion.43.own_ref
  43.1 0.8 fusion.48.q_ref
  43.9 0.9 fusion.46
  44.8 7.5 %shard_map.127 = (bf16[1024,128]{1,0:T(8,128)(2,1)}, f32[1024,1]{1,0:T(8,128)}) custom-call(s32[10]{0:T(128)} %pad_add_fusion.params_ref, bf16[1024,128]{1,0:T(8,128)(2,1)} %fusion.48.q_ref, bf16[1024,128]{1,0:T(8,128)(2,1)} %get-tuple-element.135.k_ref, bf16[1024,128]{1,0:T(8,128)(2,1)} %get-tuple-element.134.v_ref, f32[1024,1]{1,0:T(8,128)} %fusion.43.own_ref), custom_call_target="tpu_custom_call" | custom-call | flops 536870912 | bytes 1056768 | tf_op jit(solution)/shard_map/pallas_call | solution.py:188
  52.3 1.7 %select_reduce_fusion = (f32[1024]{0:T(1024)S(1)}, f32[1024]{0:T(1024)S(1)}, f32[1024]{0:T(1024)S(1)}) fusion(pred[]{:T(512)} %bitcast.13, f32[1024,1]{1,0:T(8,128)} %get-tuple-element.38, f32[1024,2,1]{1,0,2:T(8,128)S(1)} %add.168), kind=kLoop, calls=%fused_computation.75 | loop fusion | flops 3072 | bytes 24577 | tf_op jit(solution)/shard_map/jit(_where)/select_n | solution.py:21
  55.6 0.9 add_convert_fusion.3
  56.5 4.5 %all-to-all-start.1 = ((bf16[16,128,128]{2,1,0:T(8,128)(2,1)}), bf16[16,128,128]{2,1,0:T(8,128)(2,1)S(1)}, u32[]{:S(2)}, u32[]{:S(2)}) async-start(bf16[16,128,128]{2,1,0:T(8,128)(2,1)} %bitcast.219), calls=%async_computation.1 | async-start | bytes 1048576 | tf_op jit(solution)/shard_map/all_to_all | solution.py:471
  63.6 0.6 fusion.65
  66.1 2.0 %copy.169 = bf16[1,128,2048]{1,2,0:T(8,128)(2,1)} copy(bf16[1,128,2048]{2,1,0:T(8,128)(2,1)} %param.11) | data formatting | bytes 1048576 | tf_op args[3]
  68.1 2.2 %copy.170 = f32[128,16,128]{2,0,1:T(8,128)} copy(bf16[128,16,128]{0,2,1:T(8,128)(2,1)} %bitcast.229) | data formatting | bytes 1572864 | tf_op jit(solution)/shard_map/convert_element_type | solution.py:413
  70.4 1.9 %all-to-all-done.1 = bf16[16,128,128]{2,1,0:T(8,128)(2,1)S(1)} async-done(((bf16[16,128,128]{2,1,0:T(8,128)(2,1)}), bf16[16,128,128]{2,1,0:T(8,128)(2,1)S(1)}, u32[]{:S(2)}, u32[]{:S(2)}) %all-to-all-start.1) | async-done | bytes 524320 | tf_op jit(solution)/shard_map/all_to_all | solution.py:471
  72.5 1.7 %fusion.29 = (f32[16,128]{1,0:T(8,128)S(1)}, f32[128]{0:T(128)S(1)}, f32[128]{0:T(128)S(1)}, f32[16,128]{1,0:T(8,128)S(1)}) fusion(bf16[16,128,128]{2,1,0:T(8,128)(2,1)S(1)} %all-to-all-done.1, f32[128,16,128]{2,0,1:T(8,128)} %copy.170, f32[128]{0:T(128)S(1)} %get-tuple-element.127, f32[128]{0:T(128)S(1)} %get-tuple-element.126, f32[16,128]{1,0:T(8,128)S(1)} %bitcast.243), kind=kLoop, calls=%fused_computation.46 | loop fusion | flops 2617088 | bytes 1599488 | tf_op jit(solution)/shard_map/reduce_sum | solution.py:423
  74.3 0.6 pad_maximum_fusion.6
  74.9 5.4 %all-to-all-start.4 = ((f32[16,2,128]{2,1,0:T(2,128)}), f32[16,2,128]{2,1,0:T(2,128)S(1)}, u32[]{:S(2)}, u32[]{:S(2)}) async-start(f32[16,2,128]{2,1,0:T(2,128)} %pad_maximum_fusion.6), calls=%async_computation.4 | async-start | bytes 32768 | tf_op jit(solution)/shard_map/all_to_all | solution.py:485
  80.3 2.8 %fusion.28 = (bf16[16,128,128]{2,1,0:T(8,128)(2,1)}, bf16[128,16,128]{2,0,1:T(8,128)(2,1)}) fusion(bf16[16,128,128]{2,1,0:T(8,128)(2,1)S(1)} %all-to-all-done.1, f32[128,16,128]{2,0,1:T(8,128)} %copy.170, f32[128]{0:T(128)S(1)} %broadcast_multiply_fusion, f32[128]{0:T(128)S(1)} %broadcast_multiply_fusion.1, f32[16,128]{1,0:T(8,128)S(1)} %bitcast.244, ...), kind=kLoop, calls=%fused_computation.45 | loop fusion | flops 3145728 | bytes 2639872 | tf_op jit(solution)/shard_map/convert_element_type | solution.py:422
  83.1 4.5 %all-to-all-done.4 = f32[16,2,128]{2,1,0:T(2,128)S(1)} async-done(((f32[16,2,128]{2,1,0:T(2,128)}), f32[16,2,128]{2,1,0:T(2,128)S(1)}, u32[]{:S(2)}, u32[]{:S(2)}) %all-to-all-start.4) | async-done | bytes 16416 | tf_op jit(solution)/shard_map/all_to_all | solution.py:485
  87.6 3.8 %all-to-all-start.2 = ((bf16[16,128,128]{2,1,0:T(8,128)(2,1)}), bf16[16,128,128]{2,1,0:T(8,128)(2,1)S(1)}, u32[]{:S(2)}, u32[]{:S(2)}) async-start(bf16[16,128,128]{2,1,0:T(8,128)(2,1)} %get-tuple-element.100), calls=%async_computation.2 | async-start | bytes 1048576 | tf_op jit(solution)/shard_map/all_to_all | solution.py:483
  91.4 6.2 %exponential_multiply_fusion = f32[1024,1024]{1,0:T(8,128)} fusion(bf16[1024,128]{1,0:T(8,128)(2,1)S(1)} %copy-done.3, bf16[1024,128]{1,0:T(8,128)(2,1)} %get-tuple-element.135.k_ref, f32[1024]{0:T(1024)S(1)} %get-tuple-element.89, s32[]{:T(128)} %bitcast.46, s32[]{:T(128)} %bitcast.44, s32[]{:T(128)} %bitcast.42, s32[1024]{0:T(1024)S(1)} %multiply_add_fusion, ...), kind=kOutput, calls=%fused_computation.4 | convolution fusion | flops 289406976 | bytes 4729868 | tf_op jit(solution)/shard_map/while/body/eval_jaxpr/qhd,khd->hqk/dot_general | solution.py:296
  97.6 5.0 %all-to-all-done.2 = bf16[16,128,128]{2,1,0:T(8,128)(2,1)S(1)} async-done(((bf16[16,128,128]{2,1,0:T(8,128)(2,1)}), bf16[16,128,128]{2,1,0:T(8,128)(2,1)S(1)}, u32[]{:S(2)}, u32[]{:S(2)}) %all-to-all-start.2) | async-done | bytes 524320 | tf_op jit(solution)/shard_map/all_to_all | solution.py:483
  102.6 0.6 broadcast_in_dim.118
  103.2 13.3 %all-to-all-start.5 = ((f32[32,2,128]{2,1,0:T(2,128)}), f32[32,2,128]{2,1,0:T(2,128)S(1)}, u32[]{:S(2)}, u32[]{:S(2)}) async-start(f32[32,2,128]{2,1,0:T(2,128)} %broadcast_in_dim.118), calls=%async_computation.5 | async-start | bytes 65536 | tf_op jit(solution)/shard_map/all_to_all | solution.py:488
  116.5 1.4 fusion.31
  117.9 1.3 reshape.516
  119.2 1.7 fusion.35
  120.8 0.7 fusion.61
  121.6 2.8 %select_bitcast_fusion.1 = (bf16[1024,1,1,128]{0,3,2,1:T(8,128)(2,1)S(1)}, bf16[1024,1,1,128]{0,3,2,1:T(8,128)(2,1)S(1)}) fusion(pred[]{:T(512)} %bitcast.13, f32[1024,1024]{1,0:T(8,128)} %exponential_multiply_fusion, bf16[1024,1,1,128]{3,1,0,2:T(2,128)(2,1)S(1)} %get-tuple-element.103, bf16[1024,1,1,128]{3,1,0,2:T(2,128)(2,1)S(1)} %get-tuple-element.102), kind=kOutput, calls=%fused_computation.88 | convolution fusion | flops 270008320 | bytes 5242881 | tf_op jit(solution)/shard_map/while/body/eval_jaxpr/hqk,qhd->khd/dot_general | solution.py:313
  125.0 0.7 multiply_convert_fusion
  125.8 1.3 select_bitcast_fusion.3
  127.0 1.6 select_bitcast_fusion.5
  128.7 1.1 convolution_convert_fusion
  131.4 1.1 pad_maximum_fusion.3
  133.0 1.8 %pad_maximum_fusion.4 = bf16[1024,2,1,128]{0,3,2,1:T(8,128)(2,1)} fusion(bf16[1024,1,1,128]{0,3,2,1:T(8,128)(2,1)} %get-tuple-element.113, bf16[1024,1,1,128]{0,3,2,1:T(8,128)(2,1)S(1)} %copy-done.4), kind=kLoop, calls=%fused_computation.67 | loop fusion | flops 262144 | bytes 1048576 | tf_op jit(solution)/shard_map/stack | solution.py:29
  134.8 1.3 copy.176
  136.6 1.3 pad_maximum_fusion.1
  137.9 5.2 %all-to-all-start.3 = ((bf16[3,16,128,128]{3,2,0,1:T(8,128)(2,1)}), bf16[3,16,128,128]{3,2,0,1:T(8,128)(2,1)S(1)}, u32[]{:S(2)}, u32[]{:S(2)}) async-start(bf16[3,16,128,128]{3,2,0,1:T(8,128)(2,1)} %pad_maximum_fusion.1), calls=%async_computation.3 | async-start | bytes 3145728 | tf_op jit(solution)/shard_map/all_to_all | solution.py:501
  143.4 1.0 copy.185
  145.0 21.0 %all-to-all-done.3 = bf16[3,16,128,128]{3,2,0,1:T(8,128)(2,1)S(1)} async-done(((bf16[3,16,128,128]{3,2,0,1:T(8,128)(2,1)}), bf16[3,16,128,128]{3,2,0,1:T(8,128)(2,1)S(1)}, u32[]{:S(2)}, u32[]{:S(2)}) %all-to-all-start.3) | async-done | bytes 1572896 | tf_op jit(solution)/shard_map/all_to_all | solution.py:501
  166.3 1.0 copy.188
  167.6 1.0 copy.187
  168.9 1.0 copy.186
  (68 shorter events, 9.6 us)
Async XLA Ops:
  0.6 2.7 %copy-start.7 = (bf16[1,128,2048]{2,1,0:T(8,128)(2,1)S(1)}, bf16[1,128,2048]{2,1,0:T(8,128)(2,1)}, u32[]{:S(2)}) copy-start(bf16[1,128,2048]{2,1,0:T(8,128)(2,1)} %param.10) | copy-start | bytes 1572868
  5.4 10.5 %copy-start.11 = (s32[4]{0:T(128)S(1)}, s32[4]{0:T(128)}, u32[]{:S(2)}) copy-start(s32[4]{0:T(128)} %param.14) | copy-start | bytes 52
  5.4 10.5 %copy-start.12 = (s32[4]{0:T(128)S(1)}, s32[4]{0:T(128)}, u32[]{:S(2)}) copy-start(s32[4]{0:T(128)} %param.15) | copy-start | bytes 52
  5.4 33.3 %all-to-all-start = ((bf16[3,16,128,128]{3,2,0,1:T(8,128)(2,1)}), bf16[3,16,128,128]{3,2,0,1:T(8,128)(2,1)S(1)}, u32[]{:S(2)}, u32[]{:S(2)}) async-start(bf16[3,16,128,128]{3,2,0,1:T(8,128)(2,1)} %copy.155), calls=%async_computation | async-start | bytes 3145728 | tf_op jit(solution)/shard_map/all_to_all | solution.py:457
  52.3 2.6 %copy-start.8 = (bf16[1024,128]{1,0:T(8,128)(2,1)S(1)}, bf16[1024,128]{1,0:T(8,128)(2,1)}, u32[]{:S(2)}) copy-start(bf16[1024,128]{1,0:T(8,128)(2,1)} %get-tuple-element.39) | copy-start | bytes 786436
  56.5 16.0 %copy-start.9 = (f32[2048]{0:T(1024)S(1)}, f32[2048]{0:T(1024)}, u32[]{:S(2)}) copy-start(f32[2048]{0:T(1024)} %param.12) | copy-start | bytes 24580
  56.5 15.8 %all-to-all-start.1 = ((bf16[16,128,128]{2,1,0:T(8,128)(2,1)}), bf16[16,128,128]{2,1,0:T(8,128)(2,1)S(1)}, u32[]{:S(2)}, u32[]{:S(2)}) async-start(bf16[16,128,128]{2,1,0:T(8,128)(2,1)} %bitcast.219), calls=%async_computation.1 | async-start | bytes 1048576 | tf_op jit(solution)/shard_map/all_to_all | solution.py:471
  68.1 12.2 %copy-start.10 = (f32[2048]{0:T(1024)S(1)}, f32[2048]{0:T(1024)}, u32[]{:S(2)}) copy-start(f32[2048]{0:T(1024)} %param.13) | copy-start | bytes 24580
  74.3 17.1 %copy-start.3 = (bf16[1024,128]{1,0:T(8,128)(2,1)S(1)}, bf16[1024,128]{1,0:T(8,128)(2,1)}, u32[]{:S(2)}) copy-start(bf16[1024,128]{1,0:T(8,128)(2,1)} %fusion.48.q_ref) | copy-start | bytes 786436
  74.9 12.7 %all-to-all-start.4 = ((f32[16,2,128]{2,1,0:T(2,128)}), f32[16,2,128]{2,1,0:T(2,128)S(1)}, u32[]{:S(2)}, u32[]{:S(2)}) async-start(f32[16,2,128]{2,1,0:T(2,128)} %pad_maximum_fusion.6), calls=%async_computation.4 | async-start | bytes 32768 | tf_op jit(solution)/shard_map/all_to_all | solution.py:485
  87.6 15.0 %all-to-all-start.2 = ((bf16[16,128,128]{2,1,0:T(8,128)(2,1)}), bf16[16,128,128]{2,1,0:T(8,128)(2,1)S(1)}, u32[]{:S(2)}, u32[]{:S(2)}) async-start(bf16[16,128,128]{2,1,0:T(8,128)(2,1)} %get-tuple-element.100), calls=%async_computation.2 | async-start | bytes 1048576 | tf_op jit(solution)/shard_map/all_to_all | solution.py:483
  103.2 34.7 %all-to-all-start.5 = ((f32[32,2,128]{2,1,0:T(2,128)}), f32[32,2,128]{2,1,0:T(2,128)S(1)}, u32[]{:S(2)}, u32[]{:S(2)}) async-start(f32[32,2,128]{2,1,0:T(2,128)} %broadcast_in_dim.118), calls=%async_computation.5 | async-start | bytes 65536 | tf_op jit(solution)/shard_map/all_to_all | solution.py:488
  121.5 3.5 %copy-start = (f32[1024,1024]{1,0:T(8,128)S(1)}, f32[1024,1024]{1,0:T(8,128)}, u32[]{:S(2)}) copy-start(f32[1024,1024]{1,0:T(8,128)} %exponential_multiply_fusion) | copy-start | bytes 12582916
  121.6 3.5 %copy-start.6 = (bf16[1024,128]{1,0:T(8,128)(2,1)S(1)}, bf16[1024,128]{1,0:T(8,128)(2,1)}, u32[]{:S(2)}) copy-start(bf16[1024,128]{1,0:T(8,128)(2,1)} %get-tuple-element.134.v_ref) | copy-start | bytes 786436
  125.8 1.3 copy-start.5
  130.9 2.1 %copy-start.4 = (bf16[1024,1,1,128]{0,3,2,1:T(8,128)(2,1)S(1)}, bf16[1024,1,1,128]{0,3,2,1:T(8,128)(2,1)}, u32[]{:S(2)}) copy-start(bf16[1024,1,1,128]{0,3,2,1:T(8,128)(2,1)} %get-tuple-element.112) | copy-start | bytes 786436
  131.4 4.7 %copy-start.1 = (bf16[16,128,128]{1,2,0:T(8,128)(2,1)S(1)}, bf16[16,128,128]{1,2,0:T(8,128)(2,1)}, u32[]{:S(2)}) copy-start(bf16[16,128,128]{1,2,0:T(8,128)(2,1)} %convolution_convert_fusion) | copy-start | bytes 1572868
  137.9 5.2 %copy-start.2 = (bf16[128,16,128]{2,0,1:T(8,128)(2,1)S(1)}, bf16[128,16,128]{2,0,1:T(8,128)(2,1)}, u32[]{:S(2)}) copy-start(bf16[128,16,128]{2,0,1:T(8,128)(2,1)} %get-tuple-element.101) | copy-start | bytes 1572868
  137.9 28.0 %all-to-all-start.3 = ((bf16[3,16,128,128]{3,2,0,1:T(8,128)(2,1)}), bf16[3,16,128,128]{3,2,0,1:T(8,128)(2,1)S(1)}, u32[]{:S(2)}, u32[]{:S(2)}) async-start(bf16[3,16,128,128]{3,2,0,1:T(8,128)(2,1)} %pad_maximum_fusion.1), calls=%async_computation.3 | async-start | bytes 3145728 | tf_op jit(solution)/shard_map/all_to_all | solution.py:501

commit v5 on v4

--- a/solution.py
+++ b/solution.py
@@ -211,6 +211,86 @@
     )(params, q, k, v, own)
 
 
+def dilated_backward_kernel(
+    params_ref, q_ref, k_ref, v_ref, g_ref, lse_ref, delta_ref, dq_ref, dk_ref, dv_ref, dk_acc, dv_acc
+):
+    rows, head_size = q_ref.shape
+    keys = k_ref.shape[0]
+    step = pl.program_id(0)
+    scaling = 1.0 / math.sqrt(head_size)
+
+    @pl.when(step == 0)
+    def _():
+        dk_acc[...] = jnp.zeros_like(dk_acc)
+        dv_acc[...] = jnp.zeros_like(dv_acc)
+
+    counted = dilated_mask(params_ref, rows, keys, step * rows)
+    q_block = q_ref[...]
+    g_block = g_ref[...]
+    scores = (
+        lax.dot_general(
+            q_block, k_ref[...], (((1,), (1,)), ((), ())), preferred_element_type=jnp.float32
+        )
+        * scaling
+    )
+    masked = jnp.where(counted > 0, scores, -1e30)
+    prob_full = counted * jnp.exp(masked - lse_ref[...])
+    grad_prob = lax.dot_general(
+        g_block, v_ref[...], (((1,), (1,)), ((), ())), preferred_element_type=jnp.float32
+    )
+    grad_score = (prob_full * (grad_prob - delta_ref[...])).astype(jnp.bfloat16)
+    dq_ref[...] = (
+        jnp.dot(grad_score, k_ref[...], preferred_element_type=jnp.float32) * scaling
+    ).astype(dq_ref.dtype)
+    dk_acc[...] += lax.dot_general(
+        grad_score, q_block, (((0,), (0,)), ((), ())), preferred_element_type=jnp.float32
+    )
+    dv_acc[...] += lax.dot_general(
+        prob_full.astype(jnp.bfloat16),
+        g_block,
+        (((0,), (0,)), ((), ())),
+        preferred_element_type=jnp.float32,
+    )
+
+    @pl.when(step == pl.num_programs(0) - 1)
+    def _():
+        dk_ref[...] = (dk_acc[...] * scaling).astype(dk_ref.dtype)
+        dv_ref[...] = dv_acc[...].astype(dv_ref.dtype)
+
+
+def dilated_backward_call(params, q, k, v, g, lse, delta, row_block=256):
+    rows, head_size = q.shape
+    keys = k.shape[0]
+    row_spec = pl.BlockSpec((row_block, head_size), lambda i: (i, 0))
+    full_spec = pl.BlockSpec((keys, head_size), lambda i: (0, 0))
+    column_spec = pl.BlockSpec((row_block, 1), lambda i: (i, 0))
+    return pl.pallas_call(
+        dilated_backward_kernel,
+        grid=(rows // row_block,),
+        in_specs=[
+            pl.BlockSpec(memory_space=pltpu.SMEM),
+            row_spec,
+            full_spec,
+            full_spec,
+            row_spec,
+            column_spec,
+            column_spec,
+        ],
+        out_specs=[row_spec, full_spec, full_spec],
+        out_shape=[jax.ShapeDtypeStruct((rows, head_size), jnp.bfloat16)] * 3,
+        scratch_shapes=[
+            pltpu.VMEM((keys, head_size), jnp.float32),
+            pltpu.VMEM((keys, head_size), jnp.float32),
+        ],
+        compiler_params=pltpu.CompilerParams(dimension_semantics=("arbitrary",)),
+        cost_estimate=pl.CostEstimate(
+            flops=10 * rows * keys * head_size,
+            transcendentals=rows * keys,
+            bytes_accessed=2 * 8 * rows * head_size + 8 * rows,
+        ),
+    )(params, q, k, v, g, lse, delta)
+
+
 def sparse_attention_forward(
     query_row_set,
     key_row_set,
@@ -374,17 +454,30 @@
     local_parts = local_backward(
         query_row_set, key_row_set, value_row_set, grad_attended, log_norm, delta_row
     )
-    packed_parts = dilated_backward(
-        pick_rows(query_row_set, parity),
-        pick_rows(key_row_set, parity),
-        pick_rows(value_row_set, parity),
-        pick_rows(grad_attended, parity),
-        pick_rows(log_norm, parity),
-        pick_rows(delta_row, parity),
-        head_indices,
-        segment_blocks,
-        dilation_rates,
-    )
+    if query_row_set.shape[1] == 1:
+        params = mask_params(head_indices[0], segment_blocks, dilation_rates)
+        packed_parts = dilated_backward_call(
+            params,
+            pick_rows(query_row_set, parity)[:, 0],
+            pick_rows(key_row_set, parity)[:, 0],
+            pick_rows(value_row_set, parity)[:, 0],
+            pick_rows(grad_attended, parity)[:, 0],
+            pick_rows(log_norm, parity),
+            pick_rows(delta_row, parity),
+        )
+        packed_parts = tuple(part[:, None] for part in packed_parts)
+    else:
+        packed_parts = dilated_backward(
+            pick_rows(query_row_set, parity),
+            pick_rows(key_row_set, parity),
+            pick_rows(value_row_set, parity),
+            pick_rows(grad_attended, parity),
+            pick_rows(log_norm, parity),
+            pick_rows(delta_row, parity),
+            head_indices,
+            segment_blocks,
+            dilation_rates,
+        )
     return tuple(
         (
             add_parts(first_branch, second, parity)

time: 171 us -> 177 us (1.035)
  matrix products: 15.8 us -> 2.3 us
  waiting for transfers between devices: 54.5 us -> 65.9 us
  Pallas kernels: 7.48 us -> 15.8 us
  local copies, waits for them, and re-layouts: 24.5 us -> 29.2 us
  between operations: 4.94 us -> 1.04 us
    dot_general x5 -> x0, matrix products: 12.7 us -> none  [the longest x1 6.22 us: step(): jnp.einsum('qhd,khd->hqk', q_block, key_row_set, preferred_element_type=j...]
    pallas_call x0 -> x1, Pallas kernels: none -> 8.35 us  [dilated_backward_call(): pl.pallas_call(dilated_backward_kernel, grid=(rows // row_block,), in_spe...]
    all_to_all x1, waiting for transfers between devices: 5.01 us -> 11.2 us  [shards(): grad_attended = to_rows(lax.all_to_all(grad_hm, 'ctx', 0, 0, tiled=True))]
    all_to_all x1, waiting for transfers between devices: 1.89 us -> 6.97 us  [shards(): lax.all_to_all(attended.reshape(ctx_count, tokens_here, width_here), 'ctx...]
    slice x4, local copies, waits for them, and re-layouts: 2.92 us -> 6.8 us  [pick_rows(): return jnp.where(cond, pairs[:, 0], pairs[:, 1])]
    unnamed x37 -> x47, local copies, waits for them, and re-layouts: 10.5 us -> 10.4 us
  transfers between devices with their start and end apart: 6 -> 6, of which waited for: 5 -> 5; matrix products, arithmetic and copies ran while one was open for 22% -> 13% of each run, Pallas kernels for 0% -> 5%
where the time goes in v5:
time: 177 us; the launch traced here: 176 us
  waiting for transfers between devices  65.9 us (37%)
  starting transfers between devices  41.8 us (24%)
  local copies, waits for them, and re-layouts  29.2 us (16%)
  other arithmetic  20.1 us (11%)
  Pallas kernels  15.8 us (9%)
  matrix products  2.3 us (1%)
    all_to_all x1, waiting for transfers between devices, shards(): lax.all_to_all(stacked_in, 'ctx', split_axis=1, concat_axis=1, tiled=True)  22.2 us
    all_to_all x1, waiting for transfers between devices, shards(): lax.all_to_all(jnp.stack([part.reshape(ctx_count, tokens_here, width_here...  21 us
    all_to_all x1, starting transfers between devices, shards(): both = jnp.sum(lax.all_to_all(both, 'dp', 0, 0, tiled=True), axis=0)  13.4 us
    all_to_all x1, waiting for transfers between devices, shards(): grad_attended = to_rows(lax.all_to_all(grad_hm, 'ctx', 0, 0, tiled=True))  11.2 us
    all_to_all x1, starting transfers between devices, shards(): lax.all_to_all(stacked_in, 'ctx', split_axis=1, concat_axis=1, tiled=True)  10.5 us
    unnamed x47, local copies, waits for them, and re-layouts  10.4 us
    pallas_call x1, Pallas kernels, dilated_backward_call(): pl.pallas_call(dilated_backward_kernel, grid=(rows // row_block,), in_spe...  8.35 us
    pallas_call x1, Pallas kernels, dilated_forward_call(): pl.pallas_call(dilated_forward_kernel, grid=grid, in_specs=[pl.BlockSpec(...  7.47 us
  transfers between devices with their start and end apart: 6, of which 5 were waited for; matrix products, arithmetic and copies ran while one was open for 13% of the time, Pallas kernels for 5%

profile of v5, /device:TPU:1, one launch (start us, length us, event | category | flops | bytes accessed | tf_op | source)
XLA Modules:
  0.0 176.1 jit_solution(12019025270781922532)
XLA Ops:
  0.6 1.4 copy.154
  2.0 1.3 copy.153
  3.8 1.6 copy.155
  5.4 10.5 %all-to-all-start = ((bf16[3,16,128,128]{3,2,0,1:T(8,128)(2,1)}), bf16[3,16,128,128]{3,2,0,1:T(8,128)(2,1)S(1)}, u32[]{:S(2)}, u32[]{:S(2)}) async-start(bf16[3,16,128,128]{3,2,0,1:T(8,128)(2,1)} %copy.155), calls=%async_computation | async-start | bytes 3145728 | tf_op jit(solution)/shard_map/all_to_all | solution.py:550
  15.9 0.6 pad_add_fusion.params_ref
  16.5 22.2 %all-to-all-done = bf16[3,16,128,128]{3,2,0,1:T(8,128)(2,1)S(1)} async-done(((bf16[3,16,128,128]{3,2,0,1:T(8,128)(2,1)}), bf16[3,16,128,128]{3,2,0,1:T(8,128)(2,1)S(1)}, u32[]{:S(2)}, u32[]{:S(2)}) %all-to-all-start) | async-done | bytes 1572896 | tf_op jit(solution)/shard_map/all_to_all | solution.py:550
  38.8 1.7 fusion.50
  40.5 1.7 fusion.48
  42.2 1.7 fusion.49
  45.1 1.0 fusion.29.own_ref
  46.3 0.8 fusion.34.q_ref
  47.1 2.0 %fusion.32 = (bf16[1024,128]{1,0:T(8,128)(2,1)}, bf16[1024,128]{1,0:T(8,128)(2,1)}) fusion(bf16[1024,1,1,128]{3,1,0,2:T(2,128)(2,1)S(1)} %copy-done.8, bf16[1024,1,1,128]{3,1,0,2:T(2,128)(2,1)S(1)} %copy-done.7, pred[]{:T(512)} %bitcast.13, bf16[1024,1,1,128]{3,1,0,2:T(2,128)(2,1)} %get-tuple-element.68, bf16[1024,1,1,128]{3,1,0,2:T(2,128)(2,1)S(1)} %copy-done.9), kind=kLoop, calls=%fused_computation.61 | loop fusion | flops 262144 | bytes 1572865 | tf_op jit(solution)/shard_map/jit(_where)/select_n | solution.py:21
  49.1 7.5 %shard_map.127 = (bf16[1024,128]{1,0:T(8,128)(2,1)}, f32[1024,1]{1,0:T(8,128)}) custom-call(s32[10]{0:T(128)} %pad_add_fusion.params_ref, bf16[1024,128]{1,0:T(8,128)(2,1)} %fusion.34.q_ref, bf16[1024,128]{1,0:T(8,128)(2,1)} %get-tuple-element.88.k_ref, bf16[1024,128]{1,0:T(8,128)(2,1)} %get-tuple-element.87.v_ref, f32[1024,1]{1,0:T(8,128)} %fusion.29.own_ref), custom_call_target="tpu_custom_call" | custom-call | flops 536870912 | bytes 1056768 | tf_op jit(solution)/shard_map/pallas_call | solution.py:188
  56.6 1.0 select_bitcast_fusion.7
  57.7 1.3 copy.167
  59.0 1.0 fusion.36
  60.0 1.0 copy.165
  61.1 1.3 sub.69
  62.8 0.9 add_convert_fusion.3
  63.7 4.4 %all-to-all-start.1 = ((bf16[16,128,128]{2,1,0:T(8,128)(2,1)}), bf16[16,128,128]{2,1,0:T(8,128)(2,1)S(1)}, u32[]{:S(2)}, u32[]{:S(2)}) async-start(bf16[16,128,128]{2,1,0:T(8,128)(2,1)} %bitcast.181), calls=%async_computation.1 | async-start | bytes 1048576 | tf_op jit(solution)/shard_map/all_to_all | solution.py:564
  68.1 2.0 %copy.169 = bf16[1,128,2048]{1,2,0:T(8,128)(2,1)} copy(bf16[1,128,2048]{2,1,0:T(8,128)(2,1)} %param.11) | data formatting | bytes 1048576 | tf_op args[3]
  70.1 2.2 %copy.170 = f32[128,16,128]{2,0,1:T(8,128)} copy(bf16[128,16,128]{0,2,1:T(8,128)(2,1)} %bitcast.191) | data formatting | bytes 1572864 | tf_op jit(solution)/shard_map/convert_element_type | solution.py:506
  72.4 7.0 %all-to-all-done.1 = bf16[16,128,128]{2,1,0:T(8,128)(2,1)S(1)} async-done(((bf16[16,128,128]{2,1,0:T(8,128)(2,1)}), bf16[16,128,128]{2,1,0:T(8,128)(2,1)S(1)}, u32[]{:S(2)}, u32[]{:S(2)}) %all-to-all-start.1) | async-done | bytes 524320 | tf_op jit(solution)/shard_map/all_to_all | solution.py:564
  79.6 1.7 fusion.15
  81.3 0.6 pad_maximum_fusion.6
  81.9 4.5 %all-to-all-start.4 = ((f32[16,2,128]{2,1,0:T(2,128)}), f32[16,2,128]{2,1,0:T(2,128)S(1)}, u32[]{:S(2)}, u32[]{:S(2)}) async-start(f32[16,2,128]{2,1,0:T(2,128)} %pad_maximum_fusion.6), calls=%async_computation.4 | async-start | bytes 32768 | tf_op jit(solution)/shard_map/all_to_all | solution.py:578
  86.5 2.8 %fusion.14 = (bf16[16,128,128]{2,1,0:T(8,128)(2,1)}, bf16[128,16,128]{2,0,1:T(8,128)(2,1)}) fusion(bf16[16,128,128]{2,1,0:T(8,128)(2,1)S(1)} %all-to-all-done.1, f32[128,16,128]{2,0,1:T(8,128)} %copy.170, f32[128]{0:T(128)S(1)} %broadcast_multiply_fusion, f32[128]{0:T(128)S(1)} %broadcast_multiply_fusion.1, f32[16,128]{1,0:T(8,128)S(1)} %bitcast.206, ...), kind=kLoop, calls=%fused_computation.25 | loop fusion | flops 3145728 | bytes 2639872 | tf_op jit(solution)/shard_map/convert_element_type | solution.py:515
  89.3 4.5 %all-to-all-done.4 = f32[16,2,128]{2,1,0:T(2,128)S(1)} async-done(((f32[16,2,128]{2,1,0:T(2,128)}), f32[16,2,128]{2,1,0:T(2,128)S(1)}, u32[]{:S(2)}, u32[]{:S(2)}) %all-to-all-start.4) | async-done | bytes 16416 | tf_op jit(solution)/shard_map/all_to_all | solution.py:578
  93.8 3.8 %all-to-all-start.2 = ((bf16[16,128,128]{2,1,0:T(8,128)(2,1)}), bf16[16,128,128]{2,1,0:T(8,128)(2,1)S(1)}, u32[]{:S(2)}, u32[]{:S(2)}) async-start(bf16[16,128,128]{2,1,0:T(8,128)(2,1)} %get-tuple-element.61), calls=%async_computation.2 | async-start | bytes 1048576 | tf_op jit(solution)/shard_map/all_to_all | solution.py:576
  97.6 11.2 %all-to-all-done.2 = bf16[16,128,128]{2,1,0:T(8,128)(2,1)S(1)} async-done(((bf16[16,128,128]{2,1,0:T(8,128)(2,1)}), bf16[16,128,128]{2,1,0:T(8,128)(2,1)S(1)}, u32[]{:S(2)}, u32[]{:S(2)}) %all-to-all-start.2) | async-done | bytes 524320 | tf_op jit(solution)/shard_map/all_to_all | solution.py:576
  108.8 0.6 broadcast_in_dim.81
  109.5 13.4 %all-to-all-start.5 = ((f32[32,2,128]{2,1,0:T(2,128)}), f32[32,2,128]{2,1,0:T(2,128)S(1)}, u32[]{:S(2)}, u32[]{:S(2)}) async-start(f32[32,2,128]{2,1,0:T(2,128)} %broadcast_in_dim.81), calls=%async_computation.5 | async-start | bytes 65536 | tf_op jit(solution)/shard_map/all_to_all | solution.py:581
  122.9 1.7 fusion.47
  125.0 1.3 reshape.337
  126.3 2.3 %fusion.21.delta_ref = f32[1024,1]{1,0:T(8,128)} fusion(f32[1024,2,1]{1,0,2:T(8,128)} %reshape.337, pred[]{:T(512)} %bitcast.13), kind=kLoop, calls=%fused_computation.42 | loop fusion | flops 1024 | bytes 12289 | tf_op jit(solution)/shard_map/jit(_where)/select_n | solution.py:21
  128.6 0.8 fusion.31.g_ref
  129.3 8.4 %shard_map.128 = (bf16[1024,128]{1,0:T(8,128)(2,1)}, bf16[1024,128]{1,0:T(8,128)(2,1)}, bf16[1024,128]{1,0:T(8,128)(2,1)}) custom-call(s32[10]{0:T(128)} %pad_add_fusion.params_ref, bf16[1024,128]{1,0:T(8,128)(2,1)} %fusion.34.q_ref, bf16[1024,128]{1,0:T(8,128)(2,1)} %get-tuple-element.88.k_ref, bf16[1024,128]{1,0:T(8,128)(2,1)} %get-tuple-element.87.v_ref, ...), custom_call_target="tpu_custom_call" | custom-call | flops 1342177280 | bytes 2105344 | tf_op jit(solution)/shard_map/pallas_call | solution.py:267
  137.7 1.0 select_bitcast_fusion.1
  138.7 0.5 copy.177
  139.8 0.5 copy.176
  141.4 0.5 copy.175
  142.7 1.3 pad_maximum_fusion.1
  144.1 5.2 %all-to-all-start.3 = ((bf16[3,16,128,128]{3,2,0,1:T(8,128)(2,1)}), bf16[3,16,128,128]{3,2,0,1:T(8,128)(2,1)S(1)}, u32[]{:S(2)}, u32[]{:S(2)}) async-start(bf16[3,16,128,128]{3,2,0,1:T(8,128)(2,1)} %pad_maximum_fusion.1), calls=%async_computation.3 | async-start | bytes 3145728 | tf_op jit(solution)/shard_map/all_to_all | solution.py:594
  149.6 1.0 copy.185
  151.1 21.0 %all-to-all-done.3 = bf16[3,16,128,128]{3,2,0,1:T(8,128)(2,1)S(1)} async-done(((bf16[3,16,128,128]{3,2,0,1:T(8,128)(2,1)}), bf16[3,16,128,128]{3,2,0,1:T(8,128)(2,1)S(1)}, u32[]{:S(2)}, u32[]{:S(2)}) %all-to-all-start.3) | async-done | bytes 1572896 | tf_op jit(solution)/shard_map/all_to_all | solution.py:594
  172.5 1.0 copy.186
  173.8 1.0 copy.187
  175.1 1.0 copy.188
  (73 shorter events, 7.1 us)
Async XLA Ops:
  0.6 2.7 %copy-start.11 = (bf16[1,128,2048]{2,1,0:T(8,128)(2,1)S(1)}, bf16[1,128,2048]{2,1,0:T(8,128)(2,1)}, u32[]{:S(2)}) copy-start(bf16[1,128,2048]{2,1,0:T(8,128)(2,1)} %param.8) | copy-start | bytes 1572868
  5.4 10.5 %copy-start.16 = (s32[4]{0:T(128)S(1)}, s32[4]{0:T(128)}, u32[]{:S(2)}) copy-start(s32[4]{0:T(128)} %param.15) | copy-start | bytes 52
  5.4 10.5 %copy-start.17 = (s32[4]{0:T(128)S(1)}, s32[4]{0:T(128)}, u32[]{:S(2)}) copy-start(s32[4]{0:T(128)} %param.14) | copy-start | bytes 52
  5.4 33.3 %all-to-all-start = ((bf16[3,16,128,128]{3,2,0,1:T(8,128)(2,1)}), bf16[3,16,128,128]{3,2,0,1:T(8,128)(2,1)S(1)}, u32[]{:S(2)}, u32[]{:S(2)}) async-start(bf16[3,16,128,128]{3,2,0,1:T(8,128)(2,1)} %copy.155), calls=%async_computation | async-start | bytes 3145728 | tf_op jit(solution)/shard_map/all_to_all | solution.py:550
  45.0 1.1 copy-start.2
  45.1 1.3 copy-start.3
  45.1 2.1 %copy-start.7 = (bf16[1024,1,1,128]{3,1,0,2:T(2,128)(2,1)S(1)}, bf16[1024,1,1,128]{3,1,0,2:T(2,128)(2,1)}, u32[]{:S(2)}) copy-start(bf16[1024,1,1,128]{3,1,0,2:T(2,128)(2,1)} %get-tuple-element.65) | copy-start | bytes 786436
  45.1 2.0 %copy-start.8 = (bf16[1024,1,1,128]{3,1,0,2:T(2,128)(2,1)S(1)}, bf16[1024,1,1,128]{3,1,0,2:T(2,128)(2,1)}, u32[]{:S(2)}) copy-start(bf16[1024,1,1,128]{3,1,0,2:T(2,128)(2,1)} %get-tuple-element.66) | copy-start | bytes 786436
  45.1 2.0 %copy-start.9 = (bf16[1024,1,1,128]{3,1,0,2:T(2,128)(2,1)S(1)}, bf16[1024,1,1,128]{3,1,0,2:T(2,128)(2,1)}, u32[]{:S(2)}) copy-start(bf16[1024,1,1,128]{3,1,0,2:T(2,128)(2,1)} %get-tuple-element.67) | copy-start | bytes 786436
  56.6 2.5 %copy-start.10 = (f32[1024,1]{1,0:T(8,128)S(1)}, f32[1024,1]{1,0:T(8,128)}, u32[]{:S(2)}) copy-start(f32[1024,1]{1,0:T(8,128)} %get-tuple-element.11) | copy-start | bytes 12292
  60.0 2.7 %copy-start.1 = (bf16[1024,2,1,128]{3,1,0,2:T(2,128)(2,1)S(1)}, bf16[1024,2,1,128]{3,1,0,2:T(2,128)(2,1)}, u32[]{:S(2)}) copy-start(bf16[1024,2,1,128]{3,1,0,2:T(2,128)(2,1)} %copy.167) | copy-start | bytes 1572868
  63.7 15.6 %all-to-all-start.1 = ((bf16[16,128,128]{2,1,0:T(8,128)(2,1)}), bf16[16,128,128]{2,1,0:T(8,128)(2,1)S(1)}, u32[]{:S(2)}, u32[]{:S(2)}) async-start(bf16[16,128,128]{2,1,0:T(8,128)(2,1)} %bitcast.181), calls=%async_computation.1 | async-start | bytes 1048576 | tf_op jit(solution)/shard_map/all_to_all | solution.py:564
  68.1 11.5 %copy-start.14 = (f32[2048]{0:T(1024)S(1)}, f32[2048]{0:T(1024)}, u32[]{:S(2)}) copy-start(f32[2048]{0:T(1024)} %param.12) | copy-start | bytes 24580
  70.1 16.3 %copy-start.15 = (f32[2048]{0:T(1024)S(1)}, f32[2048]{0:T(1024)}, u32[]{:S(2)}) copy-start(f32[2048]{0:T(1024)} %param.13) | copy-start | bytes 24580
  81.9 11.9 %all-to-all-start.4 = ((f32[16,2,128]{2,1,0:T(2,128)}), f32[16,2,128]{2,1,0:T(2,128)S(1)}, u32[]{:S(2)}, u32[]{:S(2)}) async-start(f32[16,2,128]{2,1,0:T(2,128)} %pad_maximum_fusion.6), calls=%async_computation.4 | async-start | bytes 32768 | tf_op jit(solution)/shard_map/all_to_all | solution.py:578
  93.8 15.0 %all-to-all-start.2 = ((bf16[16,128,128]{2,1,0:T(8,128)(2,1)}), bf16[16,128,128]{2,1,0:T(8,128)(2,1)S(1)}, u32[]{:S(2)}, u32[]{:S(2)}) async-start(bf16[16,128,128]{2,1,0:T(8,128)(2,1)} %get-tuple-element.61), calls=%async_computation.2 | async-start | bytes 1048576 | tf_op jit(solution)/shard_map/all_to_all | solution.py:576
  109.5 34.6 %all-to-all-start.5 = ((f32[32,2,128]{2,1,0:T(2,128)}), f32[32,2,128]{2,1,0:T(2,128)S(1)}, u32[]{:S(2)}, u32[]{:S(2)}) async-start(f32[32,2,128]{2,1,0:T(2,128)} %broadcast_in_dim.81), calls=%async_computation.5 | async-start | bytes 65536 | tf_op jit(solution)/shard_map/all_to_all | solution.py:581
  122.9 1.7 copy-start
  126.3 2.3 %copy-start.4 = (bf16[1024,1,1,128]{3,1,0,2:T(2,128)(2,1)S(1)}, bf16[1024,1,1,128]{3,1,0,2:T(2,128)(2,1)}, u32[]{:S(2)}) copy-start(bf16[1024,1,1,128]{3,1,0,2:T(2,128)(2,1)} %get-tuple-element.63) | copy-start | bytes 786436
  126.3 2.3 %copy-start.5 = (bf16[1024,1,1,128]{3,1,0,2:T(2,128)(2,1)S(1)}, bf16[1024,1,1,128]{3,1,0,2:T(2,128)(2,1)}, u32[]{:S(2)}) copy-start(bf16[1024,1,1,128]{3,1,0,2:T(2,128)(2,1)} %get-tuple-element.64) | copy-start | bytes 786436
  138.7 1.0 copy-start.13
  140.3 1.0 copy-start.12
  144.1 5.2 %copy-start.6 = (bf16[128,16,128]{2,0,1:T(8,128)(2,1)S(1)}, bf16[128,16,128]{2,0,1:T(8,128)(2,1)}, u32[]{:S(2)}) copy-start(bf16[128,16,128]{2,0,1:T(8,128)(2,1)} %get-tuple-element.62) | copy-start | bytes 1572868
  144.1 28.0 %all-to-all-start.3 = ((bf16[3,16,128,128]{3,2,0,1:T(8,128)(2,1)}), bf16[3,16,128,128]{3,2,0,1:T(8,128)(2,1)S(1)}, u32[]{:S(2)}, u32[]{:S(2)}) async-start(bf16[3,16,128,128]{3,2,0,1:T(8,128)(2,1)} %pad_maximum_fusion.1), calls=%async_computation.3 | async-start | bytes 3145728 | tf_op jit(solution)/shard_map/all_to_all | solution.py:594

commit v6 on v4

--- a/solution.py
+++ b/solution.py
@@ -480,9 +480,11 @@
         bias_hm,
     )
     normed = token_major(normed_hm)
-    grad_attended = to_rows(lax.all_to_all(grad_hm, "ctx", 0, 0, tiled=True))
     both = jnp.stack([gain_part, bias_part], axis=1)
-    both = jnp.sum(lax.all_to_all(both, "ctx", 0, 0, tiled=True), axis=0)
+    carried = jnp.concatenate([grad_hm.astype(jnp.float32), both], axis=1)
+    carried = lax.all_to_all(carried, "ctx", 0, 0, tiled=True)
+    grad_attended = to_rows(carried[:, :tokens_here].astype(jnp.bfloat16))
+    both = jnp.sum(carried[:, tokens_here:], axis=0)
     dp_count = lax.axis_size("dp")
     both = jnp.broadcast_to(both[None], (dp_count,) + both.shape)
     both = jnp.sum(lax.all_to_all(both, "dp", 0, 0, tiled=True), axis=0)

time: 171 us -> 175 us (1.023)
  waiting for transfers between devices: 54.5 us -> 59.1 us
  starting transfers between devices: 42.5 us -> 39.5 us
    all_to_all x1, waiting for transfers between devices: 1.89 us -> 6.33 us  [shards(): lax.all_to_all(attended.reshape(ctx_count, tokens_here, width_here), 'ctx...]
    all_to_all x2 -> x1, starting transfers between devices: 9.16 us -> 5.51 us  [shards(): carried = lax.all_to_all(carried, 'ctx', 0, 0, tiled=True)]
    all_to_all x2 -> x1, waiting for transfers between devices: 9.48 us -> 8.27 us  [shards(): carried = lax.all_to_all(carried, 'ctx', 0, 0, tiled=True)]
    unnamed x37 -> x43, local copies, waits for them, and re-layouts: 10.5 us -> 10.4 us
  transfers between devices with their start and end apart: 6 -> 5, of which waited for: 5 -> 5; matrix products, arithmetic and copies ran while one was open for 22% -> 14% of each run, Pallas kernels for 0% -> 0%
where the time goes in v6:
time: 175 us; the launch traced here: 174 us
  waiting for transfers between devices  59.1 us (34%)
  starting transfers between devices  39.5 us (23%)
  local copies, waits for them, and re-layouts  25.7 us (15%)
  other arithmetic  19.9 us (11%)
  matrix products  17.2 us (10%)
  Pallas kernels  7.47 us (4%)
  between operations  4.94 us (3%)
    all_to_all x1, waiting for transfers between devices, shards(): lax.all_to_all(stacked_in, 'ctx', split_axis=1, concat_axis=1, tiled=True)  22.2 us
    all_to_all x1, waiting for transfers between devices, shards(): lax.all_to_all(jnp.stack([part.reshape(ctx_count, tokens_here, width_here...  21 us
    all_to_all x1, starting transfers between devices, shards(): both = jnp.sum(lax.all_to_all(both, 'dp', 0, 0, tiled=True), axis=0)  13.3 us
    all_to_all x1, starting transfers between devices, shards(): lax.all_to_all(stacked_in, 'ctx', split_axis=1, concat_axis=1, tiled=True)  10.5 us
    unnamed x43, local copies, waits for them, and re-layouts  10.4 us
    all_to_all x1, waiting for transfers between devices, shards(): carried = lax.all_to_all(carried, 'ctx', 0, 0, tiled=True)  8.27 us
    pallas_call x1, Pallas kernels, dilated_forward_call(): pl.pallas_call(dilated_forward_kernel, grid=grid, in_specs=[pl.BlockSpec(...  7.47 us
    all_to_all x1, waiting for transfers between devices, shards(): lax.all_to_all(attended.reshape(ctx_count, tokens_here, width_here), 'ctx...  6.33 us
  transfers between devices with their start and end apart: 5, of which 5 were waited for; matrix products, arithmetic and copies ran while one was open for 14% of the time, Pallas kernels for 0%

profile of v6, /device:TPU:1, one launch (start us, length us, event | category | flops | bytes accessed | tf_op | source)
XLA Modules:
  0.0 173.9 jit_solution(17819799296363251684)
XLA Ops:
  0.6 1.4 copy.152
  2.0 1.3 copy.153
  3.8 1.6 copy.155
  5.4 10.5 %all-to-all-start = ((bf16[3,16,128,128]{3,2,0,1:T(8,128)(2,1)}), bf16[3,16,128,128]{3,2,0,1:T(8,128)(2,1)S(1)}, u32[]{:S(2)}, u32[]{:S(2)}) async-start(bf16[3,16,128,128]{3,2,0,1:T(8,128)(2,1)} %copy.155), calls=%async_computation | async-start | bytes 3145728 | tf_op jit(solution)/shard_map/all_to_all | solution.py:457
  16.5 22.2 %all-to-all-done = bf16[3,16,128,128]{3,2,0,1:T(8,128)(2,1)S(1)} async-done(((bf16[3,16,128,128]{3,2,0,1:T(8,128)(2,1)}), bf16[3,16,128,128]{3,2,0,1:T(8,128)(2,1)S(1)}, u32[]{:S(2)}, u32[]{:S(2)}) %all-to-all-start) | async-done | bytes 1572896 | tf_op jit(solution)/shard_map/all_to_all | solution.py:457
  39.9 0.7 fusion.65
  40.7 0.7 fusion.63
  41.4 0.7 fusion.64
  42.1 1.0 fusion.44.own_ref
  43.1 0.8 fusion.49.q_ref
  43.9 0.9 fusion.47
  44.8 7.5 %shard_map.127 = (bf16[1024,128]{1,0:T(8,128)(2,1)}, f32[1024,1]{1,0:T(8,128)}) custom-call(s32[10]{0:T(128)} %pad_add_fusion.params_ref, bf16[1024,128]{1,0:T(8,128)(2,1)} %fusion.49.q_ref, bf16[1024,128]{1,0:T(8,128)(2,1)} %get-tuple-element.135.k_ref, bf16[1024,128]{1,0:T(8,128)(2,1)} %get-tuple-element.134.v_ref, f32[1024,1]{1,0:T(8,128)} %fusion.44.own_ref), custom_call_target="tpu_custom_call" | custom-call | flops 536870912 | bytes 1056768 | tf_op jit(solution)/shard_map/pallas_call | solution.py:188
  52.3 1.7 select_reduce_fusion
  55.6 0.9 add_convert_fusion.3
  56.5 4.4 %all-to-all-start.1 = ((bf16[16,128,128]{2,1,0:T(8,128)(2,1)}), bf16[16,128,128]{2,1,0:T(8,128)(2,1)S(1)}, u32[]{:S(2)}, u32[]{:S(2)}) async-start(bf16[16,128,128]{2,1,0:T(8,128)(2,1)} %bitcast.219), calls=%async_computation.1 | async-start | bytes 1048576 | tf_op jit(solution)/shard_map/all_to_all | solution.py:471
  60.9 2.0 %copy.169 = bf16[1,128,2048]{1,2,0:T(8,128)(2,1)} copy(bf16[1,128,2048]{2,1,0:T(8,128)(2,1)} %param.11) | data formatting | bytes 1048576 | tf_op args[3]
  63.0 2.2 %copy.170 = f32[128,16,128]{2,0,1:T(8,128)} copy(bf16[128,16,128]{0,2,1:T(8,128)(2,1)} %bitcast.230) | data formatting | bytes 1572864 | tf_op jit(solution)/shard_map/convert_element_type | solution.py:413
  65.8 6.3 %all-to-all-done.1 = bf16[16,128,128]{2,1,0:T(8,128)(2,1)S(1)} async-done(((bf16[16,128,128]{2,1,0:T(8,128)(2,1)}), bf16[16,128,128]{2,1,0:T(8,128)(2,1)S(1)}, u32[]{:S(2)}, u32[]{:S(2)}) %all-to-all-start.1) | async-done | bytes 524320 | tf_op jit(solution)/shard_map/all_to_all | solution.py:471
  72.4 1.8 %fusion.25 = (f32[128]{0:T(128)S(1)}, f32[16,128]{1,0:T(8,128)S(1)}, f32[128]{0:T(128)S(1)}, f32[16,128]{1,0:T(8,128)S(1)}) fusion(bf16[16,128,128]{2,1,0:T(8,128)(2,1)S(1)} %all-to-all-done.1, f32[128,16,128]{2,0,1:T(8,128)} %copy.170, f32[16,128]{1,0:T(8,128)S(1)} %bitcast.243, f32[128]{0:T(128)S(1)} %get-tuple-element.127, f32[128]{0:T(128)S(1)} %get-tuple-element.126), kind=kLoop, calls=%fused_computation.43 | loop fusion | flops 2617088 | bytes 1599488 | tf_op jit(solution)/shard_map/reduce_sum | solution.py:420
  74.2 1.3 fusion.34
  75.6 1.1 pad_maximum_fusion.2
  76.7 5.5 %all-to-all-start.2 = ((f32[16,130,128]{2,1,0:T(8,128)}), f32[16,130,128]{2,1,0:T(8,128)}, u32[]{:S(2)}, u32[]{:S(2)}) async-start(f32[16,130,128]{2,1,0:T(8,128)} %pad_maximum_fusion.2), calls=%async_computation.2 | async-start | bytes 2228224 | tf_op jit(solution)/shard_map/all_to_all | solution.py:485
  86.7 5.2 %exponential_multiply_fusion = f32[1024,1024]{1,0:T(8,128)} fusion(bf16[1024,128]{1,0:T(8,128)(2,1)S(1)} %copy-done.3, bf16[1024,128]{1,0:T(8,128)(2,1)S(1)} %copy-done.7, f32[1024]{0:T(1024)S(1)} %get-tuple-element.88, s32[]{:T(128)} %bitcast.48, s32[]{:T(128)} %bitcast.46, s32[]{:T(128)} %bitcast.44, s32[1024]{0:T(1024)S(1)} %multiply_add_fusion, ...), kind=kOutput, calls=%fused_computation.4 | convolution fusion | flops 289406976 | bytes 4729868 | tf_op jit(solution)/shard_map/while/body/eval_jaxpr/qhd,khd->hqk/dot_general | solution.py:296
  91.9 8.3 %all-to-all-done.2 = f32[16,130,128]{2,1,0:T(8,128)} async-done(((f32[16,130,128]{2,1,0:T(8,128)}), f32[16,130,128]{2,1,0:T(8,128)}, u32[]{:S(2)}, u32[]{:S(2)}) %all-to-all-start.2) | async-done | bytes 1064992 | tf_op jit(solution)/shard_map/all_to_all | solution.py:485
  100.1 1.3 slice.197
  101.5 1.4 fusion.31
  102.9 1.3 reshape.516
  104.1 1.6 fusion.36
  105.7 0.7 fusion.62
  106.5 3.6 %select_bitcast_fusion.1 = (bf16[1024,1,1,128]{0,3,2,1:T(8,128)(2,1)}, bf16[1024,1,1,128]{0,3,2,1:T(8,128)(2,1)}) fusion(pred[]{:T(512)} %bitcast.13, f32[1024,1024]{1,0:T(8,128)} %exponential_multiply_fusion, bf16[1024,1,1,128]{3,1,0,2:T(2,128)(2,1)S(1)} %get-tuple-element.103, bf16[1024,1,1,128]{3,1,0,2:T(2,128)(2,1)S(1)} %get-tuple-element.102), kind=kOutput, calls=%fused_computation.91 | convolution fusion | flops 270008320 | bytes 5242881 | tf_op jit(solution)/shard_map/while/body/eval_jaxpr/hqk,qhd->khd/dot_general | solution.py:313
  110.1 0.7 multiply_convert_fusion
  110.8 1.3 select_bitcast_fusion.3
  112.2 1.6 select_bitcast_fusion.5
  113.8 0.9 slice_reduce_fusion
  115.3 13.3 %all-to-all-start.4 = ((f32[32,2,128]{2,1,0:T(2,128)}), f32[32,2,128]{2,1,0:T(2,128)S(1)}, u32[]{:S(2)}, u32[]{:S(2)}) async-start(f32[32,2,128]{2,1,0:T(2,128)} %broadcast_in_dim.118), calls=%async_computation.4 | async-start | bytes 65536 | tf_op jit(solution)/shard_map/all_to_all | solution.py:490
  128.6 1.5 convolution_convert_fusion
  130.1 1.7 fusion.10
  133.4 1.1 pad_maximum_fusion.4
  134.9 1.8 %pad_maximum_fusion.5 = bf16[1024,2,1,128]{0,3,2,1:T(8,128)(2,1)} fusion(bf16[1024,1,1,128]{0,3,2,1:T(8,128)(2,1)} %get-tuple-element.113, bf16[1024,1,1,128]{0,3,2,1:T(8,128)(2,1)S(1)} %copy-done.4), kind=kLoop, calls=%fused_computation.70 | loop fusion | flops 262144 | bytes 1048576 | tf_op jit(solution)/shard_map/stack | solution.py:29
  136.7 1.3 copy.176
  138.4 1.3 pad_maximum_fusion.1
  139.8 1.4 all-to-all-done.4
  141.1 5.9 %all-to-all-start.3 = ((bf16[3,16,128,128]{3,2,0,1:T(8,128)(2,1)}), bf16[3,16,128,128]{3,2,0,1:T(8,128)(2,1)S(1)}, u32[]{:S(2)}, u32[]{:S(2)}) async-start(bf16[3,16,128,128]{3,2,0,1:T(8,128)(2,1)} %pad_maximum_fusion.1), calls=%async_computation.3 | async-start | bytes 3145728 | tf_op jit(solution)/shard_map/all_to_all | solution.py:503
  147.3 1.0 copy.185
  148.9 21.0 %all-to-all-done.3 = bf16[3,16,128,128]{3,2,0,1:T(8,128)(2,1)S(1)} async-done(((bf16[3,16,128,128]{3,2,0,1:T(8,128)(2,1)}), bf16[3,16,128,128]{3,2,0,1:T(8,128)(2,1)S(1)}, u32[]{:S(2)}, u32[]{:S(2)}) %all-to-all-start.3) | async-done | bytes 1572896 | tf_op jit(solution)/shard_map/all_to_all | solution.py:503
  170.3 1.0 copy.188
  171.6 1.0 copy.187
  172.9 1.0 copy.186
  (73 shorter events, 10.2 us)
Async XLA Ops:
  0.6 2.7 %copy-start.10 = (bf16[1,128,2048]{2,1,0:T(8,128)(2,1)S(1)}, bf16[1,128,2048]{2,1,0:T(8,128)(2,1)}, u32[]{:S(2)}) copy-start(bf16[1,128,2048]{2,1,0:T(8,128)(2,1)} %param.10) | copy-start | bytes 1572868
  5.4 10.5 %copy-start.14 = (s32[4]{0:T(128)S(1)}, s32[4]{0:T(128)}, u32[]{:S(2)}) copy-start(s32[4]{0:T(128)} %param.14) | copy-start | bytes 52
  5.4 10.5 %copy-start.15 = (s32[4]{0:T(128)S(1)}, s32[4]{0:T(128)}, u32[]{:S(2)}) copy-start(s32[4]{0:T(128)} %param.15) | copy-start | bytes 52
  5.4 33.3 %all-to-all-start = ((bf16[3,16,128,128]{3,2,0,1:T(8,128)(2,1)}), bf16[3,16,128,128]{3,2,0,1:T(8,128)(2,1)S(1)}, u32[]{:S(2)}, u32[]{:S(2)}) async-start(bf16[3,16,128,128]{3,2,0,1:T(8,128)(2,1)} %copy.155), calls=%async_computation | async-start | bytes 3145728 | tf_op jit(solution)/shard_map/all_to_all | solution.py:457
  54.0 1.0 copy-start.11
  56.5 15.6 %all-to-all-start.1 = ((bf16[16,128,128]{2,1,0:T(8,128)(2,1)}), bf16[16,128,128]{2,1,0:T(8,128)(2,1)S(1)}, u32[]{:S(2)}, u32[]{:S(2)}) async-start(bf16[16,128,128]{2,1,0:T(8,128)(2,1)} %bitcast.219), calls=%async_computation.1 | async-start | bytes 1048576 | tf_op jit(solution)/shard_map/all_to_all | solution.py:471
  60.9 11.5 %copy-start.12 = (f32[2048]{0:T(1024)S(1)}, f32[2048]{0:T(1024)}, u32[]{:S(2)}) copy-start(f32[2048]{0:T(1024)} %param.12) | copy-start | bytes 24580
  63.0 11.2 %copy-start.13 = (f32[2048]{0:T(1024)S(1)}, f32[2048]{0:T(1024)}, u32[]{:S(2)}) copy-start(f32[2048]{0:T(1024)} %param.13) | copy-start | bytes 24580
  72.2 2.1 %copy-start.1 = (f32[128,16,128]{2,0,1:T(8,128)S(1)}, f32[128,16,128]{2,0,1:T(8,128)}, u32[]{:S(2)}) copy-start(f32[128,16,128]{2,0,1:T(8,128)} %copy.170) | copy-start | bytes 3145732
  76.7 10.0 %copy-start.3 = (bf16[1024,128]{1,0:T(8,128)(2,1)S(1)}, bf16[1024,128]{1,0:T(8,128)(2,1)}, u32[]{:S(2)}) copy-start(bf16[1024,128]{1,0:T(8,128)(2,1)} %fusion.49.q_ref) | copy-start | bytes 786436
  76.7 10.0 %copy-start.7 = (bf16[1024,128]{1,0:T(8,128)(2,1)S(1)}, bf16[1024,128]{1,0:T(8,128)(2,1)}, u32[]{:S(2)}) copy-start(bf16[1024,128]{1,0:T(8,128)(2,1)} %get-tuple-element.135.k_ref) | copy-start | bytes 786436
  76.7 23.5 %all-to-all-start.2 = ((f32[16,130,128]{2,1,0:T(8,128)}), f32[16,130,128]{2,1,0:T(8,128)}, u32[]{:S(2)}, u32[]{:S(2)}) async-start(f32[16,130,128]{2,1,0:T(8,128)} %pad_maximum_fusion.2), calls=%async_computation.2 | async-start | bytes 2228224 | tf_op jit(solution)/shard_map/all_to_all | solution.py:485
  106.4 3.7 %copy-start = (f32[1024,1024]{1,0:T(8,128)S(1)}, f32[1024,1024]{1,0:T(8,128)}, u32[]{:S(2)}) copy-start(f32[1024,1024]{1,0:T(8,128)} %exponential_multiply_fusion) | copy-start | bytes 12582916
  106.4 3.7 %copy-start.9 = (bf16[1024,128]{1,0:T(8,128)(2,1)S(1)}, bf16[1024,128]{1,0:T(8,128)(2,1)}, u32[]{:S(2)}) copy-start(bf16[1024,128]{1,0:T(8,128)(2,1)} %get-tuple-element.134.v_ref) | copy-start | bytes 786436
  110.8 1.3 copy-start.8
  115.3 25.8 %all-to-all-start.4 = ((f32[32,2,128]{2,1,0:T(2,128)}), f32[32,2,128]{2,1,0:T(2,128)S(1)}, u32[]{:S(2)}, u32[]{:S(2)}) async-start(f32[32,2,128]{2,1,0:T(2,128)} %broadcast_in_dim.118), calls=%async_computation.4 | async-start | bytes 65536 | tf_op jit(solution)/shard_map/all_to_all | solution.py:490
  131.8 1.0 copy-start.5
  131.8 1.0 copy-start.6
  132.9 1.9 %copy-start.4 = (bf16[1024,1,1,128]{0,3,2,1:T(8,128)(2,1)S(1)}, bf16[1024,1,1,128]{0,3,2,1:T(8,128)(2,1)}, u32[]{:S(2)}) copy-start(bf16[1024,1,1,128]{0,3,2,1:T(8,128)(2,1)} %get-tuple-element.112) | copy-start | bytes 786436
  139.8 7.3 %copy-start.2 = (bf16[128,16,128]{2,0,1:T(8,128)(2,1)S(1)}, bf16[128,16,128]{2,0,1:T(8,128)(2,1)}, u32[]{:S(2)}) copy-start(bf16[128,16,128]{2,0,1:T(8,128)(2,1)} %get-tuple-element.101) | copy-start | bytes 1572868
  141.1 28.7 %all-to-all-start.3 = ((bf16[3,16,128,128]{3,2,0,1:T(8,128)(2,1)}), bf16[3,16,128,128]{3,2,0,1:T(8,128)(2,1)S(1)}, u32[]{:S(2)}, u32[]{:S(2)}) async-start(bf16[3,16,128,128]{3,2,0,1:T(8,128)(2,1)} %pad_maximum_fusion.1), calls=%async_computation.3 | async-start | bytes 3145728 | tf_op jit(solution)/shard_map/all_to_all | solution.py:503

commit v7 on v4

--- a/solution.py
+++ b/solution.py
@@ -158,13 +158,12 @@
     )
     masked = jnp.where(counted > 0, scores, -1e30)
     row_max = jnp.max(masked, axis=1, keepdims=True)
-    part_lse = row_max + jnp.log(
-        jnp.sum(counted * jnp.exp(masked - row_max), axis=1, keepdims=True)
-    )
+    shifted = counted * jnp.exp(masked - row_max)
+    part_lse = row_max + jnp.log(jnp.sum(shifted, axis=1, keepdims=True))
     own_lse = own_ref[...]
     top = jnp.maximum(part_lse, own_lse)
     log_norm = top + jnp.log(jnp.exp(part_lse - top) + jnp.exp(own_lse - top))
-    prob_bf = (counted * jnp.exp(masked - log_norm)).astype(jnp.bfloat16)
+    prob_bf = (shifted * jnp.exp(row_max - log_norm)).astype(jnp.bfloat16)
     out_ref[...] = jnp.dot(prob_bf, v_ref[...], preferred_element_type=jnp.float32).astype(
         out_ref.dtype
     )

time: 171 us -> 171 us (level)
  no operation moved by 1% of the time
where the time goes in v7:
time: 171 us; the launch traced here: 170 us
  waiting for transfers between devices  54.5 us (32%)
  starting transfers between devices  42.5 us (25%)
  local copies, waits for them, and re-layouts  24.5 us (14%)
  other arithmetic  20.2 us (12%)
  matrix products  15.8 us (9%)
  Pallas kernels  7.33 us (4%)
  between operations  4.94 us (3%)
    all_to_all x1, waiting for transfers between devices, shards(): lax.all_to_all(stacked_in, 'ctx', split_axis=1, concat_axis=1, tiled=True)  22.2 us
    all_to_all x1, waiting for transfers between devices, shards(): lax.all_to_all(jnp.stack([part.reshape(ctx_count, tokens_here, width_here...  21 us
    all_to_all x1, starting transfers between devices, shards(): both = jnp.sum(lax.all_to_all(both, 'dp', 0, 0, tiled=True), axis=0)  13.2 us
    unnamed x37, local copies, waits for them, and re-layouts  10.5 us
    all_to_all x1, starting transfers between devices, shards(): lax.all_to_all(stacked_in, 'ctx', split_axis=1, concat_axis=1, tiled=True)  10.5 us
    pallas_call x1, Pallas kernels, dilated_forward_call(): pl.pallas_call(dilated_forward_kernel, grid=grid, in_specs=[pl.BlockSpec(...  7.33 us
    dot_general x1, matrix products, step(): jnp.einsum('qhd,khd->hqk', q_block, key_row_set, preferred_element_type=j...  6.21 us
    select_n x5, other arithmetic, pick_rows(): return jnp.where(cond, pairs[:, 0], pairs[:, 1])  6.06 us
  transfers between devices with their start and end apart: 6, of which 5 were waited for; matrix products, arithmetic and copies ran while one was open for 22% of the time, Pallas kernels for 0%

profile of v7, /device:TPU:1, one launch (start us, length us, event | category | flops | bytes accessed | tf_op | source)
XLA Modules:
  0.0 169.8 jit_solution(8266914079502418108)
XLA Ops:
  0.6 1.4 copy.152
  2.0 1.3 copy.153
  3.8 1.6 copy.155
  5.4 10.5 %all-to-all-start = ((bf16[3,16,128,128]{3,2,0,1:T(8,128)(2,1)}), bf16[3,16,128,128]{3,2,0,1:T(8,128)(2,1)S(1)}, u32[]{:S(2)}, u32[]{:S(2)}) async-start(bf16[3,16,128,128]{3,2,0,1:T(8,128)(2,1)} %copy.155), calls=%async_computation | async-start | bytes 3145728 | tf_op jit(solution)/shard_map/all_to_all | solution.py:456
  16.5 22.2 %all-to-all-done = bf16[3,16,128,128]{3,2,0,1:T(8,128)(2,1)S(1)} async-done(((bf16[3,16,128,128]{3,2,0,1:T(8,128)(2,1)}), bf16[3,16,128,128]{3,2,0,1:T(8,128)(2,1)S(1)}, u32[]{:S(2)}, u32[]{:S(2)}) %all-to-all-start) | async-done | bytes 1572896 | tf_op jit(solution)/shard_map/all_to_all | solution.py:456
  39.9 0.7 fusion.64
  40.7 0.7 fusion.62
  41.4 0.7 fusion.63
  42.1 1.0 fusion.43.own_ref
  43.1 0.8 fusion.48.q_ref
  43.9 0.9 fusion.46
  44.8 7.3 %shard_map.127 = (bf16[1024,128]{1,0:T(8,128)(2,1)}, f32[1024,1]{1,0:T(8,128)}) custom-call(s32[10]{0:T(128)} %pad_add_fusion.params_ref, bf16[1024,128]{1,0:T(8,128)(2,1)} %fusion.48.q_ref, bf16[1024,128]{1,0:T(8,128)(2,1)} %get-tuple-element.135.k_ref, bf16[1024,128]{1,0:T(8,128)(2,1)} %get-tuple-element.134.v_ref, f32[1024,1]{1,0:T(8,128)} %fusion.43.own_ref), custom_call_target="tpu_custom_call" | custom-call | flops 536870912 | bytes 1056768 | tf_op jit(solution)/shard_map/pallas_call | solution.py:187
  52.2 1.7 %select_reduce_fusion = (f32[1024]{0:T(1024)S(1)}, f32[1024]{0:T(1024)S(1)}, f32[1024]{0:T(1024)S(1)}) fusion(pred[]{:T(512)} %bitcast.13, f32[1024,1]{1,0:T(8,128)} %get-tuple-element.38, f32[1024,2,1]{1,0,2:T(8,128)S(1)} %add.168), kind=kLoop, calls=%fused_computation.75 | loop fusion | flops 3072 | bytes 24577 | tf_op jit(solution)/shard_map/jit(_where)/select_n | solution.py:21
  55.4 0.9 add_convert_fusion.3
  56.4 4.5 %all-to-all-start.1 = ((bf16[16,128,128]{2,1,0:T(8,128)(2,1)}), bf16[16,128,128]{2,1,0:T(8,128)(2,1)S(1)}, u32[]{:S(2)}, u32[]{:S(2)}) async-start(bf16[16,128,128]{2,1,0:T(8,128)(2,1)} %bitcast.219), calls=%async_computation.1 | async-start | bytes 1048576 | tf_op jit(solution)/shard_map/all_to_all | solution.py:470
  63.4 0.6 fusion.65
  66.0 2.0 %copy.169 = bf16[1,128,2048]{1,2,0:T(8,128)(2,1)} copy(bf16[1,128,2048]{2,1,0:T(8,128)(2,1)} %param.11) | data formatting | bytes 1048576 | tf_op args[3]
  68.0 2.2 %copy.170 = f32[128,16,128]{2,0,1:T(8,128)} copy(bf16[128,16,128]{0,2,1:T(8,128)(2,1)} %bitcast.229) | data formatting | bytes 1572864 | tf_op jit(solution)/shard_map/convert_element_type | solution.py:412
  70.3 1.9 %all-to-all-done.1 = bf16[16,128,128]{2,1,0:T(8,128)(2,1)S(1)} async-done(((bf16[16,128,128]{2,1,0:T(8,128)(2,1)}), bf16[16,128,128]{2,1,0:T(8,128)(2,1)S(1)}, u32[]{:S(2)}, u32[]{:S(2)}) %all-to-all-start.1) | async-done | bytes 524320 | tf_op jit(solution)/shard_map/all_to_all | solution.py:470
  72.4 1.7 %fusion.29 = (f32[16,128]{1,0:T(8,128)S(1)}, f32[128]{0:T(128)S(1)}, f32[128]{0:T(128)S(1)}, f32[16,128]{1,0:T(8,128)S(1)}) fusion(bf16[16,128,128]{2,1,0:T(8,128)(2,1)S(1)} %all-to-all-done.1, f32[128,16,128]{2,0,1:T(8,128)} %copy.170, f32[128]{0:T(128)S(1)} %get-tuple-element.127, f32[128]{0:T(128)S(1)} %get-tuple-element.126, f32[16,128]{1,0:T(8,128)S(1)} %bitcast.243), kind=kLoop, calls=%fused_computation.46 | loop fusion | flops 2617088 | bytes 1599488 | tf_op jit(solution)/shard_map/reduce_sum | solution.py:422
  74.1 0.6 pad_maximum_fusion.6
  74.8 5.4 %all-to-all-start.4 = ((f32[16,2,128]{2,1,0:T(2,128)}), f32[16,2,128]{2,1,0:T(2,128)S(1)}, u32[]{:S(2)}, u32[]{:S(2)}) async-start(f32[16,2,128]{2,1,0:T(2,128)} %pad_maximum_fusion.6), calls=%async_computation.4 | async-start | bytes 32768 | tf_op jit(solution)/shard_map/all_to_all | solution.py:484
  80.2 2.8 %fusion.28 = (bf16[16,128,128]{2,1,0:T(8,128)(2,1)}, bf16[128,16,128]{2,0,1:T(8,128)(2,1)}) fusion(bf16[16,128,128]{2,1,0:T(8,128)(2,1)S(1)} %all-to-all-done.1, f32[128,16,128]{2,0,1:T(8,128)} %copy.170, f32[128]{0:T(128)S(1)} %broadcast_multiply_fusion, f32[128]{0:T(128)S(1)} %broadcast_multiply_fusion.1, f32[16,128]{1,0:T(8,128)S(1)} %bitcast.244, ...), kind=kLoop, calls=%fused_computation.45 | loop fusion | flops 3145728 | bytes 2639872 | tf_op jit(solution)/shard_map/convert_element_type | solution.py:421
  83.0 4.5 %all-to-all-done.4 = f32[16,2,128]{2,1,0:T(2,128)S(1)} async-done(((f32[16,2,128]{2,1,0:T(2,128)}), f32[16,2,128]{2,1,0:T(2,128)S(1)}, u32[]{:S(2)}, u32[]{:S(2)}) %all-to-all-start.4) | async-done | bytes 16416 | tf_op jit(solution)/shard_map/all_to_all | solution.py:484
  87.5 3.8 %all-to-all-start.2 = ((bf16[16,128,128]{2,1,0:T(8,128)(2,1)}), bf16[16,128,128]{2,1,0:T(8,128)(2,1)S(1)}, u32[]{:S(2)}, u32[]{:S(2)}) async-start(bf16[16,128,128]{2,1,0:T(8,128)(2,1)} %get-tuple-element.100), calls=%async_computation.2 | async-start | bytes 1048576 | tf_op jit(solution)/shard_map/all_to_all | solution.py:482
  91.2 6.2 %exponential_multiply_fusion = f32[1024,1024]{1,0:T(8,128)} fusion(bf16[1024,128]{1,0:T(8,128)(2,1)S(1)} %copy-done.3, bf16[1024,128]{1,0:T(8,128)(2,1)} %get-tuple-element.135.k_ref, f32[1024]{0:T(1024)S(1)} %get-tuple-element.89, s32[]{:T(128)} %bitcast.46, s32[]{:T(128)} %bitcast.44, s32[]{:T(128)} %bitcast.42, s32[1024]{0:T(1024)S(1)} %multiply_add_fusion, ...), kind=kOutput, calls=%fused_computation.4 | convolution fusion | flops 289406976 | bytes 4729868 | tf_op jit(solution)/shard_map/while/body/eval_jaxpr/qhd,khd->hqk/dot_general | solution.py:295
  97.5 5.0 %all-to-all-done.2 = bf16[16,128,128]{2,1,0:T(8,128)(2,1)S(1)} async-done(((bf16[16,128,128]{2,1,0:T(8,128)(2,1)}), bf16[16,128,128]{2,1,0:T(8,128)(2,1)S(1)}, u32[]{:S(2)}, u32[]{:S(2)}) %all-to-all-start.2) | async-done | bytes 524320 | tf_op jit(solution)/shard_map/all_to_all | solution.py:482
  102.5 0.6 broadcast_in_dim.118
  103.1 13.2 %all-to-all-start.5 = ((f32[32,2,128]{2,1,0:T(2,128)}), f32[32,2,128]{2,1,0:T(2,128)S(1)}, u32[]{:S(2)}, u32[]{:S(2)}) async-start(f32[32,2,128]{2,1,0:T(2,128)} %broadcast_in_dim.118), calls=%async_computation.5 | async-start | bytes 65536 | tf_op jit(solution)/shard_map/all_to_all | solution.py:487
  116.3 1.4 fusion.31
  117.7 1.3 reshape.516
  119.0 1.7 fusion.35
  120.7 0.7 fusion.61
  121.4 2.8 %select_bitcast_fusion.1 = (bf16[1024,1,1,128]{0,3,2,1:T(8,128)(2,1)S(1)}, bf16[1024,1,1,128]{0,3,2,1:T(8,128)(2,1)S(1)}) fusion(pred[]{:T(512)} %bitcast.13, f32[1024,1024]{1,0:T(8,128)} %exponential_multiply_fusion, bf16[1024,1,1,128]{3,1,0,2:T(2,128)(2,1)S(1)} %get-tuple-element.103, bf16[1024,1,1,128]{3,1,0,2:T(2,128)(2,1)S(1)} %get-tuple-element.102), kind=kOutput, calls=%fused_computation.88 | convolution fusion | flops 270008320 | bytes 5242881 | tf_op jit(solution)/shard_map/while/body/eval_jaxpr/hqk,qhd->khd/dot_general | solution.py:312
  124.9 0.7 multiply_convert_fusion
  125.6 1.3 select_bitcast_fusion.3
  126.9 1.6 select_bitcast_fusion.5
  128.5 1.1 convolution_convert_fusion
  131.3 1.1 pad_maximum_fusion.3
  132.9 1.8 %pad_maximum_fusion.4 = bf16[1024,2,1,128]{0,3,2,1:T(8,128)(2,1)} fusion(bf16[1024,1,1,128]{0,3,2,1:T(8,128)(2,1)} %get-tuple-element.113, bf16[1024,1,1,128]{0,3,2,1:T(8,128)(2,1)S(1)} %copy-done.4), kind=kLoop, calls=%fused_computation.67 | loop fusion | flops 262144 | bytes 1048576 | tf_op jit(solution)/shard_map/stack | solution.py:29
  134.7 1.3 copy.176
  136.4 1.3 pad_maximum_fusion.1
  137.8 5.2 %all-to-all-start.3 = ((bf16[3,16,128,128]{3,2,0,1:T(8,128)(2,1)}), bf16[3,16,128,128]{3,2,0,1:T(8,128)(2,1)S(1)}, u32[]{:S(2)}, u32[]{:S(2)}) async-start(bf16[3,16,128,128]{3,2,0,1:T(8,128)(2,1)} %pad_maximum_fusion.1), calls=%async_computation.3 | async-start | bytes 3145728 | tf_op jit(solution)/shard_map/all_to_all | solution.py:500
  143.2 1.0 copy.185
  144.8 21.0 %all-to-all-done.3 = bf16[3,16,128,128]{3,2,0,1:T(8,128)(2,1)S(1)} async-done(((bf16[3,16,128,128]{3,2,0,1:T(8,128)(2,1)}), bf16[3,16,128,128]{3,2,0,1:T(8,128)(2,1)S(1)}, u32[]{:S(2)}, u32[]{:S(2)}) %all-to-all-start.3) | async-done | bytes 1572896 | tf_op jit(solution)/shard_map/all_to_all | solution.py:500
  166.2 1.0 copy.188
  167.5 1.0 copy.187
  168.8 1.0 copy.186
  (68 shorter events, 9.6 us)
Async XLA Ops:
  0.6 2.7 %copy-start.7 = (bf16[1,128,2048]{2,1,0:T(8,128)(2,1)S(1)}, bf16[1,128,2048]{2,1,0:T(8,128)(2,1)}, u32[]{:S(2)}) copy-start(bf16[1,128,2048]{2,1,0:T(8,128)(2,1)} %param.10) | copy-start | bytes 1572868
  5.4 10.5 %copy-start.11 = (s32[4]{0:T(128)S(1)}, s32[4]{0:T(128)}, u32[]{:S(2)}) copy-start(s32[4]{0:T(128)} %param.14) | copy-start | bytes 52
  5.4 10.5 %copy-start.12 = (s32[4]{0:T(128)S(1)}, s32[4]{0:T(128)}, u32[]{:S(2)}) copy-start(s32[4]{0:T(128)} %param.15) | copy-start | bytes 52
  5.4 33.3 %all-to-all-start = ((bf16[3,16,128,128]{3,2,0,1:T(8,128)(2,1)}), bf16[3,16,128,128]{3,2,0,1:T(8,128)(2,1)S(1)}, u32[]{:S(2)}, u32[]{:S(2)}) async-start(bf16[3,16,128,128]{3,2,0,1:T(8,128)(2,1)} %copy.155), calls=%async_computation | async-start | bytes 3145728 | tf_op jit(solution)/shard_map/all_to_all | solution.py:456
  52.2 2.6 %copy-start.8 = (bf16[1024,128]{1,0:T(8,128)(2,1)S(1)}, bf16[1024,128]{1,0:T(8,128)(2,1)}, u32[]{:S(2)}) copy-start(bf16[1024,128]{1,0:T(8,128)(2,1)} %get-tuple-element.39) | copy-start | bytes 786436
  56.4 16.0 %copy-start.9 = (f32[2048]{0:T(1024)S(1)}, f32[2048]{0:T(1024)}, u32[]{:S(2)}) copy-start(f32[2048]{0:T(1024)} %param.12) | copy-start | bytes 24580
  56.4 15.8 %all-to-all-start.1 = ((bf16[16,128,128]{2,1,0:T(8,128)(2,1)}), bf16[16,128,128]{2,1,0:T(8,128)(2,1)S(1)}, u32[]{:S(2)}, u32[]{:S(2)}) async-start(bf16[16,128,128]{2,1,0:T(8,128)(2,1)} %bitcast.219), calls=%async_computation.1 | async-start | bytes 1048576 | tf_op jit(solution)/shard_map/all_to_all | solution.py:470
  68.0 12.2 %copy-start.10 = (f32[2048]{0:T(1024)S(1)}, f32[2048]{0:T(1024)}, u32[]{:S(2)}) copy-start(f32[2048]{0:T(1024)} %param.13) | copy-start | bytes 24580
  74.1 17.1 %copy-start.3 = (bf16[1024,128]{1,0:T(8,128)(2,1)S(1)}, bf16[1024,128]{1,0:T(8,128)(2,1)}, u32[]{:S(2)}) copy-start(bf16[1024,128]{1,0:T(8,128)(2,1)} %fusion.48.q_ref) | copy-start | bytes 786436
  74.8 12.7 %all-to-all-start.4 = ((f32[16,2,128]{2,1,0:T(2,128)}), f32[16,2,128]{2,1,0:T(2,128)S(1)}, u32[]{:S(2)}, u32[]{:S(2)}) async-start(f32[16,2,128]{2,1,0:T(2,128)} %pad_maximum_fusion.6), calls=%async_computation.4 | async-start | bytes 32768 | tf_op jit(solution)/shard_map/all_to_all | solution.py:484
  87.5 15.0 %all-to-all-start.2 = ((bf16[16,128,128]{2,1,0:T(8,128)(2,1)}), bf16[16,128,128]{2,1,0:T(8,128)(2,1)S(1)}, u32[]{:S(2)}, u32[]{:S(2)}) async-start(bf16[16,128,128]{2,1,0:T(8,128)(2,1)} %get-tuple-element.100), calls=%async_computation.2 | async-start | bytes 1048576 | tf_op jit(solution)/shard_map/all_to_all | solution.py:482
  103.1 34.7 %all-to-all-start.5 = ((f32[32,2,128]{2,1,0:T(2,128)}), f32[32,2,128]{2,1,0:T(2,128)S(1)}, u32[]{:S(2)}, u32[]{:S(2)}) async-start(f32[32,2,128]{2,1,0:T(2,128)} %broadcast_in_dim.118), calls=%async_computation.5 | async-start | bytes 65536 | tf_op jit(solution)/shard_map/all_to_all | solution.py:487
  121.4 3.5 %copy-start = (f32[1024,1024]{1,0:T(8,128)S(1)}, f32[1024,1024]{1,0:T(8,128)}, u32[]{:S(2)}) copy-start(f32[1024,1024]{1,0:T(8,128)} %exponential_multiply_fusion) | copy-start | bytes 12582916
  121.4 3.5 %copy-start.6 = (bf16[1024,128]{1,0:T(8,128)(2,1)S(1)}, bf16[1024,128]{1,0:T(8,128)(2,1)}, u32[]{:S(2)}) copy-start(bf16[1024,128]{1,0:T(8,128)(2,1)} %get-tuple-element.134.v_ref) | copy-start | bytes 786436
  125.6 1.3 copy-start.5
  130.8 2.1 %copy-start.4 = (bf16[1024,1,1,128]{0,3,2,1:T(8,128)(2,1)S(1)}, bf16[1024,1,1,128]{0,3,2,1:T(8,128)(2,1)}, u32[]{:S(2)}) copy-start(bf16[1024,1,1,128]{0,3,2,1:T(8,128)(2,1)} %get-tuple-element.112) | copy-start | bytes 786436
  131.3 4.7 %copy-start.1 = (bf16[16,128,128]{1,2,0:T(8,128)(2,1)S(1)}, bf16[16,128,128]{1,2,0:T(8,128)(2,1)}, u32[]{:S(2)}) copy-start(bf16[16,128,128]{1,2,0:T(8,128)(2,1)} %convolution_convert_fusion) | copy-start | bytes 1572868
  137.8 5.2 %copy-start.2 = (bf16[128,16,128]{2,0,1:T(8,128)(2,1)S(1)}, bf16[128,16,128]{2,0,1:T(8,128)(2,1)}, u32[]{:S(2)}) copy-start(bf16[128,16,128]{2,0,1:T(8,128)(2,1)} %get-tuple-element.101) | copy-start | bytes 1572868
  137.8 28.0 %all-to-all-start.3 = ((bf16[3,16,128,128]{3,2,0,1:T(8,128)(2,1)}), bf16[3,16,128,128]{3,2,0,1:T(8,128)(2,1)S(1)}, u32[]{:S(2)}, u32[]{:S(2)}) async-start(bf16[3,16,128,128]{3,2,0,1:T(8,128)(2,1)} %pad_maximum_fusion.1), calls=%async_computation.3 | async-start | bytes 3145728 | tf_op jit(solution)/shard_map/all_to_all | solution.py:500

commit v8 on v7

--- a/solution.py
+++ b/solution.py
@@ -180,7 +180,7 @@
     )
 
 
-def dilated_forward_call(params, q, k, v, own, row_block=256):
+def dilated_forward_call(params, q, k, v, own, row_block=512):
     rows, head_size = q.shape
     keys = k.shape[0]
     grid = (rows // row_block,)

time: 171 us -> 171 us (level)
  no operation moved by 1% of the time
where the time goes in v8:
time: 171 us; the launch traced here: 170 us
  waiting for transfers between devices  54.5 us (32%)
  starting transfers between devices  42.5 us (25%)
  local copies, waits for them, and re-layouts  24.5 us (14%)
  other arithmetic  20.1 us (12%)
  matrix products  15.8 us (9%)
  Pallas kernels  7.17 us (4%)
  between operations  4.94 us (3%)
    all_to_all x1, waiting for transfers between devices, shards(): lax.all_to_all(stacked_in, 'ctx', split_axis=1, concat_axis=1, tiled=True)  22.2 us
    all_to_all x1, waiting for transfers between devices, shards(): lax.all_to_all(jnp.stack([part.reshape(ctx_count, tokens_here, width_here...  21 us
    all_to_all x1, starting transfers between devices, shards(): both = jnp.sum(lax.all_to_all(both, 'dp', 0, 0, tiled=True), axis=0)  13.2 us
    unnamed x37, local copies, waits for them, and re-layouts  10.5 us
    all_to_all x1, starting transfers between devices, shards(): lax.all_to_all(stacked_in, 'ctx', split_axis=1, concat_axis=1, tiled=True)  10.5 us
    pallas_call x1, Pallas kernels, dilated_forward_call(): pl.pallas_call(dilated_forward_kernel, grid=grid, in_specs=[pl.BlockSpec(...  7.17 us
    dot_general x1, matrix products, step(): jnp.einsum('qhd,khd->hqk', q_block, key_row_set, preferred_element_type=j...  6.22 us
    select_n x5, other arithmetic, pick_rows(): return jnp.where(cond, pairs[:, 0], pairs[:, 1])  5.97 us
  transfers between devices with their start and end apart: 6, of which 5 were waited for; matrix products, arithmetic and copies ran while one was open for 22% of the time, Pallas kernels for 0%

profile of v8, /device:TPU:1, one launch (start us, length us, event | category | flops | bytes accessed | tf_op | source)
XLA Modules:
  0.0 169.6 jit_solution(11223099456708669563)
XLA Ops:
  0.6 1.4 copy.152
  2.0 1.3 copy.153
  3.8 1.6 copy.155
  5.4 10.5 %all-to-all-start = ((bf16[3,16,128,128]{3,2,0,1:T(8,128)(2,1)}), bf16[3,16,128,128]{3,2,0,1:T(8,128)(2,1)S(1)}, u32[]{:S(2)}, u32[]{:S(2)}) async-start(bf16[3,16,128,128]{3,2,0,1:T(8,128)(2,1)} %copy.155), calls=%async_computation | async-start | bytes 3145728 | tf_op jit(solution)/shard_map/all_to_all | solution.py:456
  16.5 22.2 %all-to-all-done = bf16[3,16,128,128]{3,2,0,1:T(8,128)(2,1)S(1)} async-done(((bf16[3,16,128,128]{3,2,0,1:T(8,128)(2,1)}), bf16[3,16,128,128]{3,2,0,1:T(8,128)(2,1)S(1)}, u32[]{:S(2)}, u32[]{:S(2)}) %all-to-all-start) | async-done | bytes 1572896 | tf_op jit(solution)/shard_map/all_to_all | solution.py:456
  39.9 0.7 fusion.64
  40.7 0.7 fusion.62
  41.4 0.7 fusion.63
  42.1 1.0 fusion.43.own_ref
  43.1 0.8 fusion.48.q_ref
  43.9 0.9 fusion.46
  44.8 7.2 %shard_map.127 = (bf16[1024,128]{1,0:T(8,128)(2,1)}, f32[1024,1]{1,0:T(8,128)}) custom-call(s32[10]{0:T(128)} %pad_add_fusion.params_ref, bf16[1024,128]{1,0:T(8,128)(2,1)} %fusion.48.q_ref, bf16[1024,128]{1,0:T(8,128)(2,1)} %get-tuple-element.135.k_ref, bf16[1024,128]{1,0:T(8,128)(2,1)} %get-tuple-element.134.v_ref, f32[1024,1]{1,0:T(8,128)} %fusion.43.own_ref), custom_call_target="tpu_custom_call" | custom-call | flops 536870912 | bytes 1056768 | tf_op jit(solution)/shard_map/pallas_call | solution.py:187
  52.0 1.7 %select_reduce_fusion = (f32[1024]{0:T(1024)S(1)}, f32[1024]{0:T(1024)S(1)}, f32[1024]{0:T(1024)S(1)}) fusion(pred[]{:T(512)} %bitcast.13, f32[1024,1]{1,0:T(8,128)} %get-tuple-element.38, f32[1024,2,1]{1,0,2:T(8,128)S(1)} %add.168), kind=kLoop, calls=%fused_computation.75 | loop fusion | flops 3072 | bytes 24577 | tf_op jit(solution)/shard_map/jit(_where)/select_n | solution.py:21
  55.3 0.9 add_convert_fusion.3
  56.2 4.5 %all-to-all-start.1 = ((bf16[16,128,128]{2,1,0:T(8,128)(2,1)}), bf16[16,128,128]{2,1,0:T(8,128)(2,1)S(1)}, u32[]{:S(2)}, u32[]{:S(2)}) async-start(bf16[16,128,128]{2,1,0:T(8,128)(2,1)} %bitcast.219), calls=%async_computation.1 | async-start | bytes 1048576 | tf_op jit(solution)/shard_map/all_to_all | solution.py:470
  63.3 0.6 fusion.65
  65.8 2.0 %copy.169 = bf16[1,128,2048]{1,2,0:T(8,128)(2,1)} copy(bf16[1,128,2048]{2,1,0:T(8,128)(2,1)} %param.11) | data formatting | bytes 1048576 | tf_op args[3]
  67.8 2.2 %copy.170 = f32[128,16,128]{2,0,1:T(8,128)} copy(bf16[128,16,128]{0,2,1:T(8,128)(2,1)} %bitcast.229) | data formatting | bytes 1572864 | tf_op jit(solution)/shard_map/convert_element_type | solution.py:412
  70.1 1.9 %all-to-all-done.1 = bf16[16,128,128]{2,1,0:T(8,128)(2,1)S(1)} async-done(((bf16[16,128,128]{2,1,0:T(8,128)(2,1)}), bf16[16,128,128]{2,1,0:T(8,128)(2,1)S(1)}, u32[]{:S(2)}, u32[]{:S(2)}) %all-to-all-start.1) | async-done | bytes 524320 | tf_op jit(solution)/shard_map/all_to_all | solution.py:470
  72.2 1.7 %fusion.29 = (f32[16,128]{1,0:T(8,128)S(1)}, f32[128]{0:T(128)S(1)}, f32[128]{0:T(128)S(1)}, f32[16,128]{1,0:T(8,128)S(1)}) fusion(bf16[16,128,128]{2,1,0:T(8,128)(2,1)S(1)} %all-to-all-done.1, f32[128,16,128]{2,0,1:T(8,128)} %copy.170, f32[128]{0:T(128)S(1)} %get-tuple-element.127, f32[128]{0:T(128)S(1)} %get-tuple-element.126, f32[16,128]{1,0:T(8,128)S(1)} %bitcast.243), kind=kLoop, calls=%fused_computation.46 | loop fusion | flops 2617088 | bytes 1599488 | tf_op jit(solution)/shard_map/reduce_sum | solution.py:422
  74.0 0.6 pad_maximum_fusion.6
  74.6 5.4 %all-to-all-start.4 = ((f32[16,2,128]{2,1,0:T(2,128)}), f32[16,2,128]{2,1,0:T(2,128)S(1)}, u32[]{:S(2)}, u32[]{:S(2)}) async-start(f32[16,2,128]{2,1,0:T(2,128)} %pad_maximum_fusion.6), calls=%async_computation.4 | async-start | bytes 32768 | tf_op jit(solution)/shard_map/all_to_all | solution.py:484
  80.0 2.8 %fusion.28 = (bf16[16,128,128]{2,1,0:T(8,128)(2,1)}, bf16[128,16,128]{2,0,1:T(8,128)(2,1)}) fusion(bf16[16,128,128]{2,1,0:T(8,128)(2,1)S(1)} %all-to-all-done.1, f32[128,16,128]{2,0,1:T(8,128)} %copy.170, f32[128]{0:T(128)S(1)} %broadcast_multiply_fusion, f32[128]{0:T(128)S(1)} %broadcast_multiply_fusion.1, f32[16,128]{1,0:T(8,128)S(1)} %bitcast.244, ...), kind=kLoop, calls=%fused_computation.45 | loop fusion | flops 3145728 | bytes 2639872 | tf_op jit(solution)/shard_map/convert_element_type | solution.py:421
  82.8 4.5 %all-to-all-done.4 = f32[16,2,128]{2,1,0:T(2,128)S(1)} async-done(((f32[16,2,128]{2,1,0:T(2,128)}), f32[16,2,128]{2,1,0:T(2,128)S(1)}, u32[]{:S(2)}, u32[]{:S(2)}) %all-to-all-start.4) | async-done | bytes 16416 | tf_op jit(solution)/shard_map/all_to_all | solution.py:484
  87.3 3.8 %all-to-all-start.2 = ((bf16[16,128,128]{2,1,0:T(8,128)(2,1)}), bf16[16,128,128]{2,1,0:T(8,128)(2,1)S(1)}, u32[]{:S(2)}, u32[]{:S(2)}) async-start(bf16[16,128,128]{2,1,0:T(8,128)(2,1)} %get-tuple-element.100), calls=%async_computation.2 | async-start | bytes 1048576 | tf_op jit(solution)/shard_map/all_to_all | solution.py:482
  91.1 6.2 %exponential_multiply_fusion = f32[1024,1024]{1,0:T(8,128)} fusion(bf16[1024,128]{1,0:T(8,128)(2,1)S(1)} %copy-done.3, bf16[1024,128]{1,0:T(8,128)(2,1)} %get-tuple-element.135.k_ref, f32[1024]{0:T(1024)S(1)} %get-tuple-element.89, s32[]{:T(128)} %bitcast.46, s32[]{:T(128)} %bitcast.44, s32[]{:T(128)} %bitcast.42, s32[1024]{0:T(1024)S(1)} %multiply_add_fusion, ...), kind=kOutput, calls=%fused_computation.4 | convolution fusion | flops 289406976 | bytes 4729868 | tf_op jit(solution)/shard_map/while/body/eval_jaxpr/qhd,khd->hqk/dot_general | solution.py:295
  97.3 5.0 %all-to-all-done.2 = bf16[16,128,128]{2,1,0:T(8,128)(2,1)S(1)} async-done(((bf16[16,128,128]{2,1,0:T(8,128)(2,1)}), bf16[16,128,128]{2,1,0:T(8,128)(2,1)S(1)}, u32[]{:S(2)}, u32[]{:S(2)}) %all-to-all-start.2) | async-done | bytes 524320 | tf_op jit(solution)/shard_map/all_to_all | solution.py:482
  102.3 0.6 broadcast_in_dim.118
  102.9 13.2 %all-to-all-start.5 = ((f32[32,2,128]{2,1,0:T(2,128)}), f32[32,2,128]{2,1,0:T(2,128)S(1)}, u32[]{:S(2)}, u32[]{:S(2)}) async-start(f32[32,2,128]{2,1,0:T(2,128)} %broadcast_in_dim.118), calls=%async_computation.5 | async-start | bytes 65536 | tf_op jit(solution)/shard_map/all_to_all | solution.py:487
  116.2 1.4 fusion.31
  117.6 1.3 reshape.516
  118.8 1.6 fusion.35
  120.4 0.7 fusion.61
  121.2 2.8 %select_bitcast_fusion.1 = (bf16[1024,1,1,128]{0,3,2,1:T(8,128)(2,1)S(1)}, bf16[1024,1,1,128]{0,3,2,1:T(8,128)(2,1)S(1)}) fusion(pred[]{:T(512)} %bitcast.13, f32[1024,1024]{1,0:T(8,128)} %exponential_multiply_fusion, bf16[1024,1,1,128]{3,1,0,2:T(2,128)(2,1)S(1)} %get-tuple-element.103, bf16[1024,1,1,128]{3,1,0,2:T(2,128)(2,1)S(1)} %get-tuple-element.102), kind=kOutput, calls=%fused_computation.88 | convolution fusion | flops 270008320 | bytes 5242881 | tf_op jit(solution)/shard_map/while/body/eval_jaxpr/hqk,qhd->khd/dot_general | solution.py:312
  124.6 0.7 multiply_convert_fusion
  125.4 1.3 select_bitcast_fusion.3
  126.7 1.6 select_bitcast_fusion.5
  128.3 1.1 convolution_convert_fusion
  131.1 1.1 pad_maximum_fusion.3
  132.6 1.8 %pad_maximum_fusion.4 = bf16[1024,2,1,128]{0,3,2,1:T(8,128)(2,1)} fusion(bf16[1024,1,1,128]{0,3,2,1:T(8,128)(2,1)} %get-tuple-element.113, bf16[1024,1,1,128]{0,3,2,1:T(8,128)(2,1)S(1)} %copy-done.4), kind=kLoop, calls=%fused_computation.67 | loop fusion | flops 262144 | bytes 1048576 | tf_op jit(solution)/shard_map/stack | solution.py:29
  134.4 1.3 copy.176
  136.2 1.3 pad_maximum_fusion.1
  137.5 5.2 %all-to-all-start.3 = ((bf16[3,16,128,128]{3,2,0,1:T(8,128)(2,1)}), bf16[3,16,128,128]{3,2,0,1:T(8,128)(2,1)S(1)}, u32[]{:S(2)}, u32[]{:S(2)}) async-start(bf16[3,16,128,128]{3,2,0,1:T(8,128)(2,1)} %pad_maximum_fusion.1), calls=%async_computation.3 | async-start | bytes 3145728 | tf_op jit(solution)/shard_map/all_to_all | solution.py:500
  143.0 1.0 copy.185
  144.6 21.0 %all-to-all-done.3 = bf16[3,16,128,128]{3,2,0,1:T(8,128)(2,1)S(1)} async-done(((bf16[3,16,128,128]{3,2,0,1:T(8,128)(2,1)}), bf16[3,16,128,128]{3,2,0,1:T(8,128)(2,1)S(1)}, u32[]{:S(2)}, u32[]{:S(2)}) %all-to-all-start.3) | async-done | bytes 1572896 | tf_op jit(solution)/shard_map/all_to_all | solution.py:500
  166.0 1.0 copy.188
  167.3 1.0 copy.187
  168.6 1.0 copy.186
  (68 shorter events, 9.6 us)
Async XLA Ops:
  0.6 2.7 %copy-start.7 = (bf16[1,128,2048]{2,1,0:T(8,128)(2,1)S(1)}, bf16[1,128,2048]{2,1,0:T(8,128)(2,1)}, u32[]{:S(2)}) copy-start(bf16[1,128,2048]{2,1,0:T(8,128)(2,1)} %param.10) | copy-start | bytes 1572868
  5.4 10.5 %copy-start.11 = (s32[4]{0:T(128)S(1)}, s32[4]{0:T(128)}, u32[]{:S(2)}) copy-start(s32[4]{0:T(128)} %param.14) | copy-start | bytes 52
  5.4 10.5 %copy-start.12 = (s32[4]{0:T(128)S(1)}, s32[4]{0:T(128)}, u32[]{:S(2)}) copy-start(s32[4]{0:T(128)} %param.15) | copy-start | bytes 52
  5.4 33.3 %all-to-all-start = ((bf16[3,16,128,128]{3,2,0,1:T(8,128)(2,1)}), bf16[3,16,128,128]{3,2,0,1:T(8,128)(2,1)S(1)}, u32[]{:S(2)}, u32[]{:S(2)}) async-start(bf16[3,16,128,128]{3,2,0,1:T(8,128)(2,1)} %copy.155), calls=%async_computation | async-start | bytes 3145728 | tf_op jit(solution)/shard_map/all_to_all | solution.py:456
  52.0 2.6 %copy-start.8 = (bf16[1024,128]{1,0:T(8,128)(2,1)S(1)}, bf16[1024,128]{1,0:T(8,128)(2,1)}, u32[]{:S(2)}) copy-start(bf16[1024,128]{1,0:T(8,128)(2,1)} %get-tuple-element.39) | copy-start | bytes 786436
  56.2 16.0 %copy-start.9 = (f32[2048]{0:T(1024)S(1)}, f32[2048]{0:T(1024)}, u32[]{:S(2)}) copy-start(f32[2048]{0:T(1024)} %param.12) | copy-start | bytes 24580
  56.2 15.8 %all-to-all-start.1 = ((bf16[16,128,128]{2,1,0:T(8,128)(2,1)}), bf16[16,128,128]{2,1,0:T(8,128)(2,1)S(1)}, u32[]{:S(2)}, u32[]{:S(2)}) async-start(bf16[16,128,128]{2,1,0:T(8,128)(2,1)} %bitcast.219), calls=%async_computation.1 | async-start | bytes 1048576 | tf_op jit(solution)/shard_map/all_to_all | solution.py:470
  67.8 12.2 %copy-start.10 = (f32[2048]{0:T(1024)S(1)}, f32[2048]{0:T(1024)}, u32[]{:S(2)}) copy-start(f32[2048]{0:T(1024)} %param.13) | copy-start | bytes 24580
  74.0 17.1 %copy-start.3 = (bf16[1024,128]{1,0:T(8,128)(2,1)S(1)}, bf16[1024,128]{1,0:T(8,128)(2,1)}, u32[]{:S(2)}) copy-start(bf16[1024,128]{1,0:T(8,128)(2,1)} %fusion.48.q_ref) | copy-start | bytes 786436
  74.6 12.7 %all-to-all-start.4 = ((f32[16,2,128]{2,1,0:T(2,128)}), f32[16,2,128]{2,1,0:T(2,128)S(1)}, u32[]{:S(2)}, u32[]{:S(2)}) async-start(f32[16,2,128]{2,1,0:T(2,128)} %pad_maximum_fusion.6), calls=%async_computation.4 | async-start | bytes 32768 | tf_op jit(solution)/shard_map/all_to_all | solution.py:484
  87.3 15.0 %all-to-all-start.2 = ((bf16[16,128,128]{2,1,0:T(8,128)(2,1)}), bf16[16,128,128]{2,1,0:T(8,128)(2,1)S(1)}, u32[]{:S(2)}, u32[]{:S(2)}) async-start(bf16[16,128,128]{2,1,0:T(8,128)(2,1)} %get-tuple-element.100), calls=%async_computation.2 | async-start | bytes 1048576 | tf_op jit(solution)/shard_map/all_to_all | solution.py:482
  102.9 34.6 %all-to-all-start.5 = ((f32[32,2,128]{2,1,0:T(2,128)}), f32[32,2,128]{2,1,0:T(2,128)S(1)}, u32[]{:S(2)}, u32[]{:S(2)}) async-start(f32[32,2,128]{2,1,0:T(2,128)} %broadcast_in_dim.118), calls=%async_computation.5 | async-start | bytes 65536 | tf_op jit(solution)/shard_map/all_to_all | solution.py:487
  121.1 3.5 %copy-start = (f32[1024,1024]{1,0:T(8,128)S(1)}, f32[1024,1024]{1,0:T(8,128)}, u32[]{:S(2)}) copy-start(f32[1024,1024]{1,0:T(8,128)} %exponential_multiply_fusion) | copy-start | bytes 12582916
  121.2 3.5 %copy-start.6 = (bf16[1024,128]{1,0:T(8,128)(2,1)S(1)}, bf16[1024,128]{1,0:T(8,128)(2,1)}, u32[]{:S(2)}) copy-start(bf16[1024,128]{1,0:T(8,128)(2,1)} %get-tuple-element.134.v_ref) | copy-start | bytes 786436
  125.4 1.3 copy-start.5
  130.6 2.1 %copy-start.4 = (bf16[1024,1,1,128]{0,3,2,1:T(8,128)(2,1)S(1)}, bf16[1024,1,1,128]{0,3,2,1:T(8,128)(2,1)}, u32[]{:S(2)}) copy-start(bf16[1024,1,1,128]{0,3,2,1:T(8,128)(2,1)} %get-tuple-element.112) | copy-start | bytes 786436
  131.0 4.7 %copy-start.1 = (bf16[16,128,128]{1,2,0:T(8,128)(2,1)S(1)}, bf16[16,128,128]{1,2,0:T(8,128)(2,1)}, u32[]{:S(2)}) copy-start(bf16[16,128,128]{1,2,0:T(8,128)(2,1)} %convolution_convert_fusion) | copy-start | bytes 1572868
  137.5 5.2 %copy-start.2 = (bf16[128,16,128]{2,0,1:T(8,128)(2,1)S(1)}, bf16[128,16,128]{2,0,1:T(8,128)(2,1)}, u32[]{:S(2)}) copy-start(bf16[128,16,128]{2,0,1:T(8,128)(2,1)} %get-tuple-element.101) | copy-start | bytes 1572868
  137.5 28.0 %all-to-all-start.3 = ((bf16[3,16,128,128]{3,2,0,1:T(8,128)(2,1)}), bf16[3,16,128,128]{3,2,0,1:T(8,128)(2,1)S(1)}, u32[]{:S(2)}, u32[]{:S(2)}) async-start(bf16[3,16,128,128]{3,2,0,1:T(8,128)(2,1)} %pad_maximum_fusion.1), calls=%async_computation.3 | async-start | bytes 3145728 | tf_op jit(solution)/shard_map/all_to_all | solution.py:500
